TPU v7x, 256 devices: a whole 4x4x8 slice. The times are simulated.
256 devices in a mesh: tm: 8 (over x, core), space: 32 (over y, z).
Axes of the slice: x: 4, y: 4, z: 8, core: 2. Of those that a mesh axis runs over, the one named last changes fastest.
Arguments:
- snapshots: bfloat16 [2016, 5, 64, 8, 128], P('tm', None, 'space'), may hold values from -6 to 6
- picks: int32 [1792], P('tm'), may hold values from 0 to 251, as said below
- basis: bfloat16 [32, 5, 64, 8, 128], P(None, None, 'space'), may hold values from -0.01953125 to 0.01953125
- kappa: float32 [5, 64, 8, 128], P(None, 'space'), may hold values from 0.03 to 0.16
Outputs:
- coefficients: float32 [1792, 32], P('tm')
- factor: float32 [561, 561], replicated
Inputs may be any that keep to these rules, and one draw needn't show every extreme that they name: `picks`: within each time group's 224 consecutive entries the indices are distinct, and 0 and 251 both occur.
All inputs are finite; a program needn't handle non-finite values.
Results may differ from a plain program's by a relative error of at most 0.0003.
Values may be sent and summed in bfloat16 or wider, within the bound.
No kernel may reach another device: no remote copies, remote signals or barrier semaphores. Data moves between devices by JAX's collectives and lax.ppermute only.
A program may use at most 64 MiB of HBM per device.

v0:
```python
import functools

import jax
import jax.numpy as jnp
import numpy as np
from jax import lax
from jax.experimental import pallas as pl
from jax.experimental.pallas import tpu as pltpu
from jax.sharding import PartitionSpec as P

PANEL = 128


def split3(x):
    hi = x.astype(jnp.bfloat16)
    rest = x - hi.astype(jnp.float32)
    mid = rest.astype(jnp.bfloat16)
    lo = (rest - mid.astype(jnp.float32)).astype(jnp.bfloat16)
    return hi, mid, lo


def dot3(a, b):
    a1, a2, a3 = split3(a)
    b1, b2, b3 = split3(b)
    def d(x, y):
        return jnp.dot(x, y, preferred_element_type=jnp.float32)
    return d(a1, b1) + (d(a1, b2) + d(a2, b1)) + (d(a1, b3) + d(a3, b1) + d(a2, b2))


def chol_kernel(a_ref, r_ref, w_ref, blk_ref, *, size, valid):
    panels = size // PANEL
    r_ref[...] = jnp.zeros((size, size), jnp.float32)
    w_ref[...] = a_ref[...]
    rows = lax.broadcasted_iota(jnp.int32, (PANEL, 2 * PANEL), 0)
    lanes = lax.broadcasted_iota(jnp.int32, (PANEL, 2 * PANEL), 1)
    eye = (rows[:, :PANEL] == lanes[:, :PANEL]).astype(jnp.float32)
    row_lanes = lax.broadcasted_iota(jnp.int32, (1, 2 * PANEL), 1)
    col_rows = lax.broadcasted_iota(jnp.int32, (PANEL, 1), 0)
    for p in range(panels):
        c0 = p * PANEL
        c1 = c0 + PANEL
        steps = min(PANEL, valid - c0)
        blk_ref[:, :PANEL] = w_ref[c0:c1, c0:c1]
        blk_ref[:, PANEL:] = eye

        def step(j, carry):
            row = blk_ref[pl.ds(j, 1), :]
            pivot = jnp.sum(jnp.where(row_lanes == j, row, 0.0), axis=1, keepdims=True)
            scale = lax.rsqrt(pivot)
            scaled = row * scale
            block = blk_ref[...]
            column = jnp.sum(jnp.where(lanes[:, :PANEL] == j, block[:, :PANEL], 0.0), axis=1, keepdims=True)
            coef = jnp.where(col_rows > j, column * scale, 0.0)
            updated = block - coef * scaled
            blk_ref[...] = jnp.where(rows == j, scaled, updated)
            return carry

        lax.fori_loop(0, steps, step, 0)
        block = blk_ref[...]
        upper = jnp.where(lanes[:, :PANEL] >= rows[:, :PANEL], block[:, :PANEL], 0.0)
        r_ref[c0:c1, c0:c1] = upper
        if p + 1 < panels:
            inv_t = block[:, PANEL:]
            right = dot3(inv_t, w_ref[c0:c1, c1:size])
            r_ref[c0:c1, c1:size] = right
            w_ref[c1:size, c1:size] = w_ref[c1:size, c1:size] - dot3(right.T, right)


def cholesky_upper(gram):
    n = gram.shape[0]
    size = -(-n // PANEL) * PANEL
    padded = jnp.pad(gram, ((0, size - n), (0, size - n)))
    fill = (jnp.arange(size) >= n).astype(jnp.float32)
    padded = padded + jnp.diag(fill)
    out = pl.pallas_call(
        functools.partial(chol_kernel, size=size, valid=n),
        out_shape=jax.ShapeDtypeStruct((size, size), jnp.float32),
        scratch_shapes=[pltpu.VMEM((size, size), jnp.float32), pltpu.VMEM((PANEL, 2 * PANEL), jnp.float32)],
    )(padded)
    return out[:n, :n]


def neighbour_planes(block, axis, dim):
    count = lax.axis_size(axis)
    forward = [(i, i + 1) for i in range(count - 1)]
    backward = [(target, source) for source, target in forward]
    width = block.shape[dim]
    low = lax.ppermute(lax.slice_in_dim(block, width - 1, width, axis=dim), axis, forward)
    high = lax.ppermute(lax.slice_in_dim(block, 0, 1, axis=dim), axis, backward)
    return jnp.concatenate([low, block, high], axis=dim)


def adjoint_basis(basis, kappa):
    wide = basis.astype(jnp.float32)
    scaled = kappa[None] * wide
    padded = neighbour_planes(scaled, "space", 2)
    padded = jnp.pad(padded, ((0, 0), (0, 0), (0, 0), (1, 1), (1, 1)))
    center = padded[:, :, 1:-1, 1:-1, 1:-1]
    beside = padded[:, :, 2:, 1:-1, 1:-1] + padded[:, :, :-2, 1:-1, 1:-1]
    beside = beside + padded[:, :, 1:-1, 2:, 1:-1] + padded[:, :, 1:-1, :-2, 1:-1]
    beside = beside + padded[:, :, 1:-1, 1:-1, 2:] + padded[:, :, 1:-1, 1:-1, :-2]
    return wide + (beside - 6.0 * center)


def butterfly_sum(x, axis):
    count = lax.axis_size(axis)
    if count & (count - 1):
        return lax.psum(x, axis)
    step = 1
    while step < count:
        x = x + lax.ppermute(x, axis, [(i, i ^ step) for i in range(count)])
        step *= 2
    return x


def butterfly_gather(x, axis, dim):
    count = lax.axis_size(axis)
    if count & (count - 1):
        return lax.all_gather(x, axis, axis=dim, tiled=True)
    index = lax.axis_index(axis)
    step = 1
    while step < count:
        other = lax.ppermute(x, axis, [(i, i ^ step) for i in range(count)])
        low = (index // step) % 2 == 0
        x = jnp.where(low, jnp.concatenate([x, other], dim), jnp.concatenate([other, x], dim))
        step *= 2
    return x


def expand_rows(coeffs_t):
    count = coeffs_t.shape[0]
    first, second = np.triu_indices(count)
    quad = jnp.take(coeffs_t, first, axis=0) * jnp.take(coeffs_t, second, axis=0)
    ones = jnp.ones((1, coeffs_t.shape[1]), coeffs_t.dtype)
    return jnp.concatenate([ones, coeffs_t, quad], axis=0)


def body(snapshots, picks, basis, kappa):
    modes = basis.shape[0]
    adjoint = adjoint_basis(basis, kappa).reshape(modes, -1)
    stored = snapshots.shape[0]
    flat = snapshots.reshape(stored, -1).astype(jnp.float32)
    partial_t = lax.dot_general(
        adjoint,
        flat,
        (((1,), (1,)), ((), ())),
        precision=lax.Precision.HIGHEST,
        preferred_element_type=jnp.float32,
    )
    part_t = jnp.take(partial_t, picks, axis=1)
    own_t = butterfly_sum(part_t, "space")
    coeffs_t = butterfly_gather(own_t, "tm", 1)
    features_t = expand_rows(coeffs_t)
    gram = lax.dot_general(
        features_t,
        features_t,
        (((1,), (1,)), ((), ())),
        precision=lax.Precision.HIGHEST,
        preferred_element_type=jnp.float32,
    ) / coeffs_t.shape[1]
    factor = cholesky_upper(gram)
    return (own_t.T, factor)


def solution(mesh):
    in_specs = (
        P("tm", None, "space", None, None),
        P("tm"),
        P(None, None, "space", None, None),
        P(None, "space", None, None),
    )
    out_specs = (P("tm", None), P())
    return jax.shard_map(body, mesh=mesh, in_specs=in_specs, out_specs=out_specs, check_vma=False)
```

profile of v0, /device:TPU:24, one launch (start us, length us, event | category | flops | bytes accessed | tf_op | source)
XLA Modules:
  0.0 190.8 jit_solution(14582500640429935074)
XLA Ops:
  1.9 7.9 %collective-permute-start = (f32[32,5,1,8,128]{4,3,2,1,0:T(8,128)S(1)}, f32[32,5,1,8,128]{4,3,2,1,0:T(8,128)S(1)}, u32[]{:S(2)}, u32[]{:S(2)}) collective-permute-start(f32[32,5,1,8,128]{4,3,2,1,0:T(8,128)S(1)} %get-tuple-element.8), channel_id=1, source_target_pairs={{1,0},{2,1},{3,2},{4,3},{5,4},{6,5},{7,6},{8,7},{9,8},{10,9},{11,1... | collective-permute-start | bytes 1966088 | tf_op jit(solution)/shard_map/ppermute | solution.py:89
  9.9 1.9 %collective-permute-start.1 = (f32[32,5,1,8,128]{4,3,2,1,0:T(8,128)S(1)}, f32[32,5,1,8,128]{4,3,2,1,0:T(8,128)S(1)}, u32[]{:S(2)}, u32[]{:S(2)}) collective-permute-start(f32[32,5,1,8,128]{4,3,2,1,0:T(8,128)S(1)} %get-tuple-element.7), channel_id=1, source_target_pairs={{0,1},{1,2},{2,3},{3,4},{4,5},{5,6},{6,7},{7,8},{8,9},{9,10},{10,1... | collective-permute-start | bytes 1966088 | tf_op jit(solution)/shard_map/ppermute | solution.py:88
  11.9 12.0 %collective-permute-done = f32[32,5,1,8,128]{4,3,2,1,0:T(8,128)S(1)} collective-permute-done((f32[32,5,1,8,128]{4,3,2,1,0:T(8,128)S(1)}, f32[32,5,1,8,128]{4,3,2,1,0:T(8,128)S(1)}, u32[]{:S(2)}, u32[]{:S(2)}) %collective-permute-start) | collective-permute-done | bytes 655392 | tf_op jit(solution)/shard_map/ppermute | solution.py:89
  23.9 6.2 %collective-permute-done.1 = f32[32,5,1,8,128]{4,3,2,1,0:T(8,128)S(1)} collective-permute-done((f32[32,5,1,8,128]{4,3,2,1,0:T(8,128)S(1)}, f32[32,5,1,8,128]{4,3,2,1,0:T(8,128)S(1)}, u32[]{:S(2)}, u32[]{:S(2)}) %collective-permute-start.1) | collective-permute-done | bytes 655392 | tf_op jit(solution)/shard_map/ppermute | solution.py:88
  30.9 4.5 %select_maximum_fusion = f32[32,5,4,10,130]{4,3,2,1,0:T(8,128)S(1)} fusion(f32[32,5,1,8,128]{4,3,2,1,0:T(8,128)S(1)} %collective-permute-done, f32[32,5,2,8,128]{4,3,2,1,0:T(8,128)S(1)} %convert_multiply_fusion, f32[32,5,1,8,128]{4,3,2,1,0:T(8,128)S(1)} %collective-permute-done.1), kind=kLoop, calls=%fused_computation.7 | loop fusion | flops 12480000 | bytes 5949440 | tf_op jit(solution)/shard_map/concatenate | solution.py:90
  35.5 4.4 %convert_add_fusion = f32[32,5,2,8,128]{4,3,2,1,0:T(8,128)} fusion(bf16[32,5,2,8,128]{4,3,2,1,0:T(8,128)(2,1)} %param.10, f32[32,5,4,10,130]{4,3,2,1,0:T(8,128)S(1)} %select_maximum_fusion, f32[32,5,2,8,128]{4,3,2,1,0:T(8,128)} %copy-done, f32[32,5,1,8,128]{4,3,2,1,0:T(8,128)} %copy-done.1, f32[32,5,1,8,128]{4,3,2,1,0:T(8,128)S(1)} %collective-permute-done), kind=kLoop, calls=%fused_computation.22 | loop fusion | flops 3604480 | bytes 9830400 | tf_op jit(solution)/shard_map/add | solution.py:102
  39.8 7.4 %fusion.17 = f32[32,252]{0,1:T(8,128)S(1)} fusion(bf16[252,5,2,8,128]{4,3,2,1,0:T(8,128)(2,1)} %param.8, f32[32,5,2,8,128]{4,3,2,1,0:T(8,128)} %convert_add_fusion), kind=kOutput, calls=%fused_computation.34 | convolution fusion | flops 990904320 | bytes 6503936 | tf_op jit(solution)/shard_map/dot_general | solution.py:143
  48.2 4.8 %collective-permute-done.2 = f32[32,224]{0,1:T(8,128)S(1)} collective-permute-done((f32[32,224]{0,1:T(8,128)S(1)}, f32[32,224]{0,1:T(8,128)S(1)}, u32[]{:S(2)}, u32[]{:S(2)}) %collective-permute-start.2) | collective-permute-done | bytes 28704 | tf_op jit(solution)/shard_map/ppermute | solution.py:111
  53.2 7.6 %collective-permute-done.3 = f32[32,224]{0,1:T(8,128)S(1)} collective-permute-done((f32[32,224]{0,1:T(8,128)S(1)}, f32[32,224]{0,1:T(8,128)S(1)}, u32[]{:S(2)}, u32[]{:S(2)}) %collective-permute-start.3) | collective-permute-done | bytes 28704 | tf_op jit(solution)/shard_map/ppermute | solution.py:111
  60.9 8.7 %collective-permute-done.4 = f32[32,224]{0,1:T(8,128)S(1)} collective-permute-done((f32[32,224]{0,1:T(8,128)S(1)}, f32[32,224]{0,1:T(8,128)S(1)}, u32[]{:S(2)}, u32[]{:S(2)}) %collective-permute-start.4) | collective-permute-done | bytes 28704 | tf_op jit(solution)/shard_map/ppermute | solution.py:111
  69.7 4.8 %collective-permute-done.5 = f32[32,224]{0,1:T(8,128)S(1)} collective-permute-done((f32[32,224]{0,1:T(8,128)S(1)}, f32[32,224]{0,1:T(8,128)S(1)}, u32[]{:S(2)}, u32[]{:S(2)}) %collective-permute-start.5) | collective-permute-done | bytes 28704 | tf_op jit(solution)/shard_map/ppermute | solution.py:111
  75.6 5.3 %collective-permute-done.6 = f32[32,224]{0,1:T(8,128)S(1)} collective-permute-done((f32[32,224]{0,1:T(8,128)S(1)}, f32[32,224]{0,1:T(8,128)S(1)}, u32[]{:S(2)}, u32[]{:S(2)}) %collective-permute-start.6) | collective-permute-done | bytes 28704 | tf_op jit(solution)/shard_map/ppermute | solution.py:111
  81.1 1.2 collective-permute-done.7
  82.5 1.6 collective-permute-start.8
  84.1 2.8 %collective-permute-done.8 = f32[32,448]{1,0:T(8,128)S(1)} collective-permute-done((f32[32,448]{1,0:T(8,128)S(1)}, f32[32,448]{1,0:T(8,128)S(1)}, u32[]{:S(2)}, u32[]{:S(2)}) %collective-permute-start.8) | collective-permute-done | bytes 57376 | tf_op jit(solution)/shard_map/ppermute | solution.py:123
  86.9 3.3 %collective-permute-start.9 = (f32[32,896]{1,0:T(8,128)S(1)}, f32[32,896]{1,0:T(8,128)S(1)}, u32[]{:S(2)}, u32[]{:S(2)}) collective-permute-start(f32[32,896]{1,0:T(8,128)S(1)} %maximum_select_fusion.1), channel_id=1, source_target_pairs={{0,128},{32,160},{64,192},{96,224},{128,0},{160,32},{192,64},{224,... | collective-permute-start | bytes 344072 | tf_op jit(solution)/shard_map/ppermute | solution.py:123
  91.0 2.5 %collective-permute-done.9 = f32[32,896]{1,0:T(8,128)S(1)} collective-permute-done((f32[32,896]{1,0:T(8,128)S(1)}, f32[32,896]{1,0:T(8,128)S(1)}, u32[]{:S(2)}, u32[]{:S(2)}) %collective-permute-start.9) | collective-permute-done | bytes 114720 | tf_op jit(solution)/shard_map/ppermute | solution.py:123
  93.5 4.3 %gather_fusion.1 = f32[528,1792]{1,0:T(8,128)} fusion(f32[32,1792]{1,0:T(8,128)S(1)} %maximum_select_fusion, s32[1024]{0:T(1024)S(1)} %pad_clamp_fusion.1), kind=kCustom, calls=%fused_computation.clone | custom fusion | bytes 7571520 | tf_op jit(solution)/shard_map/jit(_take)/gather | solution.py:133
  97.8 4.3 %gather_fusion.2 = f32[528,1792]{1,0:T(8,128)} fusion(f32[32,1792]{1,0:T(8,128)S(1)} %maximum_select_fusion, s32[1024]{0:T(1024)S(1)} %pad_clamp_fusion), kind=kCustom, calls=%fused_computation.1.clone | custom fusion | bytes 7571520 | tf_op jit(solution)/shard_map/jit(_take)/gather | solution.py:133
  102.1 3.7 %mul.21 = f32[528,1792]{1,0:T(8,128)S(1)} multiply(f32[528,1792]{1,0:T(8,128)} %gather_fusion.1, f32[528,1792]{1,0:T(8,128)} %gather_fusion.2) | non-fusion elementwise | flops 946176 | bytes 11354112 | tf_op jit(solution)/shard_map/mul | solution.py:133
  105.8 10.3 %fusion.11 = f32[561,561]{1,0:T(8,128)S(1)} fusion(f32[528,1792]{1,0:T(8,128)S(1)} %mul.21, f32[32,1792]{1,0:T(8,128)S(1)} %maximum_select_fusion, f32[561]{0:T(1024)S(1)} %pad.10.clone), kind=kOutput, calls=%fused_computation.24 | convolution fusion | flops 6770085888 | bytes 5275208 | tf_op jit(solution)/shard_map/dot_general | solution.py:154
  116.2 1.4 select_add_fusion.a_ref
  117.5 70.7 %shard_map.77 = f32[640,640]{1,0:T(8,128)} custom-call(f32[640,640]{1,0:T(8,128)} %select_add_fusion.a_ref), custom_call_target="tpu_custom_call" | custom-call | tf_op jit(solution)/shard_map/pallas_call | solution.py:75
  188.3 2.6 %slice.54 = f32[561,561]{1,0:T(8,128)} slice(f32[640,640]{1,0:T(8,128)} %shard_map.77), slice={[0:561], [0:561]} | slice | bytes 2517768 | tf_op jit(solution)/shard_map/slice | solution.py:80
  (38 shorter events, 5.7 us)
Async XLA Ops:
  0.6 11.2 %copy-start.4 = (s32[224]{0:T(256)S(1)}, s32[224]{0:T(256)}, u32[]{:S(2)}) copy-start(s32[224]{0:T(256)} %param.9) | copy-start | bytes 2692
  1.8 28.3 %copy-start = (f32[32,5,2,8,128]{4,3,2,1,0:T(8,128)}, f32[32,5,2,8,128]{4,3,2,1,0:T(8,128)S(1)}, u32[]{:S(2)}) copy-start(f32[32,5,2,8,128]{4,3,2,1,0:T(8,128)S(1)} %convert_multiply_fusion) | copy-start | bytes 3932164
  1.9 21.9 %collective-permute-start = (f32[32,5,1,8,128]{4,3,2,1,0:T(8,128)S(1)}, f32[32,5,1,8,128]{4,3,2,1,0:T(8,128)S(1)}, u32[]{:S(2)}, u32[]{:S(2)}) collective-permute-start(f32[32,5,1,8,128]{4,3,2,1,0:T(8,128)S(1)} %get-tuple-element.8), channel_id=1, source_target_pairs={{1,0},{2,1},{3,2},{4,3},{5,4},{6,5},{7,6},{8,7},{9,8},{10,9},{11,1... | collective-permute-start | bytes 1966088 | tf_op jit(solution)/shard_map/ppermute | solution.py:89
  9.9 20.2 %collective-permute-start.1 = (f32[32,5,1,8,128]{4,3,2,1,0:T(8,128)S(1)}, f32[32,5,1,8,128]{4,3,2,1,0:T(8,128)S(1)}, u32[]{:S(2)}, u32[]{:S(2)}) collective-permute-start(f32[32,5,1,8,128]{4,3,2,1,0:T(8,128)S(1)} %get-tuple-element.7), channel_id=1, source_target_pairs={{0,1},{1,2},{2,3},{3,4},{4,5},{5,6},{6,7},{7,8},{8,9},{9,10},{10,1... | collective-permute-start | bytes 1966088 | tf_op jit(solution)/shard_map/ppermute | solution.py:88
  30.1 0.8 copy-start.1
  47.3 43.0 %copy-start.3 = (s32[528]{0:T(1024)S(1)}, s32[528]{0:T(1024)}, u32[]{:S(2)}) copy-start(s32[528]{0:T(1024)} %constant.127) | copy-start | bytes 6340
  47.3 43.0 %copy-start.2 = (s32[528]{0:T(1024)S(1)}, s32[528]{0:T(1024)}, u32[]{:S(2)}) copy-start(s32[528]{0:T(1024)} %constant.128) | copy-start | bytes 6340
  48.1 4.9 %collective-permute-start.2 = (f32[32,224]{0,1:T(8,128)S(1)}, f32[32,224]{0,1:T(8,128)S(1)}, u32[]{:S(2)}, u32[]{:S(2)}) collective-permute-start(f32[32,224]{0,1:T(8,128)S(1)} %select_bitcast_fusion), channel_id=1, source_target_pairs={{0,1},{1,0},{2,3},{3,2},{4,5},{5,4},{6,7},{7,6},{8,9},{9,8},{10,11... | collective-permute-start | bytes 86024 | tf_op jit(solution)/shard_map/ppermute | solution.py:111
  53.1 7.7 %collective-permute-start.3 = (f32[32,224]{0,1:T(8,128)S(1)}, f32[32,224]{0,1:T(8,128)S(1)}, u32[]{:S(2)}, u32[]{:S(2)}) collective-permute-start(f32[32,224]{0,1:T(8,128)S(1)} %fusion.25), channel_id=1, source_target_pairs={{0,2},{1,3},{2,0},{3,1},{4,6},{5,7},{6,4},{7,5},{8,10},{9,11},{10,... | collective-permute-start | bytes 86024 | tf_op jit(solution)/shard_map/ppermute | solution.py:111
  60.8 8.8 %collective-permute-start.4 = (f32[32,224]{0,1:T(8,128)S(1)}, f32[32,224]{0,1:T(8,128)S(1)}, u32[]{:S(2)}, u32[]{:S(2)}) collective-permute-start(f32[32,224]{0,1:T(8,128)S(1)} %add.76), channel_id=1, source_target_pairs={{0,4},{1,5},{2,6},{3,7},{4,0},{5,1},{6,2},{7,3},{8,12},{9,13},{10,... | collective-permute-start | bytes 86024 | tf_op jit(solution)/shard_map/ppermute | solution.py:111
  69.6 4.9 %collective-permute-start.5 = (f32[32,224]{0,1:T(8,128)S(1)}, f32[32,224]{0,1:T(8,128)S(1)}, u32[]{:S(2)}, u32[]{:S(2)}) collective-permute-start(f32[32,224]{0,1:T(8,128)S(1)} %add.77), channel_id=1, source_target_pairs={{0,8},{1,9},{2,10},{3,11},{4,12},{5,13},{6,14},{7,15},{8,0},{9,1},... | collective-permute-start | bytes 86024 | tf_op jit(solution)/shard_map/ppermute | solution.py:111
  74.5 6.4 %collective-permute-start.6 = (f32[32,224]{0,1:T(8,128)S(1)}, f32[32,224]{0,1:T(8,128)S(1)}, u32[]{:S(2)}, u32[]{:S(2)}) collective-permute-start(f32[32,224]{0,1:T(8,128)S(1)} %add.78), channel_id=1, source_target_pairs={{0,16},{1,17},{2,18},{3,19},{4,20},{5,21},{6,22},{7,23},{8,24},{9,... | collective-permute-start | bytes 86024 | tf_op jit(solution)/shard_map/ppermute | solution.py:111
  80.9 1.4 collective-permute-start.7
  82.5 4.4 %collective-permute-start.8 = (f32[32,448]{1,0:T(8,128)S(1)}, f32[32,448]{1,0:T(8,128)S(1)}, u32[]{:S(2)}, u32[]{:S(2)}) collective-permute-start(f32[32,448]{1,0:T(8,128)S(1)} %maximum_select_fusion.2), channel_id=1, source_target_pairs={{0,64},{32,96},{64,0},{96,32},{128,192},{160,224},{192,128},{224,1... | collective-permute-start | bytes 172040 | tf_op jit(solution)/shard_map/ppermute | solution.py:123
  86.9 6.6 %collective-permute-start.9 = (f32[32,896]{1,0:T(8,128)S(1)}, f32[32,896]{1,0:T(8,128)S(1)}, u32[]{:S(2)}, u32[]{:S(2)}) collective-permute-start(f32[32,896]{1,0:T(8,128)S(1)} %maximum_select_fusion.1), channel_id=1, source_target_pairs={{0,128},{32,160},{64,192},{96,224},{128,0},{160,32},{192,64},{224,... | collective-permute-start | bytes 344072 | tf_op jit(solution)/shard_map/ppermute | solution.py:123
where the time goes:
time: 191 us
  Pallas kernels  70.7 us (37%)
  waiting for transfers between devices  55.8 us (29%)
  matrix products  17.8 us (9%)
  starting transfers between devices  16.3 us (9%)
  other arithmetic  15.6 us (8%)
  local copies, waits for them, and re-layouts  13.7 us (7%)
    pallas_call x1, Pallas kernels, cholesky_upper(): pl.pallas_call(functools.partial(chol_kernel, size=size, valid=n), out_sh...  70.7 us
    ppermute x5, waiting for transfers between devices, butterfly_sum(): x = x + lax.ppermute(x, axis, [(i, i ^ step) for i in range(count)])  31.1 us
    ppermute x1, waiting for transfers between devices, neighbour_planes(): high = lax.ppermute(lax.slice_in_dim(block, 0, 1, axis=dim), axis, backward)  12 us
    dot_general x1, matrix products, body(): lax.dot_general(features_t, features_t, (((1,), (1,)), ((), ())), precisi...  10.3 us
    ppermute x1, starting transfers between devices, neighbour_planes(): high = lax.ppermute(lax.slice_in_dim(block, 0, 1, axis=dim), axis, backward)  7.94 us
    dot_general x1, matrix products, body(): lax.dot_general(adjoint, flat, (((1,), (1,)), ((), ())), precision=lax.Pr...  7.42 us
    ppermute x3, waiting for transfers between devices, butterfly_gather(): other = lax.ppermute(x, axis, [(i, i ^ step) for i in range(count)])  6.49 us
    ppermute x1, waiting for transfers between devices, neighbour_planes(): lax.ppermute(lax.slice_in_dim(block, width - 1, width, axis=dim), axis, f...  6.23 us
  transfers between devices with their start and end apart: 10, of which 10 were waited for; matrix products, arithmetic and copies ran while one was open for 0% of the time, Pallas kernels for 0%

commit v1 on v0

--- a/solution.py
+++ b/solution.py
@@ -45,14 +45,12 @@
 
         def step(j, carry):
             row = blk_ref[pl.ds(j, 1), :]
-            pivot = jnp.sum(jnp.where(row_lanes == j, row, 0.0), axis=1, keepdims=True)
-            scale = lax.rsqrt(pivot)
-            scaled = row * scale
-            block = blk_ref[...]
-            column = jnp.sum(jnp.where(lanes[:, :PANEL] == j, block[:, :PANEL], 0.0), axis=1, keepdims=True)
-            coef = jnp.where(col_rows > j, column * scale, 0.0)
-            updated = block - coef * scaled
-            blk_ref[...] = jnp.where(rows == j, scaled, updated)
+            pivot = jnp.sum(jnp.where(row_lanes[:, :PANEL] == j, row[:, :PANEL], 0.0), axis=1, keepdims=True)
+            scaled = row * lax.rsqrt(pivot)
+            column = jnp.transpose(jnp.broadcast_to(scaled[:, :PANEL], (8, PANEL)))[:, 0:1]
+            coef = jnp.where(col_rows > j, column, 0.0)
+            blk_ref[...] = blk_ref[...] - coef * scaled
+            blk_ref[pl.ds(j, 1), :] = scaled
             return carry
 
         lax.fori_loop(0, steps, step, 0)

time: 191 us -> 272 us (1.42)
  Pallas kernels: 70.7 us -> 152 us
    pallas_call x1, Pallas kernels: 70.7 us -> 152 us  [cholesky_upper(): pl.pallas_call(functools.partial(chol_kernel, size=size, valid=n), out_sh...]
where the time goes in v1:
time: 272 us
  Pallas kernels  152 us (56%)
  waiting for transfers between devices  55.8 us (21%)
  matrix products  17.8 us (7%)
  starting transfers between devices  16.3 us (6%)
  other arithmetic  15.6 us (6%)
  local copies, waits for them, and re-layouts  13.7 us (5%)
    pallas_call x1, Pallas kernels, cholesky_upper(): pl.pallas_call(functools.partial(chol_kernel, size=size, valid=n), out_sh...  152 us
    ppermute x5, waiting for transfers between devices, butterfly_sum(): x = x + lax.ppermute(x, axis, [(i, i ^ step) for i in range(count)])  31.1 us
    ppermute x1, waiting for transfers between devices, neighbour_planes(): high = lax.ppermute(lax.slice_in_dim(block, 0, 1, axis=dim), axis, backward)  12 us
    dot_general x1, matrix products, body(): lax.dot_general(features_t, features_t, (((1,), (1,)), ((), ())), precisi...  10.3 us
    ppermute x1, starting transfers between devices, neighbour_planes(): high = lax.ppermute(lax.slice_in_dim(block, 0, 1, axis=dim), axis, backward)  7.94 us
    dot_general x1, matrix products, body(): lax.dot_general(adjoint, flat, (((1,), (1,)), ((), ())), precision=lax.Pr...  7.42 us
    ppermute x3, waiting for transfers between devices, butterfly_gather(): other = lax.ppermute(x, axis, [(i, i ^ step) for i in range(count)])  6.49 us
    ppermute x1, waiting for transfers between devices, neighbour_planes(): lax.ppermute(lax.slice_in_dim(block, width - 1, width, axis=dim), axis, f...  6.23 us
  transfers between devices with their start and end apart: 10, of which 10 were waited for; matrix products, arithmetic and copies ran while one was open for 0% of the time, Pallas kernels for 0%

profile of v1, /device:TPU:24, one launch (start us, length us, event | category | flops | bytes accessed | tf_op | source)
XLA Modules:
  0.0 271.8 jit_solution(7378624237362529757)
XLA Ops:
  1.9 7.9 %collective-permute-start = (f32[32,5,1,8,128]{4,3,2,1,0:T(8,128)S(1)}, f32[32,5,1,8,128]{4,3,2,1,0:T(8,128)S(1)}, u32[]{:S(2)}, u32[]{:S(2)}) collective-permute-start(f32[32,5,1,8,128]{4,3,2,1,0:T(8,128)S(1)} %get-tuple-element.8), channel_id=1, source_target_pairs={{1,0},{2,1},{3,2},{4,3},{5,4},{6,5},{7,6},{8,7},{9,8},{10,9},{11,1... | collective-permute-start | bytes 1966088 | tf_op jit(solution)/shard_map/ppermute | solution.py:87
  9.9 1.9 collective-permute-start.1
  11.9 12.0 %collective-permute-done = f32[32,5,1,8,128]{4,3,2,1,0:T(8,128)S(1)} collective-permute-done((f32[32,5,1,8,128]{4,3,2,1,0:T(8,128)S(1)}, f32[32,5,1,8,128]{4,3,2,1,0:T(8,128)S(1)}, u32[]{:S(2)}, u32[]{:S(2)}) %collective-permute-start) | collective-permute-done | bytes 655392 | tf_op jit(solution)/shard_map/ppermute | solution.py:87
  23.9 6.2 %collective-permute-done.1 = f32[32,5,1,8,128]{4,3,2,1,0:T(8,128)S(1)} collective-permute-done((f32[32,5,1,8,128]{4,3,2,1,0:T(8,128)S(1)}, f32[32,5,1,8,128]{4,3,2,1,0:T(8,128)S(1)}, u32[]{:S(2)}, u32[]{:S(2)}) %collective-permute-start.1) | collective-permute-done | bytes 655392 | tf_op jit(solution)/shard_map/ppermute | solution.py:86
  30.9 4.5 %select_maximum_fusion = f32[32,5,4,10,130]{4,3,2,1,0:T(8,128)S(1)} fusion(f32[32,5,1,8,128]{4,3,2,1,0:T(8,128)S(1)} %collective-permute-done, f32[32,5,2,8,128]{4,3,2,1,0:T(8,128)S(1)} %convert_multiply_fusion, f32[32,5,1,8,128]{4,3,2,1,0:T(8,128)S(1)} %collective-permute-done.1), kind=kLoop, calls=%fused_computation.7 | loop fusion | flops 12480000 | bytes 5949440 | tf_op jit(solution)/shard_map/concatenate | solution.py:88
  35.5 4.4 %convert_add_fusion = f32[32,5,2,8,128]{4,3,2,1,0:T(8,128)} fusion(bf16[32,5,2,8,128]{4,3,2,1,0:T(8,128)(2,1)} %param.10, f32[32,5,4,10,130]{4,3,2,1,0:T(8,128)S(1)} %select_maximum_fusion, f32[32,5,2,8,128]{4,3,2,1,0:T(8,128)} %copy-done, f32[32,5,1,8,128]{4,3,2,1,0:T(8,128)} %copy-done.1, f32[32,5,1,8,128]{4,3,2,1,0:T(8,128)S(1)} %collective-permute-done), kind=kLoop, calls=%fused_computation.22 | loop fusion | flops 3604480 | bytes 9830400 | tf_op jit(solution)/shard_map/add | solution.py:100
  39.8 7.4 %fusion.17 = f32[32,252]{0,1:T(8,128)S(1)} fusion(bf16[252,5,2,8,128]{4,3,2,1,0:T(8,128)(2,1)} %param.8, f32[32,5,2,8,128]{4,3,2,1,0:T(8,128)} %convert_add_fusion), kind=kOutput, calls=%fused_computation.34 | convolution fusion | flops 990904320 | bytes 6503936 | tf_op jit(solution)/shard_map/dot_general | solution.py:141
  48.2 4.8 %collective-permute-done.2 = f32[32,224]{0,1:T(8,128)S(1)} collective-permute-done((f32[32,224]{0,1:T(8,128)S(1)}, f32[32,224]{0,1:T(8,128)S(1)}, u32[]{:S(2)}, u32[]{:S(2)}) %collective-permute-start.2) | collective-permute-done | bytes 28704 | tf_op jit(solution)/shard_map/ppermute | solution.py:109
  53.2 7.6 %collective-permute-done.3 = f32[32,224]{0,1:T(8,128)S(1)} collective-permute-done((f32[32,224]{0,1:T(8,128)S(1)}, f32[32,224]{0,1:T(8,128)S(1)}, u32[]{:S(2)}, u32[]{:S(2)}) %collective-permute-start.3) | collective-permute-done | bytes 28704 | tf_op jit(solution)/shard_map/ppermute | solution.py:109
  60.9 8.7 %collective-permute-done.4 = f32[32,224]{0,1:T(8,128)S(1)} collective-permute-done((f32[32,224]{0,1:T(8,128)S(1)}, f32[32,224]{0,1:T(8,128)S(1)}, u32[]{:S(2)}, u32[]{:S(2)}) %collective-permute-start.4) | collective-permute-done | bytes 28704 | tf_op jit(solution)/shard_map/ppermute | solution.py:109
  69.7 4.8 %collective-permute-done.5 = f32[32,224]{0,1:T(8,128)S(1)} collective-permute-done((f32[32,224]{0,1:T(8,128)S(1)}, f32[32,224]{0,1:T(8,128)S(1)}, u32[]{:S(2)}, u32[]{:S(2)}) %collective-permute-start.5) | collective-permute-done | bytes 28704 | tf_op jit(solution)/shard_map/ppermute | solution.py:109
  75.6 5.3 %collective-permute-done.6 = f32[32,224]{0,1:T(8,128)S(1)} collective-permute-done((f32[32,224]{0,1:T(8,128)S(1)}, f32[32,224]{0,1:T(8,128)S(1)}, u32[]{:S(2)}, u32[]{:S(2)}) %collective-permute-start.6) | collective-permute-done | bytes 28704 | tf_op jit(solution)/shard_map/ppermute | solution.py:109
  81.1 1.2 collective-permute-done.7
  82.5 1.6 collective-permute-start.8
  84.1 2.8 %collective-permute-done.8 = f32[32,448]{1,0:T(8,128)S(1)} collective-permute-done((f32[32,448]{1,0:T(8,128)S(1)}, f32[32,448]{1,0:T(8,128)S(1)}, u32[]{:S(2)}, u32[]{:S(2)}) %collective-permute-start.8) | collective-permute-done | bytes 57376 | tf_op jit(solution)/shard_map/ppermute | solution.py:121
  86.9 3.3 %collective-permute-start.9 = (f32[32,896]{1,0:T(8,128)S(1)}, f32[32,896]{1,0:T(8,128)S(1)}, u32[]{:S(2)}, u32[]{:S(2)}) collective-permute-start(f32[32,896]{1,0:T(8,128)S(1)} %maximum_select_fusion.1), channel_id=1, source_target_pairs={{0,128},{32,160},{64,192},{96,224},{128,0},{160,32},{192,64},{224,... | collective-permute-start | bytes 344072 | tf_op jit(solution)/shard_map/ppermute | solution.py:121
  91.0 2.5 collective-permute-done.9
  93.5 4.3 %gather_fusion.1 = f32[528,1792]{1,0:T(8,128)} fusion(f32[32,1792]{1,0:T(8,128)S(1)} %maximum_select_fusion, s32[1024]{0:T(1024)S(1)} %pad_clamp_fusion.1), kind=kCustom, calls=%fused_computation.clone | custom fusion | bytes 7571520 | tf_op jit(solution)/shard_map/jit(_take)/gather | solution.py:131
  97.8 4.3 %gather_fusion.2 = f32[528,1792]{1,0:T(8,128)} fusion(f32[32,1792]{1,0:T(8,128)S(1)} %maximum_select_fusion, s32[1024]{0:T(1024)S(1)} %pad_clamp_fusion), kind=kCustom, calls=%fused_computation.1.clone | custom fusion | bytes 7571520 | tf_op jit(solution)/shard_map/jit(_take)/gather | solution.py:131
  102.1 3.7 %mul.21 = f32[528,1792]{1,0:T(8,128)S(1)} multiply(f32[528,1792]{1,0:T(8,128)} %gather_fusion.1, f32[528,1792]{1,0:T(8,128)} %gather_fusion.2) | non-fusion elementwise | flops 946176 | bytes 11354112 | tf_op jit(solution)/shard_map/mul | solution.py:131
  105.8 10.3 %fusion.11 = f32[561,561]{1,0:T(8,128)S(1)} fusion(f32[528,1792]{1,0:T(8,128)S(1)} %mul.21, f32[32,1792]{1,0:T(8,128)S(1)} %maximum_select_fusion, f32[561]{0:T(1024)S(1)} %pad.10.clone), kind=kOutput, calls=%fused_computation.24 | convolution fusion | flops 6770085888 | bytes 5275208 | tf_op jit(solution)/shard_map/dot_general | solution.py:152
  116.2 1.4 select_add_fusion.a_ref
  117.5 151.7 %shard_map.77 = f32[640,640]{1,0:T(8,128)} custom-call(f32[640,640]{1,0:T(8,128)} %select_add_fusion.a_ref), custom_call_target="tpu_custom_call" | custom-call | tf_op jit(solution)/shard_map/pallas_call | solution.py:73
  269.2 2.6 slice.54
  (38 shorter events, 5.7 us)
Async XLA Ops:
  0.6 11.2 %copy-start.4 = (s32[224]{0:T(256)S(1)}, s32[224]{0:T(256)}, u32[]{:S(2)}) copy-start(s32[224]{0:T(256)} %param.9) | copy-start | bytes 2692
  1.8 28.3 %copy-start = (f32[32,5,2,8,128]{4,3,2,1,0:T(8,128)}, f32[32,5,2,8,128]{4,3,2,1,0:T(8,128)S(1)}, u32[]{:S(2)}) copy-start(f32[32,5,2,8,128]{4,3,2,1,0:T(8,128)S(1)} %convert_multiply_fusion) | copy-start | bytes 3932164
  1.9 21.9 %collective-permute-start = (f32[32,5,1,8,128]{4,3,2,1,0:T(8,128)S(1)}, f32[32,5,1,8,128]{4,3,2,1,0:T(8,128)S(1)}, u32[]{:S(2)}, u32[]{:S(2)}) collective-permute-start(f32[32,5,1,8,128]{4,3,2,1,0:T(8,128)S(1)} %get-tuple-element.8), channel_id=1, source_target_pairs={{1,0},{2,1},{3,2},{4,3},{5,4},{6,5},{7,6},{8,7},{9,8},{10,9},{11,1... | collective-permute-start | bytes 1966088 | tf_op jit(solution)/shard_map/ppermute | solution.py:87
  9.9 20.2 %collective-permute-start.1 = (f32[32,5,1,8,128]{4,3,2,1,0:T(8,128)S(1)}, f32[32,5,1,8,128]{4,3,2,1,0:T(8,128)S(1)}, u32[]{:S(2)}, u32[]{:S(2)}) collective-permute-start(f32[32,5,1,8,128]{4,3,2,1,0:T(8,128)S(1)} %get-tuple-element.7), channel_id=1, source_target_pairs={{0,1},{1,2},{2,3},{3,4},{4,5},{5,6},{6,7},{7,8},{8,9},{9,10},{10,1... | collective-permute-start | bytes 1966088 | tf_op jit(solution)/shard_map/ppermute | solution.py:86
  30.1 0.8 copy-start.1
  47.3 43.0 %copy-start.3 = (s32[528]{0:T(1024)S(1)}, s32[528]{0:T(1024)}, u32[]{:S(2)}) copy-start(s32[528]{0:T(1024)} %constant.127) | copy-start | bytes 6340
  47.3 43.0 %copy-start.2 = (s32[528]{0:T(1024)S(1)}, s32[528]{0:T(1024)}, u32[]{:S(2)}) copy-start(s32[528]{0:T(1024)} %constant.128) | copy-start | bytes 6340
  48.1 4.9 %collective-permute-start.2 = (f32[32,224]{0,1:T(8,128)S(1)}, f32[32,224]{0,1:T(8,128)S(1)}, u32[]{:S(2)}, u32[]{:S(2)}) collective-permute-start(f32[32,224]{0,1:T(8,128)S(1)} %select_bitcast_fusion), channel_id=1, source_target_pairs={{0,1},{1,0},{2,3},{3,2},{4,5},{5,4},{6,7},{7,6},{8,9},{9,8},{10,11... | collective-permute-start | bytes 86024 | tf_op jit(solution)/shard_map/ppermute | solution.py:109
  53.1 7.7 %collective-permute-start.3 = (f32[32,224]{0,1:T(8,128)S(1)}, f32[32,224]{0,1:T(8,128)S(1)}, u32[]{:S(2)}, u32[]{:S(2)}) collective-permute-start(f32[32,224]{0,1:T(8,128)S(1)} %fusion.25), channel_id=1, source_target_pairs={{0,2},{1,3},{2,0},{3,1},{4,6},{5,7},{6,4},{7,5},{8,10},{9,11},{10,... | collective-permute-start | bytes 86024 | tf_op jit(solution)/shard_map/ppermute | solution.py:109
  60.8 8.8 %collective-permute-start.4 = (f32[32,224]{0,1:T(8,128)S(1)}, f32[32,224]{0,1:T(8,128)S(1)}, u32[]{:S(2)}, u32[]{:S(2)}) collective-permute-start(f32[32,224]{0,1:T(8,128)S(1)} %add.76), channel_id=1, source_target_pairs={{0,4},{1,5},{2,6},{3,7},{4,0},{5,1},{6,2},{7,3},{8,12},{9,13},{10,... | collective-permute-start | bytes 86024 | tf_op jit(solution)/shard_map/ppermute | solution.py:109
  69.6 4.9 %collective-permute-start.5 = (f32[32,224]{0,1:T(8,128)S(1)}, f32[32,224]{0,1:T(8,128)S(1)}, u32[]{:S(2)}, u32[]{:S(2)}) collective-permute-start(f32[32,224]{0,1:T(8,128)S(1)} %add.77), channel_id=1, source_target_pairs={{0,8},{1,9},{2,10},{3,11},{4,12},{5,13},{6,14},{7,15},{8,0},{9,1},... | collective-permute-start | bytes 86024 | tf_op jit(solution)/shard_map/ppermute | solution.py:109
  74.5 6.4 %collective-permute-start.6 = (f32[32,224]{0,1:T(8,128)S(1)}, f32[32,224]{0,1:T(8,128)S(1)}, u32[]{:S(2)}, u32[]{:S(2)}) collective-permute-start(f32[32,224]{0,1:T(8,128)S(1)} %add.78), channel_id=1, source_target_pairs={{0,16},{1,17},{2,18},{3,19},{4,20},{5,21},{6,22},{7,23},{8,24},{9,... | collective-permute-start | bytes 86024 | tf_op jit(solution)/shard_map/ppermute | solution.py:109
  80.9 1.4 collective-permute-start.7
  82.5 4.4 %collective-permute-start.8 = (f32[32,448]{1,0:T(8,128)S(1)}, f32[32,448]{1,0:T(8,128)S(1)}, u32[]{:S(2)}, u32[]{:S(2)}) collective-permute-start(f32[32,448]{1,0:T(8,128)S(1)} %maximum_select_fusion.2), channel_id=1, source_target_pairs={{0,64},{32,96},{64,0},{96,32},{128,192},{160,224},{192,128},{224,1... | collective-permute-start | bytes 172040 | tf_op jit(solution)/shard_map/ppermute | solution.py:121
  86.9 6.6 %collective-permute-start.9 = (f32[32,896]{1,0:T(8,128)S(1)}, f32[32,896]{1,0:T(8,128)S(1)}, u32[]{:S(2)}, u32[]{:S(2)}) collective-permute-start(f32[32,896]{1,0:T(8,128)S(1)} %maximum_select_fusion.1), channel_id=1, source_target_pairs={{0,128},{32,160},{64,192},{96,224},{128,0},{160,32},{192,64},{224,... | collective-permute-start | bytes 344072 | tf_op jit(solution)/shard_map/ppermute | solution.py:121

commit v2 on v1

--- a/solution.py
+++ b/solution.py
@@ -34,26 +34,39 @@
     rows = lax.broadcasted_iota(jnp.int32, (PANEL, 2 * PANEL), 0)
     lanes = lax.broadcasted_iota(jnp.int32, (PANEL, 2 * PANEL), 1)
     eye = (rows[:, :PANEL] == lanes[:, :PANEL]).astype(jnp.float32)
-    row_lanes = lax.broadcasted_iota(jnp.int32, (1, 2 * PANEL), 1)
+    group_lanes = lax.broadcasted_iota(jnp.int32, (8, PANEL), 1)
+    group_rows = lax.broadcasted_iota(jnp.int32, (8, 1), 0)
     col_rows = lax.broadcasted_iota(jnp.int32, (PANEL, 1), 0)
     for p in range(panels):
         c0 = p * PANEL
         c1 = c0 + PANEL
-        steps = min(PANEL, valid - c0)
+        groups = -(-min(PANEL, valid - c0) // 8)
         blk_ref[:, :PANEL] = w_ref[c0:c1, c0:c1]
         blk_ref[:, PANEL:] = eye
 
-        def step(j, carry):
-            row = blk_ref[pl.ds(j, 1), :]
-            pivot = jnp.sum(jnp.where(row_lanes[:, :PANEL] == j, row[:, :PANEL], 0.0), axis=1, keepdims=True)
-            scaled = row * lax.rsqrt(pivot)
-            column = jnp.transpose(jnp.broadcast_to(scaled[:, :PANEL], (8, PANEL)))[:, 0:1]
-            coef = jnp.where(col_rows > j, column, 0.0)
-            blk_ref[...] = blk_ref[...] - coef * scaled
-            blk_ref[pl.ds(j, 1), :] = scaled
+        def group_step(g, carry):
+            base = pl.multiple_of(g * 8, 8)
+            eight = blk_ref[pl.ds(base, 8), :]
+            for i in range(8):
+                j = base + i
+                row = eight[i : i + 1, :]
+                hit = group_lanes == j
+                pivot = jnp.sum(jnp.where(hit[:1], row[:, :PANEL], 0.0), axis=1, keepdims=True)
+                scale = lax.rsqrt(pivot)
+                scaled = row * scale
+                column = jnp.sum(jnp.where(hit, eight[:, :PANEL], 0.0), axis=1, keepdims=True)
+                coef = jnp.where(group_rows > i, column * scale, 0.0)
+                eight = jnp.where(group_rows == i, scaled, eight - coef * scaled)
+            blk_ref[pl.ds(base, 8), :] = eight
+            lead = jnp.transpose(eight[:, :PANEL])
+            lead = jnp.where(col_rows >= base + 8, lead, 0.0)
+            block = blk_ref[...]
+            for i in range(8):
+                block = block - lead[:, i : i + 1] * eight[i : i + 1, :]
+            blk_ref[...] = block
             return carry
 
-        lax.fori_loop(0, steps, step, 0)
+        lax.fori_loop(0, groups, group_step, 0)
         block = blk_ref[...]
         upper = jnp.where(lanes[:, :PANEL] >= rows[:, :PANEL], block[:, :PANEL], 0.0)
         r_ref[c0:c1, c0:c1] = upper

time: 272 us -> 201 us (0.74)
  Pallas kernels: 152 us -> 80.4 us
    pallas_call x1, Pallas kernels: 152 us -> 80.4 us  [cholesky_upper(): pl.pallas_call(functools.partial(chol_kernel, size=size, valid=n), out_sh...]
where the time goes in v2:
time: 201 us; the launch traced here: 200 us
  Pallas kernels  80.4 us (40%)
  waiting for transfers between devices  55.8 us (28%)
  matrix products  17.8 us (9%)
  starting transfers between devices  16.1 us (8%)
  other arithmetic  15.6 us (8%)
  local copies, waits for them, and re-layouts  13.8 us (7%)
    pallas_call x1, Pallas kernels, cholesky_upper(): pl.pallas_call(functools.partial(chol_kernel, size=size, valid=n), out_sh...  80.4 us
    ppermute x5, waiting for transfers between devices, butterfly_sum(): x = x + lax.ppermute(x, axis, [(i, i ^ step) for i in range(count)])  31.1 us
    ppermute x1, waiting for transfers between devices, neighbour_planes(): high = lax.ppermute(lax.slice_in_dim(block, 0, 1, axis=dim), axis, backward)  12 us
    dot_general x1, matrix products, body(): lax.dot_general(features_t, features_t, (((1,), (1,)), ((), ())), precisi...  10.3 us
    ppermute x1, starting transfers between devices, neighbour_planes(): high = lax.ppermute(lax.slice_in_dim(block, 0, 1, axis=dim), axis, backward)  7.94 us
    dot_general x1, matrix products, body(): lax.dot_general(adjoint, flat, (((1,), (1,)), ((), ())), precision=lax.Pr...  7.42 us
    ppermute x3, waiting for transfers between devices, butterfly_gather(): other = lax.ppermute(x, axis, [(i, i ^ step) for i in range(count)])  6.48 us
    ppermute x1, waiting for transfers between devices, neighbour_planes(): lax.ppermute(lax.slice_in_dim(block, width - 1, width, axis=dim), axis, f...  6.23 us
  transfers between devices with their start and end apart: 10, of which 10 were waited for; matrix products, arithmetic and copies ran while one was open for 0% of the time, Pallas kernels for 0%

profile of v2, /device:TPU:24, one launch (start us, length us, event | category | flops | bytes accessed | tf_op | source)
XLA Modules:
  0.0 200.4 jit_solution(12667970026702487174)
XLA Ops:
  1.9 7.9 %collective-permute-start = (f32[32,5,1,8,128]{4,3,2,1,0:T(8,128)S(1)}, f32[32,5,1,8,128]{4,3,2,1,0:T(8,128)S(1)}, u32[]{:S(2)}, u32[]{:S(2)}) collective-permute-start(f32[32,5,1,8,128]{4,3,2,1,0:T(8,128)S(1)} %get-tuple-element.8), channel_id=1, source_target_pairs={{1,0},{2,1},{3,2},{4,3},{5,4},{6,5},{7,6},{8,7},{9,8},{10,9},{11,1... | collective-permute-start | bytes 1966088 | tf_op jit(solution)/shard_map/ppermute | solution.py:100
  9.9 1.9 collective-permute-start.1
  11.9 12.0 %collective-permute-done = f32[32,5,1,8,128]{4,3,2,1,0:T(8,128)S(1)} collective-permute-done((f32[32,5,1,8,128]{4,3,2,1,0:T(8,128)S(1)}, f32[32,5,1,8,128]{4,3,2,1,0:T(8,128)S(1)}, u32[]{:S(2)}, u32[]{:S(2)}) %collective-permute-start) | collective-permute-done | bytes 655392 | tf_op jit(solution)/shard_map/ppermute | solution.py:100
  23.9 6.2 %collective-permute-done.1 = f32[32,5,1,8,128]{4,3,2,1,0:T(8,128)S(1)} collective-permute-done((f32[32,5,1,8,128]{4,3,2,1,0:T(8,128)S(1)}, f32[32,5,1,8,128]{4,3,2,1,0:T(8,128)S(1)}, u32[]{:S(2)}, u32[]{:S(2)}) %collective-permute-start.1) | collective-permute-done | bytes 655392 | tf_op jit(solution)/shard_map/ppermute | solution.py:99
  30.9 4.5 %select_maximum_fusion = f32[32,5,4,10,130]{4,3,2,1,0:T(8,128)S(1)} fusion(f32[32,5,1,8,128]{4,3,2,1,0:T(8,128)S(1)} %collective-permute-done, f32[32,5,2,8,128]{4,3,2,1,0:T(8,128)S(1)} %convert_multiply_fusion, f32[32,5,1,8,128]{4,3,2,1,0:T(8,128)S(1)} %collective-permute-done.1), kind=kLoop, calls=%fused_computation.7 | loop fusion | flops 12480000 | bytes 5949440 | tf_op jit(solution)/shard_map/concatenate | solution.py:101
  35.5 4.4 %convert_add_fusion = f32[32,5,2,8,128]{4,3,2,1,0:T(8,128)} fusion(bf16[32,5,2,8,128]{4,3,2,1,0:T(8,128)(2,1)} %param.10, f32[32,5,4,10,130]{4,3,2,1,0:T(8,128)S(1)} %select_maximum_fusion, f32[32,5,2,8,128]{4,3,2,1,0:T(8,128)} %copy-done, f32[32,5,1,8,128]{4,3,2,1,0:T(8,128)} %copy-done.1, f32[32,5,1,8,128]{4,3,2,1,0:T(8,128)S(1)} %collective-permute-done), kind=kLoop, calls=%fused_computation.22 | loop fusion | flops 3604480 | bytes 9830400 | tf_op jit(solution)/shard_map/add | solution.py:113
  39.8 7.4 %fusion.17 = f32[32,252]{0,1:T(8,128)S(1)} fusion(bf16[252,5,2,8,128]{4,3,2,1,0:T(8,128)(2,1)} %param.8, f32[32,5,2,8,128]{4,3,2,1,0:T(8,128)} %convert_add_fusion), kind=kOutput, calls=%fused_computation.34 | convolution fusion | flops 990904320 | bytes 6503936 | tf_op jit(solution)/shard_map/dot_general | solution.py:154
  48.2 4.8 %collective-permute-done.2 = f32[32,224]{0,1:T(8,128)S(1)} collective-permute-done((f32[32,224]{0,1:T(8,128)S(1)}, f32[32,224]{0,1:T(8,128)S(1)}, u32[]{:S(2)}, u32[]{:S(2)}) %collective-permute-start.2) | collective-permute-done | bytes 28704 | tf_op jit(solution)/shard_map/ppermute | solution.py:122
  53.2 7.6 %collective-permute-done.3 = f32[32,224]{0,1:T(8,128)S(1)} collective-permute-done((f32[32,224]{0,1:T(8,128)S(1)}, f32[32,224]{0,1:T(8,128)S(1)}, u32[]{:S(2)}, u32[]{:S(2)}) %collective-permute-start.3) | collective-permute-done | bytes 28704 | tf_op jit(solution)/shard_map/ppermute | solution.py:122
  60.9 8.7 %collective-permute-done.4 = f32[32,224]{0,1:T(8,128)S(1)} collective-permute-done((f32[32,224]{0,1:T(8,128)S(1)}, f32[32,224]{0,1:T(8,128)S(1)}, u32[]{:S(2)}, u32[]{:S(2)}) %collective-permute-start.4) | collective-permute-done | bytes 28704 | tf_op jit(solution)/shard_map/ppermute | solution.py:122
  69.7 4.8 %collective-permute-done.5 = f32[32,224]{0,1:T(8,128)S(1)} collective-permute-done((f32[32,224]{0,1:T(8,128)S(1)}, f32[32,224]{0,1:T(8,128)S(1)}, u32[]{:S(2)}, u32[]{:S(2)}) %collective-permute-start.5) | collective-permute-done | bytes 28704 | tf_op jit(solution)/shard_map/ppermute | solution.py:122
  75.6 5.3 %collective-permute-done.6 = f32[32,224]{0,1:T(8,128)S(1)} collective-permute-done((f32[32,224]{0,1:T(8,128)S(1)}, f32[32,224]{0,1:T(8,128)S(1)}, u32[]{:S(2)}, u32[]{:S(2)}) %collective-permute-start.6) | collective-permute-done | bytes 28704 | tf_op jit(solution)/shard_map/ppermute | solution.py:122
  81.1 1.2 collective-permute-done.7
  82.5 1.6 collective-permute-start.8
  84.1 2.8 %collective-permute-done.8 = f32[32,448]{1,0:T(8,128)S(1)} collective-permute-done((f32[32,448]{1,0:T(8,128)S(1)}, f32[32,448]{1,0:T(8,128)S(1)}, u32[]{:S(2)}, u32[]{:S(2)}) %collective-permute-start.8) | collective-permute-done | bytes 57376 | tf_op jit(solution)/shard_map/ppermute | solution.py:134
  86.9 3.1 %collective-permute-start.9 = (f32[32,896]{1,0:T(8,128)S(1)}, f32[32,896]{1,0:T(8,128)S(1)}, u32[]{:S(2)}, u32[]{:S(2)}) collective-permute-start(f32[32,896]{1,0:T(8,128)S(1)} %maximum_select_fusion.1), channel_id=1, source_target_pairs={{0,128},{32,160},{64,192},{96,224},{128,0},{160,32},{192,64},{224,... | collective-permute-start | bytes 344072 | tf_op jit(solution)/shard_map/ppermute | solution.py:134
  90.8 2.5 %collective-permute-done.9 = f32[32,896]{1,0:T(8,128)S(1)} collective-permute-done((f32[32,896]{1,0:T(8,128)S(1)}, f32[32,896]{1,0:T(8,128)S(1)}, u32[]{:S(2)}, u32[]{:S(2)}) %collective-permute-start.9) | collective-permute-done | bytes 114720 | tf_op jit(solution)/shard_map/ppermute | solution.py:134
  93.3 4.5 %gather_fusion.1 = f32[528,1792]{1,0:T(8,128)} fusion(f32[32,1792]{1,0:T(8,128)S(1)} %maximum_select_fusion, s32[1024]{0:T(1024)S(1)} %pad_clamp_fusion.1), kind=kCustom, calls=%fused_computation.clone | custom fusion | bytes 7571520 | tf_op jit(solution)/shard_map/jit(_take)/gather | solution.py:144
  97.8 4.3 %gather_fusion.2 = f32[528,1792]{1,0:T(8,128)} fusion(f32[32,1792]{1,0:T(8,128)S(1)} %maximum_select_fusion, s32[1024]{0:T(1024)S(1)} %pad_clamp_fusion), kind=kCustom, calls=%fused_computation.1.clone | custom fusion | bytes 7571520 | tf_op jit(solution)/shard_map/jit(_take)/gather | solution.py:144
  102.1 3.7 %mul.21 = f32[528,1792]{1,0:T(8,128)S(1)} multiply(f32[528,1792]{1,0:T(8,128)} %gather_fusion.1, f32[528,1792]{1,0:T(8,128)} %gather_fusion.2) | non-fusion elementwise | flops 946176 | bytes 11354112 | tf_op jit(solution)/shard_map/mul | solution.py:144
  105.8 10.3 %fusion.11 = f32[561,561]{1,0:T(8,128)S(1)} fusion(f32[528,1792]{1,0:T(8,128)S(1)} %mul.21, f32[32,1792]{1,0:T(8,128)S(1)} %maximum_select_fusion, f32[561]{0:T(1024)S(1)} %pad.10.clone), kind=kOutput, calls=%fused_computation.24 | convolution fusion | flops 6770085888 | bytes 5275208 | tf_op jit(solution)/shard_map/dot_general | solution.py:165
  116.2 1.4 select_add_fusion.a_ref
  117.5 80.4 %shard_map.77 = f32[640,640]{1,0:T(8,128)} custom-call(f32[640,640]{1,0:T(8,128)} %select_add_fusion.a_ref), custom_call_target="tpu_custom_call" | custom-call | tf_op jit(solution)/shard_map/pallas_call | solution.py:86
  197.9 2.6 %slice.54 = f32[561,561]{1,0:T(8,128)} slice(f32[640,640]{1,0:T(8,128)} %shard_map.77), slice={[0:561], [0:561]} | slice | bytes 2517768 | tf_op jit(solution)/shard_map/slice | solution.py:91
  (38 shorter events, 5.7 us)
Async XLA Ops:
  0.6 11.2 %copy-start.4 = (s32[224]{0:T(256)S(1)}, s32[224]{0:T(256)}, u32[]{:S(2)}) copy-start(s32[224]{0:T(256)} %param.9) | copy-start | bytes 2692
  1.8 28.3 %copy-start = (f32[32,5,2,8,128]{4,3,2,1,0:T(8,128)}, f32[32,5,2,8,128]{4,3,2,1,0:T(8,128)S(1)}, u32[]{:S(2)}) copy-start(f32[32,5,2,8,128]{4,3,2,1,0:T(8,128)S(1)} %convert_multiply_fusion) | copy-start | bytes 3932164
  1.9 21.9 %collective-permute-start = (f32[32,5,1,8,128]{4,3,2,1,0:T(8,128)S(1)}, f32[32,5,1,8,128]{4,3,2,1,0:T(8,128)S(1)}, u32[]{:S(2)}, u32[]{:S(2)}) collective-permute-start(f32[32,5,1,8,128]{4,3,2,1,0:T(8,128)S(1)} %get-tuple-element.8), channel_id=1, source_target_pairs={{1,0},{2,1},{3,2},{4,3},{5,4},{6,5},{7,6},{8,7},{9,8},{10,9},{11,1... | collective-permute-start | bytes 1966088 | tf_op jit(solution)/shard_map/ppermute | solution.py:100
  9.9 20.2 %collective-permute-start.1 = (f32[32,5,1,8,128]{4,3,2,1,0:T(8,128)S(1)}, f32[32,5,1,8,128]{4,3,2,1,0:T(8,128)S(1)}, u32[]{:S(2)}, u32[]{:S(2)}) collective-permute-start(f32[32,5,1,8,128]{4,3,2,1,0:T(8,128)S(1)} %get-tuple-element.7), channel_id=1, source_target_pairs={{0,1},{1,2},{2,3},{3,4},{4,5},{5,6},{6,7},{7,8},{8,9},{9,10},{10,1... | collective-permute-start | bytes 1966088 | tf_op jit(solution)/shard_map/ppermute | solution.py:99
  30.1 0.8 copy-start.1
  47.3 42.8 %copy-start.3 = (s32[528]{0:T(1024)S(1)}, s32[528]{0:T(1024)}, u32[]{:S(2)}) copy-start(s32[528]{0:T(1024)} %constant.127) | copy-start | bytes 6340
  47.3 42.8 %copy-start.2 = (s32[528]{0:T(1024)S(1)}, s32[528]{0:T(1024)}, u32[]{:S(2)}) copy-start(s32[528]{0:T(1024)} %constant.128) | copy-start | bytes 6340
  48.1 4.9 %collective-permute-start.2 = (f32[32,224]{0,1:T(8,128)S(1)}, f32[32,224]{0,1:T(8,128)S(1)}, u32[]{:S(2)}, u32[]{:S(2)}) collective-permute-start(f32[32,224]{0,1:T(8,128)S(1)} %select_bitcast_fusion), channel_id=1, source_target_pairs={{0,1},{1,0},{2,3},{3,2},{4,5},{5,4},{6,7},{7,6},{8,9},{9,8},{10,11... | collective-permute-start | bytes 86024 | tf_op jit(solution)/shard_map/ppermute | solution.py:122
  53.1 7.7 %collective-permute-start.3 = (f32[32,224]{0,1:T(8,128)S(1)}, f32[32,224]{0,1:T(8,128)S(1)}, u32[]{:S(2)}, u32[]{:S(2)}) collective-permute-start(f32[32,224]{0,1:T(8,128)S(1)} %fusion.25), channel_id=1, source_target_pairs={{0,2},{1,3},{2,0},{3,1},{4,6},{5,7},{6,4},{7,5},{8,10},{9,11},{10,... | collective-permute-start | bytes 86024 | tf_op jit(solution)/shard_map/ppermute | solution.py:122
  60.8 8.8 %collective-permute-start.4 = (f32[32,224]{0,1:T(8,128)S(1)}, f32[32,224]{0,1:T(8,128)S(1)}, u32[]{:S(2)}, u32[]{:S(2)}) collective-permute-start(f32[32,224]{0,1:T(8,128)S(1)} %add.76), channel_id=1, source_target_pairs={{0,4},{1,5},{2,6},{3,7},{4,0},{5,1},{6,2},{7,3},{8,12},{9,13},{10,... | collective-permute-start | bytes 86024 | tf_op jit(solution)/shard_map/ppermute | solution.py:122
  69.6 4.9 %collective-permute-start.5 = (f32[32,224]{0,1:T(8,128)S(1)}, f32[32,224]{0,1:T(8,128)S(1)}, u32[]{:S(2)}, u32[]{:S(2)}) collective-permute-start(f32[32,224]{0,1:T(8,128)S(1)} %add.77), channel_id=1, source_target_pairs={{0,8},{1,9},{2,10},{3,11},{4,12},{5,13},{6,14},{7,15},{8,0},{9,1},... | collective-permute-start | bytes 86024 | tf_op jit(solution)/shard_map/ppermute | solution.py:122
  74.5 6.4 %collective-permute-start.6 = (f32[32,224]{0,1:T(8,128)S(1)}, f32[32,224]{0,1:T(8,128)S(1)}, u32[]{:S(2)}, u32[]{:S(2)}) collective-permute-start(f32[32,224]{0,1:T(8,128)S(1)} %add.78), channel_id=1, source_target_pairs={{0,16},{1,17},{2,18},{3,19},{4,20},{5,21},{6,22},{7,23},{8,24},{9,... | collective-permute-start | bytes 86024 | tf_op jit(solution)/shard_map/ppermute | solution.py:122
  80.9 1.4 collective-permute-start.7
  82.5 4.4 %collective-permute-start.8 = (f32[32,448]{1,0:T(8,128)S(1)}, f32[32,448]{1,0:T(8,128)S(1)}, u32[]{:S(2)}, u32[]{:S(2)}) collective-permute-start(f32[32,448]{1,0:T(8,128)S(1)} %maximum_select_fusion.2), channel_id=1, source_target_pairs={{0,64},{32,96},{64,0},{96,32},{128,192},{160,224},{192,128},{224,1... | collective-permute-start | bytes 172040 | tf_op jit(solution)/shard_map/ppermute | solution.py:134
  86.9 6.4 %collective-permute-start.9 = (f32[32,896]{1,0:T(8,128)S(1)}, f32[32,896]{1,0:T(8,128)S(1)}, u32[]{:S(2)}, u32[]{:S(2)}) collective-permute-start(f32[32,896]{1,0:T(8,128)S(1)} %maximum_select_fusion.1), channel_id=1, source_target_pairs={{0,128},{32,160},{64,192},{96,224},{128,0},{160,32},{192,64},{224,... | collective-permute-start | bytes 344072 | tf_op jit(solution)/shard_map/ppermute | solution.py:134

commit v3 on v0

--- a/solution.py
+++ b/solution.py
@@ -87,19 +87,18 @@
     width = block.shape[dim]
     low = lax.ppermute(lax.slice_in_dim(block, width - 1, width, axis=dim), axis, forward)
     high = lax.ppermute(lax.slice_in_dim(block, 0, 1, axis=dim), axis, backward)
-    return jnp.concatenate([low, block, high], axis=dim)
+    return low, high
 
 
-def adjoint_basis(basis, kappa):
+def interior_adjoint(basis, kappa):
     wide = basis.astype(jnp.float32)
     scaled = kappa[None] * wide
-    padded = neighbour_planes(scaled, "space", 2)
-    padded = jnp.pad(padded, ((0, 0), (0, 0), (0, 0), (1, 1), (1, 1)))
+    padded = jnp.pad(scaled, ((0, 0), (0, 0), (1, 1), (1, 1), (1, 1)))
     center = padded[:, :, 1:-1, 1:-1, 1:-1]
     beside = padded[:, :, 2:, 1:-1, 1:-1] + padded[:, :, :-2, 1:-1, 1:-1]
     beside = beside + padded[:, :, 1:-1, 2:, 1:-1] + padded[:, :, 1:-1, :-2, 1:-1]
     beside = beside + padded[:, :, 1:-1, 1:-1, 2:] + padded[:, :, 1:-1, 1:-1, :-2]
-    return wide + (beside - 6.0 * center)
+    return wide + (beside - 6.0 * center), scaled
 
 
 def butterfly_sum(x, axis):
@@ -135,18 +134,27 @@
     return jnp.concatenate([ones, coeffs_t, quad], axis=0)
 
 
-def body(snapshots, picks, basis, kappa):
-    modes = basis.shape[0]
-    adjoint = adjoint_basis(basis, kappa).reshape(modes, -1)
-    stored = snapshots.shape[0]
-    flat = snapshots.reshape(stored, -1).astype(jnp.float32)
-    partial_t = lax.dot_general(
-        adjoint,
-        flat,
+def project(left, right):
+    return lax.dot_general(
+        left,
+        right,
         (((1,), (1,)), ((), ())),
         precision=lax.Precision.HIGHEST,
         preferred_element_type=jnp.float32,
     )
+
+
+def body(snapshots, picks, basis, kappa):
+    modes = basis.shape[0]
+    stored = snapshots.shape[0]
+    inner, scaled = interior_adjoint(basis, kappa)
+    low, high = neighbour_planes(scaled, "space", 2)
+    flat = snapshots.reshape(stored, -1).astype(jnp.float32)
+    partial_t = project(inner.reshape(modes, -1), flat)
+    first = snapshots[:, :, 0].reshape(stored, -1).astype(jnp.float32)
+    last = snapshots[:, :, -1].reshape(stored, -1).astype(jnp.float32)
+    edges = project(low.reshape(modes, -1), first) + project(high.reshape(modes, -1), last)
+    partial_t = partial_t + edges
     part_t = jnp.take(partial_t, picks, axis=1)
     own_t = butterfly_sum(part_t, "space")
     coeffs_t = butterfly_gather(own_t, "tm", 1)

time: 191 us -> 177 us (0.927)
  waiting for transfers between devices: 55.8 us -> 46.5 us
  other arithmetic: 15.6 us -> 6.84 us
  matrix products: 17.8 us -> 21.4 us
    ppermute x1, waiting for transfers between devices: 12 us -> 4.34 us  [neighbour_planes(): high = lax.ppermute(lax.slice_in_dim(block, 0, 1, axis=dim), axis, backward)]
    concatenate x1 -> x0, other arithmetic: 4.53 us -> none  [neighbour_planes(): return jnp.concatenate([low, block, high], axis=dim)]
    add x1 -> x0, other arithmetic: 4.37 us -> none  [adjoint_basis(): return wide + (beside - 6.0 * center)]
    dot_general x1 -> x3, matrix products: 7.42 us -> 11.1 us  [project(): lax.dot_general(left, right, (((1,), (1,)), ((), ())), precision=lax.Prec...]
    ppermute x1, waiting for transfers between devices: 6.23 us -> 4.18 us  [neighbour_planes(): lax.ppermute(lax.slice_in_dim(block, width - 1, width, axis=dim), axis, f...]
  transfers between devices with their start and end apart: 10 -> 10, of which waited for: 10 -> 10; matrix products, arithmetic and copies ran while one was open for 0% -> 6% of each run, Pallas kernels for 0% -> 0%
where the time goes in v3:
time: 177 us
  Pallas kernels  70.8 us (40%)
  waiting for transfers between devices  46.5 us (26%)
  matrix products  21.4 us (12%)
  starting transfers between devices  16.3 us (9%)
  local copies, waits for them, and re-layouts  13.8 us (8%)
  other arithmetic  6.84 us (4%)
    pallas_call x1, Pallas kernels, cholesky_upper(): pl.pallas_call(functools.partial(chol_kernel, size=size, valid=n), out_sh...  70.8 us
    ppermute x5, waiting for transfers between devices, butterfly_sum(): x = x + lax.ppermute(x, axis, [(i, i ^ step) for i in range(count)])  31.5 us
    dot_general x3, matrix products, project(): lax.dot_general(left, right, (((1,), (1,)), ((), ())), precision=lax.Prec...  11.1 us
    dot_general x1, matrix products, body(): lax.dot_general(features_t, features_t, (((1,), (1,)), ((), ())), precisi...  10.3 us
    ppermute x1, starting transfers between devices, neighbour_planes(): high = lax.ppermute(lax.slice_in_dim(block, 0, 1, axis=dim), axis, backward)  8.08 us
    ppermute x3, waiting for transfers between devices, butterfly_gather(): other = lax.ppermute(x, axis, [(i, i ^ step) for i in range(count)])  6.48 us
    ppermute x3, starting transfers between devices, butterfly_gather(): other = lax.ppermute(x, axis, [(i, i ^ step) for i in range(count)])  4.96 us
    ppermute x1, waiting for transfers between devices, neighbour_planes(): high = lax.ppermute(lax.slice_in_dim(block, 0, 1, axis=dim), axis, backward)  4.34 us
  transfers between devices with their start and end apart: 10, of which 10 were waited for; matrix products, arithmetic and copies ran while one was open for 6% of the time, Pallas kernels for 0%

profile of v3, /device:TPU:24, one launch (start us, length us, event | category | flops | bytes accessed | tf_op | source)
XLA Modules:
  0.0 176.6 jit_solution(10112502834208196061)
XLA Ops:
  0.6 1.3 convert_multiply_fusion
  2.1 8.1 %collective-permute-start.1 = (f32[32,5,1,8,128]{4,0,3,1,2:T(8,128)S(1)}, f32[32,5,1,8,128]{4,0,3,1,2:T(8,128)S(1)}, u32[]{:S(2)}, u32[]{:S(2)}) collective-permute-start(f32[32,5,1,8,128]{4,0,3,1,2:T(8,128)S(1)} %get-tuple-element.10), channel_id=1, source_target_pairs={{1,0},{2,1},{3,2},{4,3},{5,4},{6,5},{7,6},{8,7},{9,8},{10,9},{11,1... | collective-permute-start | bytes 1966088 | tf_op jit(solution)/shard_map/ppermute | solution.py:89
  10.2 2.2 %collective-permute-start = (f32[32,5,1,8,128]{4,0,3,1,2:T(8,128)S(1)}, f32[32,5,1,8,128]{4,0,3,1,2:T(8,128)S(1)}, u32[]{:S(2)}, u32[]{:S(2)}) collective-permute-start(f32[32,5,1,8,128]{4,0,3,1,2:T(8,128)S(1)} %get-tuple-element.9), channel_id=1, source_target_pairs={{0,1},{1,2},{2,3},{3,4},{4,5},{5,6},{6,7},{7,8},{8,9},{9,10},{10,1... | collective-permute-start | bytes 1966088 | tf_op jit(solution)/shard_map/ppermute | solution.py:88
  12.4 6.4 %fusion.22 = f32[32,252]{1,0:T(8,128)S(1)} fusion(bf16[252,5,2,8,128]{4,3,2,1,0:T(8,128)(2,1)} %param.8, f32[32,5,2,8,128]{4,0,3,1,2:T(8,128)S(1)} %convert_multiply_fusion, bf16[32,5,2,8,128]{4,3,2,1,0:T(8,128)(2,1)S(1)} %copy-done), kind=kOutput, calls=%fused_computation.35 | convolution fusion | flops 993853440 | bytes 7159296 | tf_op jit(solution)/shard_map/dot_general | solution.py:138
  19.8 4.3 %collective-permute-done.1 = f32[32,5,1,8,128]{4,0,3,1,2:T(8,128)S(1)} collective-permute-done((f32[32,5,1,8,128]{4,0,3,1,2:T(8,128)S(1)}, f32[32,5,1,8,128]{4,0,3,1,2:T(8,128)S(1)}, u32[]{:S(2)}, u32[]{:S(2)}) %collective-permute-start.1) | collective-permute-done | bytes 655392 | tf_op jit(solution)/shard_map/ppermute | solution.py:89
  24.1 2.3 %fusion.21 = f32[32,252]{1,0:T(8,128)S(1)} fusion(bf16[252,5,1,8,128]{4,3,2,1,0:T(8,128)(2,1)S(1)} %get-tuple-element.8, f32[32,5,1,8,128]{4,0,3,1,2:T(8,128)S(1)} %collective-permute-done.1), kind=kOutput, calls=%fused_computation.34 | convolution fusion | flops 495452160 | bytes 3268096 | tf_op jit(solution)/shard_map/dot_general | solution.py:138
  26.5 4.2 %collective-permute-done = f32[32,5,1,8,128]{4,0,3,1,2:T(8,128)S(1)} collective-permute-done((f32[32,5,1,8,128]{4,0,3,1,2:T(8,128)S(1)}, f32[32,5,1,8,128]{4,0,3,1,2:T(8,128)S(1)}, u32[]{:S(2)}, u32[]{:S(2)}) %collective-permute-start) | collective-permute-done | bytes 655392 | tf_op jit(solution)/shard_map/ppermute | solution.py:88
  30.6 2.3 %fusion.28 = f32[32,252]{1,0:T(8,128)S(1)} fusion(f32[32,252]{1,0:T(8,128)S(1)} %fusion.22, f32[32,252]{1,0:T(8,128)S(1)} %fusion.21, bf16[252,5,1,8,128]{4,3,2,1,0:T(8,128)(2,1)S(1)} %get-tuple-element.7, f32[32,5,1,8,128]{4,0,3,1,2:T(8,128)S(1)} %collective-permute-done), kind=kOutput, calls=%fused_computation.37 | convolution fusion | flops 495468288 | bytes 3332608 | tf_op jit(solution)/shard_map/dot_general | solution.py:138
  34.0 4.8 %collective-permute-done.2 = f32[32,224]{0,1:T(8,128)S(1)} collective-permute-done((f32[32,224]{0,1:T(8,128)S(1)}, f32[32,224]{0,1:T(8,128)S(1)}, u32[]{:S(2)}, u32[]{:S(2)}) %collective-permute-start.2) | collective-permute-done | bytes 28704 | tf_op jit(solution)/shard_map/ppermute | solution.py:110
  39.0 7.6 %collective-permute-done.3 = f32[32,224]{0,1:T(8,128)S(1)} collective-permute-done((f32[32,224]{0,1:T(8,128)S(1)}, f32[32,224]{0,1:T(8,128)S(1)}, u32[]{:S(2)}, u32[]{:S(2)}) %collective-permute-start.3) | collective-permute-done | bytes 28704 | tf_op jit(solution)/shard_map/ppermute | solution.py:110
  46.7 8.7 %collective-permute-done.4 = f32[32,224]{0,1:T(8,128)S(1)} collective-permute-done((f32[32,224]{0,1:T(8,128)S(1)}, f32[32,224]{0,1:T(8,128)S(1)}, u32[]{:S(2)}, u32[]{:S(2)}) %collective-permute-start.4) | collective-permute-done | bytes 28704 | tf_op jit(solution)/shard_map/ppermute | solution.py:110
  55.5 4.8 %collective-permute-done.5 = f32[32,224]{0,1:T(8,128)S(1)} collective-permute-done((f32[32,224]{0,1:T(8,128)S(1)}, f32[32,224]{0,1:T(8,128)S(1)}, u32[]{:S(2)}, u32[]{:S(2)}) %collective-permute-start.5) | collective-permute-done | bytes 28704 | tf_op jit(solution)/shard_map/ppermute | solution.py:110
  61.0 5.6 %collective-permute-done.6 = f32[32,224]{0,1:T(8,128)S(1)} collective-permute-done((f32[32,224]{0,1:T(8,128)S(1)}, f32[32,224]{0,1:T(8,128)S(1)}, u32[]{:S(2)}, u32[]{:S(2)}) %collective-permute-start.6) | collective-permute-done | bytes 28704 | tf_op jit(solution)/shard_map/ppermute | solution.py:110
  68.3 1.6 collective-permute-start.8
  69.9 2.8 %collective-permute-done.8 = f32[32,448]{1,0:T(8,128)S(1)} collective-permute-done((f32[32,448]{1,0:T(8,128)S(1)}, f32[32,448]{1,0:T(8,128)S(1)}, u32[]{:S(2)}, u32[]{:S(2)}) %collective-permute-start.8) | collective-permute-done | bytes 57376 | tf_op jit(solution)/shard_map/ppermute | solution.py:122
  72.8 3.3 %collective-permute-start.9 = (f32[32,896]{1,0:T(8,128)S(1)}, f32[32,896]{1,0:T(8,128)S(1)}, u32[]{:S(2)}, u32[]{:S(2)}) collective-permute-start(f32[32,896]{1,0:T(8,128)S(1)} %maximum_select_fusion.1), channel_id=1, source_target_pairs={{0,128},{32,160},{64,192},{96,224},{128,0},{160,32},{192,64},{224,... | collective-permute-start | bytes 344072 | tf_op jit(solution)/shard_map/ppermute | solution.py:122
  76.8 2.5 %collective-permute-done.9 = f32[32,896]{1,0:T(8,128)S(1)} collective-permute-done((f32[32,896]{1,0:T(8,128)S(1)}, f32[32,896]{1,0:T(8,128)S(1)}, u32[]{:S(2)}, u32[]{:S(2)}) %collective-permute-start.9) | collective-permute-done | bytes 114720 | tf_op jit(solution)/shard_map/ppermute | solution.py:122
  79.3 4.3 %gather_fusion.1 = f32[528,1792]{1,0:T(8,128)} fusion(f32[32,1792]{1,0:T(8,128)S(1)} %maximum_select_fusion, s32[1024]{0:T(1024)S(1)} %pad_clamp_fusion.1), kind=kCustom, calls=%fused_computation.clone | custom fusion | bytes 7571520 | tf_op jit(solution)/shard_map/jit(_take)/gather | solution.py:132
  83.7 4.3 %gather_fusion.2 = f32[528,1792]{1,0:T(8,128)} fusion(f32[32,1792]{1,0:T(8,128)S(1)} %maximum_select_fusion, s32[1024]{0:T(1024)S(1)} %pad_clamp_fusion), kind=kCustom, calls=%fused_computation.1.clone | custom fusion | bytes 7571520 | tf_op jit(solution)/shard_map/jit(_take)/gather | solution.py:132
  87.9 3.7 %mul.21 = f32[528,1792]{1,0:T(8,128)S(1)} multiply(f32[528,1792]{1,0:T(8,128)} %gather_fusion.1, f32[528,1792]{1,0:T(8,128)} %gather_fusion.2) | non-fusion elementwise | flops 946176 | bytes 11354112 | tf_op jit(solution)/shard_map/mul | solution.py:132
  91.6 10.3 %fusion.10 = f32[561,561]{1,0:T(8,128)S(1)} fusion(f32[528,1792]{1,0:T(8,128)S(1)} %mul.21, f32[32,1792]{1,0:T(8,128)S(1)} %maximum_select_fusion, f32[561]{0:T(1024)S(1)} %pad.10.clone), kind=kOutput, calls=%fused_computation.25 | convolution fusion | flops 6770085888 | bytes 5275208 | tf_op jit(solution)/shard_map/dot_general | solution.py:162
  102.0 1.4 select_add_fusion.a_ref
  103.3 70.8 %shard_map.77 = f32[640,640]{1,0:T(8,128)} custom-call(f32[640,640]{1,0:T(8,128)} %select_add_fusion.a_ref), custom_call_target="tpu_custom_call" | custom-call | tf_op jit(solution)/shard_map/pallas_call | solution.py:75
  174.1 2.6 %slice.53 = f32[561,561]{1,0:T(8,128)} slice(f32[640,640]{1,0:T(8,128)} %shard_map.77), slice={[0:561], [0:561]} | slice | bytes 2517768 | tf_op jit(solution)/shard_map/slice | solution.py:80
  (43 shorter events, 5.6 us)
Async XLA Ops:
  1.9 10.4 %copy-start = (bf16[32,5,2,8,128]{4,3,2,1,0:T(8,128)(2,1)S(1)}, bf16[32,5,2,8,128]{4,3,2,1,0:T(8,128)(2,1)}, u32[]{:S(2)}) copy-start(bf16[32,5,2,8,128]{4,3,2,1,0:T(8,128)(2,1)} %param.10) | copy-start | bytes 1966084
  2.1 22.1 %collective-permute-start.1 = (f32[32,5,1,8,128]{4,0,3,1,2:T(8,128)S(1)}, f32[32,5,1,8,128]{4,0,3,1,2:T(8,128)S(1)}, u32[]{:S(2)}, u32[]{:S(2)}) collective-permute-start(f32[32,5,1,8,128]{4,0,3,1,2:T(8,128)S(1)} %get-tuple-element.10), channel_id=1, source_target_pairs={{1,0},{2,1},{3,2},{4,3},{5,4},{6,5},{7,6},{8,7},{9,8},{10,9},{11,1... | collective-permute-start | bytes 1966088 | tf_op jit(solution)/shard_map/ppermute | solution.py:89
  10.1 8.7 %slice-start = ((s8[5160960]{0:T(1024)(128)(4,1)}), s8[4194304]{0:T(1024)(128)(4,1)S(1)}, s32[]{:S(2)}) async-start(s8[5160960]{0:T(1024)(128)(4,1)} %bitcast.42), calls=%async_computation | async-start | bytes 8388608
  10.2 8.6 %copy-start.3 = (s32[224]{0:T(256)S(1)}, s32[224]{0:T(256)}, u32[]{:S(2)}) copy-start(s32[224]{0:T(256)} %param.9) | copy-start | bytes 2692
  10.2 8.7 %slice-start.1 = ((s8[5160960]{0:T(1024)(128)(4,1)}), s8[966656]{0:T(1024)(128)(4,1)S(1)}, s32[]{:S(2)}) async-start(s8[5160960]{0:T(1024)(128)(4,1)} %bitcast.42), calls=%async_computation.1 | async-start | bytes 1933312
  10.2 20.5 %collective-permute-start = (f32[32,5,1,8,128]{4,0,3,1,2:T(8,128)S(1)}, f32[32,5,1,8,128]{4,0,3,1,2:T(8,128)S(1)}, u32[]{:S(2)}, u32[]{:S(2)}) collective-permute-start(f32[32,5,1,8,128]{4,0,3,1,2:T(8,128)S(1)} %get-tuple-element.9), channel_id=1, source_target_pairs={{0,1},{1,2},{2,3},{3,4},{4,5},{5,6},{6,7},{7,8},{8,9},{9,10},{10,1... | collective-permute-start | bytes 1966088 | tf_op jit(solution)/shard_map/ppermute | solution.py:88
  33.0 43.1 %copy-start.2 = (s32[528]{0:T(1024)S(1)}, s32[528]{0:T(1024)}, u32[]{:S(2)}) copy-start(s32[528]{0:T(1024)} %constant.127) | copy-start | bytes 6340
  33.0 43.1 %copy-start.1 = (s32[528]{0:T(1024)S(1)}, s32[528]{0:T(1024)}, u32[]{:S(2)}) copy-start(s32[528]{0:T(1024)} %constant.128) | copy-start | bytes 6340
  33.9 4.9 %collective-permute-start.2 = (f32[32,224]{0,1:T(8,128)S(1)}, f32[32,224]{0,1:T(8,128)S(1)}, u32[]{:S(2)}, u32[]{:S(2)}) collective-permute-start(f32[32,224]{0,1:T(8,128)S(1)} %select_bitcast_fusion), channel_id=1, source_target_pairs={{0,1},{1,0},{2,3},{3,2},{4,5},{5,4},{6,7},{7,6},{8,9},{9,8},{10,11... | collective-permute-start | bytes 86024 | tf_op jit(solution)/shard_map/ppermute | solution.py:110
  38.9 7.7 %collective-permute-start.3 = (f32[32,224]{0,1:T(8,128)S(1)}, f32[32,224]{0,1:T(8,128)S(1)}, u32[]{:S(2)}, u32[]{:S(2)}) collective-permute-start(f32[32,224]{0,1:T(8,128)S(1)} %fusion.35), channel_id=1, source_target_pairs={{0,2},{1,3},{2,0},{3,1},{4,6},{5,7},{6,4},{7,5},{8,10},{9,11},{10,... | collective-permute-start | bytes 86024 | tf_op jit(solution)/shard_map/ppermute | solution.py:110
  46.6 8.8 %collective-permute-start.4 = (f32[32,224]{0,1:T(8,128)S(1)}, f32[32,224]{0,1:T(8,128)S(1)}, u32[]{:S(2)}, u32[]{:S(2)}) collective-permute-start(f32[32,224]{0,1:T(8,128)S(1)} %add.84), channel_id=1, source_target_pairs={{0,4},{1,5},{2,6},{3,7},{4,0},{5,1},{6,2},{7,3},{8,12},{9,13},{10,... | collective-permute-start | bytes 86024 | tf_op jit(solution)/shard_map/ppermute | solution.py:110
  55.4 4.9 %collective-permute-start.5 = (f32[32,224]{0,1:T(8,128)S(1)}, f32[32,224]{0,1:T(8,128)S(1)}, u32[]{:S(2)}, u32[]{:S(2)}) collective-permute-start(f32[32,224]{0,1:T(8,128)S(1)} %add.85), channel_id=1, source_target_pairs={{0,8},{1,9},{2,10},{3,11},{4,12},{5,13},{6,14},{7,15},{8,0},{9,1},... | collective-permute-start | bytes 86024 | tf_op jit(solution)/shard_map/ppermute | solution.py:110
  60.3 6.4 %collective-permute-start.6 = (f32[32,224]{0,1:T(8,128)S(1)}, f32[32,224]{0,1:T(8,128)S(1)}, u32[]{:S(2)}, u32[]{:S(2)}) collective-permute-start(f32[32,224]{0,1:T(8,128)S(1)} %add.86), channel_id=1, source_target_pairs={{0,16},{1,17},{2,18},{3,19},{4,20},{5,21},{6,22},{7,23},{8,24},{9,... | collective-permute-start | bytes 86024 | tf_op jit(solution)/shard_map/ppermute | solution.py:110
  66.7 1.4 collective-permute-start.7
  68.3 4.4 %collective-permute-start.8 = (f32[32,448]{1,0:T(8,128)S(1)}, f32[32,448]{1,0:T(8,128)S(1)}, u32[]{:S(2)}, u32[]{:S(2)}) collective-permute-start(f32[32,448]{1,0:T(8,128)S(1)} %maximum_select_fusion.2), channel_id=1, source_target_pairs={{0,64},{32,96},{64,0},{96,32},{128,192},{160,224},{192,128},{224,1... | collective-permute-start | bytes 172040 | tf_op jit(solution)/shard_map/ppermute | solution.py:122
  72.8 6.6 %collective-permute-start.9 = (f32[32,896]{1,0:T(8,128)S(1)}, f32[32,896]{1,0:T(8,128)S(1)}, u32[]{:S(2)}, u32[]{:S(2)}) collective-permute-start(f32[32,896]{1,0:T(8,128)S(1)} %maximum_select_fusion.1), channel_id=1, source_target_pairs={{0,128},{32,160},{64,192},{96,224},{128,0},{160,32},{192,64},{224,... | collective-permute-start | bytes 344072 | tf_op jit(solution)/shard_map/ppermute | solution.py:122

commit v4 on v3

--- a/solution.py
+++ b/solution.py
@@ -45,14 +45,14 @@
 
         def step(j, carry):
             row = blk_ref[pl.ds(j, 1), :]
-            pivot = jnp.sum(jnp.where(row_lanes == j, row, 0.0), axis=1, keepdims=True)
+            pivot = jnp.sum(jnp.where(row_lanes[:, :PANEL] == j, row[:, :PANEL], 0.0), axis=1, keepdims=True)
             scale = lax.rsqrt(pivot)
             scaled = row * scale
             block = blk_ref[...]
             column = jnp.sum(jnp.where(lanes[:, :PANEL] == j, block[:, :PANEL], 0.0), axis=1, keepdims=True)
             coef = jnp.where(col_rows > j, column * scale, 0.0)
-            updated = block - coef * scaled
-            blk_ref[...] = jnp.where(rows == j, scaled, updated)
+            blk_ref[...] = block - coef * scaled
+            blk_ref[pl.ds(j, 1), :] = scaled
             return carry
 
         lax.fori_loop(0, steps, step, 0)

time: 177 us -> 174 us (0.983)
  Pallas kernels: 70.8 us -> 67.8 us
    pallas_call x1, Pallas kernels: 70.8 us -> 67.8 us  [cholesky_upper(): pl.pallas_call(functools.partial(chol_kernel, size=size, valid=n), out_sh...]
where the time goes in v4:
time: 174 us
  Pallas kernels  67.8 us (39%)
  waiting for transfers between devices  46.5 us (27%)
  matrix products  21.4 us (12%)
  starting transfers between devices  16.3 us (9%)
  local copies, waits for them, and re-layouts  13.8 us (8%)
  other arithmetic  6.84 us (4%)
    pallas_call x1, Pallas kernels, cholesky_upper(): pl.pallas_call(functools.partial(chol_kernel, size=size, valid=n), out_sh...  67.8 us
    ppermute x5, waiting for transfers between devices, butterfly_sum(): x = x + lax.ppermute(x, axis, [(i, i ^ step) for i in range(count)])  31.5 us
    dot_general x3, matrix products, project(): lax.dot_general(left, right, (((1,), (1,)), ((), ())), precision=lax.Prec...  11.1 us
    dot_general x1, matrix products, body(): lax.dot_general(features_t, features_t, (((1,), (1,)), ((), ())), precisi...  10.3 us
    ppermute x1, starting transfers between devices, neighbour_planes(): high = lax.ppermute(lax.slice_in_dim(block, 0, 1, axis=dim), axis, backward)  8.08 us
    ppermute x3, waiting for transfers between devices, butterfly_gather(): other = lax.ppermute(x, axis, [(i, i ^ step) for i in range(count)])  6.48 us
    ppermute x3, starting transfers between devices, butterfly_gather(): other = lax.ppermute(x, axis, [(i, i ^ step) for i in range(count)])  4.96 us
    ppermute x1, waiting for transfers between devices, neighbour_planes(): high = lax.ppermute(lax.slice_in_dim(block, 0, 1, axis=dim), axis, backward)  4.34 us
  transfers between devices with their start and end apart: 10, of which 10 were waited for; matrix products, arithmetic and copies ran while one was open for 6% of the time, Pallas kernels for 0%

profile of v4, /device:TPU:24, one launch (start us, length us, event | category | flops | bytes accessed | tf_op | source)
XLA Modules:
  0.0 173.7 jit_solution(1822147729514093732)
XLA Ops:
  0.6 1.3 convert_multiply_fusion
  2.1 8.1 %collective-permute-start.1 = (f32[32,5,1,8,128]{4,0,3,1,2:T(8,128)S(1)}, f32[32,5,1,8,128]{4,0,3,1,2:T(8,128)S(1)}, u32[]{:S(2)}, u32[]{:S(2)}) collective-permute-start(f32[32,5,1,8,128]{4,0,3,1,2:T(8,128)S(1)} %get-tuple-element.10), channel_id=1, source_target_pairs={{1,0},{2,1},{3,2},{4,3},{5,4},{6,5},{7,6},{8,7},{9,8},{10,9},{11,1... | collective-permute-start | bytes 1966088 | tf_op jit(solution)/shard_map/ppermute | solution.py:89
  10.2 2.2 %collective-permute-start = (f32[32,5,1,8,128]{4,0,3,1,2:T(8,128)S(1)}, f32[32,5,1,8,128]{4,0,3,1,2:T(8,128)S(1)}, u32[]{:S(2)}, u32[]{:S(2)}) collective-permute-start(f32[32,5,1,8,128]{4,0,3,1,2:T(8,128)S(1)} %get-tuple-element.9), channel_id=1, source_target_pairs={{0,1},{1,2},{2,3},{3,4},{4,5},{5,6},{6,7},{7,8},{8,9},{9,10},{10,1... | collective-permute-start | bytes 1966088 | tf_op jit(solution)/shard_map/ppermute | solution.py:88
  12.4 6.4 %fusion.22 = f32[32,252]{1,0:T(8,128)S(1)} fusion(bf16[252,5,2,8,128]{4,3,2,1,0:T(8,128)(2,1)} %param.8, f32[32,5,2,8,128]{4,0,3,1,2:T(8,128)S(1)} %convert_multiply_fusion, bf16[32,5,2,8,128]{4,3,2,1,0:T(8,128)(2,1)S(1)} %copy-done), kind=kOutput, calls=%fused_computation.35 | convolution fusion | flops 993853440 | bytes 7159296 | tf_op jit(solution)/shard_map/dot_general | solution.py:138
  19.8 4.3 %collective-permute-done.1 = f32[32,5,1,8,128]{4,0,3,1,2:T(8,128)S(1)} collective-permute-done((f32[32,5,1,8,128]{4,0,3,1,2:T(8,128)S(1)}, f32[32,5,1,8,128]{4,0,3,1,2:T(8,128)S(1)}, u32[]{:S(2)}, u32[]{:S(2)}) %collective-permute-start.1) | collective-permute-done | bytes 655392 | tf_op jit(solution)/shard_map/ppermute | solution.py:89
  24.1 2.3 %fusion.21 = f32[32,252]{1,0:T(8,128)S(1)} fusion(bf16[252,5,1,8,128]{4,3,2,1,0:T(8,128)(2,1)S(1)} %get-tuple-element.8, f32[32,5,1,8,128]{4,0,3,1,2:T(8,128)S(1)} %collective-permute-done.1), kind=kOutput, calls=%fused_computation.34 | convolution fusion | flops 495452160 | bytes 3268096 | tf_op jit(solution)/shard_map/dot_general | solution.py:138
  26.5 4.2 %collective-permute-done = f32[32,5,1,8,128]{4,0,3,1,2:T(8,128)S(1)} collective-permute-done((f32[32,5,1,8,128]{4,0,3,1,2:T(8,128)S(1)}, f32[32,5,1,8,128]{4,0,3,1,2:T(8,128)S(1)}, u32[]{:S(2)}, u32[]{:S(2)}) %collective-permute-start) | collective-permute-done | bytes 655392 | tf_op jit(solution)/shard_map/ppermute | solution.py:88
  30.6 2.3 %fusion.28 = f32[32,252]{1,0:T(8,128)S(1)} fusion(f32[32,252]{1,0:T(8,128)S(1)} %fusion.22, f32[32,252]{1,0:T(8,128)S(1)} %fusion.21, bf16[252,5,1,8,128]{4,3,2,1,0:T(8,128)(2,1)S(1)} %get-tuple-element.7, f32[32,5,1,8,128]{4,0,3,1,2:T(8,128)S(1)} %collective-permute-done), kind=kOutput, calls=%fused_computation.37 | convolution fusion | flops 495468288 | bytes 3332608 | tf_op jit(solution)/shard_map/dot_general | solution.py:138
  34.0 4.8 %collective-permute-done.2 = f32[32,224]{0,1:T(8,128)S(1)} collective-permute-done((f32[32,224]{0,1:T(8,128)S(1)}, f32[32,224]{0,1:T(8,128)S(1)}, u32[]{:S(2)}, u32[]{:S(2)}) %collective-permute-start.2) | collective-permute-done | bytes 28704 | tf_op jit(solution)/shard_map/ppermute | solution.py:110
  39.0 7.6 %collective-permute-done.3 = f32[32,224]{0,1:T(8,128)S(1)} collective-permute-done((f32[32,224]{0,1:T(8,128)S(1)}, f32[32,224]{0,1:T(8,128)S(1)}, u32[]{:S(2)}, u32[]{:S(2)}) %collective-permute-start.3) | collective-permute-done | bytes 28704 | tf_op jit(solution)/shard_map/ppermute | solution.py:110
  46.7 8.7 %collective-permute-done.4 = f32[32,224]{0,1:T(8,128)S(1)} collective-permute-done((f32[32,224]{0,1:T(8,128)S(1)}, f32[32,224]{0,1:T(8,128)S(1)}, u32[]{:S(2)}, u32[]{:S(2)}) %collective-permute-start.4) | collective-permute-done | bytes 28704 | tf_op jit(solution)/shard_map/ppermute | solution.py:110
  55.5 4.8 %collective-permute-done.5 = f32[32,224]{0,1:T(8,128)S(1)} collective-permute-done((f32[32,224]{0,1:T(8,128)S(1)}, f32[32,224]{0,1:T(8,128)S(1)}, u32[]{:S(2)}, u32[]{:S(2)}) %collective-permute-start.5) | collective-permute-done | bytes 28704 | tf_op jit(solution)/shard_map/ppermute | solution.py:110
  61.0 5.6 %collective-permute-done.6 = f32[32,224]{0,1:T(8,128)S(1)} collective-permute-done((f32[32,224]{0,1:T(8,128)S(1)}, f32[32,224]{0,1:T(8,128)S(1)}, u32[]{:S(2)}, u32[]{:S(2)}) %collective-permute-start.6) | collective-permute-done | bytes 28704 | tf_op jit(solution)/shard_map/ppermute | solution.py:110
  68.3 1.6 collective-permute-start.8
  69.9 2.8 %collective-permute-done.8 = f32[32,448]{1,0:T(8,128)S(1)} collective-permute-done((f32[32,448]{1,0:T(8,128)S(1)}, f32[32,448]{1,0:T(8,128)S(1)}, u32[]{:S(2)}, u32[]{:S(2)}) %collective-permute-start.8) | collective-permute-done | bytes 57376 | tf_op jit(solution)/shard_map/ppermute | solution.py:122
  72.8 3.3 %collective-permute-start.9 = (f32[32,896]{1,0:T(8,128)S(1)}, f32[32,896]{1,0:T(8,128)S(1)}, u32[]{:S(2)}, u32[]{:S(2)}) collective-permute-start(f32[32,896]{1,0:T(8,128)S(1)} %maximum_select_fusion.1), channel_id=1, source_target_pairs={{0,128},{32,160},{64,192},{96,224},{128,0},{160,32},{192,64},{224,... | collective-permute-start | bytes 344072 | tf_op jit(solution)/shard_map/ppermute | solution.py:122
  76.8 2.5 %collective-permute-done.9 = f32[32,896]{1,0:T(8,128)S(1)} collective-permute-done((f32[32,896]{1,0:T(8,128)S(1)}, f32[32,896]{1,0:T(8,128)S(1)}, u32[]{:S(2)}, u32[]{:S(2)}) %collective-permute-start.9) | collective-permute-done | bytes 114720 | tf_op jit(solution)/shard_map/ppermute | solution.py:122
  79.3 4.3 %gather_fusion.1 = f32[528,1792]{1,0:T(8,128)} fusion(f32[32,1792]{1,0:T(8,128)S(1)} %maximum_select_fusion, s32[1024]{0:T(1024)S(1)} %pad_clamp_fusion.1), kind=kCustom, calls=%fused_computation.clone | custom fusion | bytes 7571520 | tf_op jit(solution)/shard_map/jit(_take)/gather | solution.py:132
  83.7 4.3 %gather_fusion.2 = f32[528,1792]{1,0:T(8,128)} fusion(f32[32,1792]{1,0:T(8,128)S(1)} %maximum_select_fusion, s32[1024]{0:T(1024)S(1)} %pad_clamp_fusion), kind=kCustom, calls=%fused_computation.1.clone | custom fusion | bytes 7571520 | tf_op jit(solution)/shard_map/jit(_take)/gather | solution.py:132
  87.9 3.7 %mul.21 = f32[528,1792]{1,0:T(8,128)S(1)} multiply(f32[528,1792]{1,0:T(8,128)} %gather_fusion.1, f32[528,1792]{1,0:T(8,128)} %gather_fusion.2) | non-fusion elementwise | flops 946176 | bytes 11354112 | tf_op jit(solution)/shard_map/mul | solution.py:132
  91.6 10.3 %fusion.10 = f32[561,561]{1,0:T(8,128)S(1)} fusion(f32[528,1792]{1,0:T(8,128)S(1)} %mul.21, f32[32,1792]{1,0:T(8,128)S(1)} %maximum_select_fusion, f32[561]{0:T(1024)S(1)} %pad.10.clone), kind=kOutput, calls=%fused_computation.25 | convolution fusion | flops 6770085888 | bytes 5275208 | tf_op jit(solution)/shard_map/dot_general | solution.py:162
  102.0 1.4 select_add_fusion.a_ref
  103.3 67.8 %shard_map.77 = f32[640,640]{1,0:T(8,128)} custom-call(f32[640,640]{1,0:T(8,128)} %select_add_fusion.a_ref), custom_call_target="tpu_custom_call" | custom-call | tf_op jit(solution)/shard_map/pallas_call | solution.py:75
  171.2 2.6 %slice.53 = f32[561,561]{1,0:T(8,128)} slice(f32[640,640]{1,0:T(8,128)} %shard_map.77), slice={[0:561], [0:561]} | slice | bytes 2517768 | tf_op jit(solution)/shard_map/slice | solution.py:80
  (43 shorter events, 5.6 us)
Async XLA Ops:
  1.9 10.4 %copy-start = (bf16[32,5,2,8,128]{4,3,2,1,0:T(8,128)(2,1)S(1)}, bf16[32,5,2,8,128]{4,3,2,1,0:T(8,128)(2,1)}, u32[]{:S(2)}) copy-start(bf16[32,5,2,8,128]{4,3,2,1,0:T(8,128)(2,1)} %param.10) | copy-start | bytes 1966084
  2.1 22.1 %collective-permute-start.1 = (f32[32,5,1,8,128]{4,0,3,1,2:T(8,128)S(1)}, f32[32,5,1,8,128]{4,0,3,1,2:T(8,128)S(1)}, u32[]{:S(2)}, u32[]{:S(2)}) collective-permute-start(f32[32,5,1,8,128]{4,0,3,1,2:T(8,128)S(1)} %get-tuple-element.10), channel_id=1, source_target_pairs={{1,0},{2,1},{3,2},{4,3},{5,4},{6,5},{7,6},{8,7},{9,8},{10,9},{11,1... | collective-permute-start | bytes 1966088 | tf_op jit(solution)/shard_map/ppermute | solution.py:89
  10.1 8.7 %slice-start = ((s8[5160960]{0:T(1024)(128)(4,1)}), s8[4194304]{0:T(1024)(128)(4,1)S(1)}, s32[]{:S(2)}) async-start(s8[5160960]{0:T(1024)(128)(4,1)} %bitcast.42), calls=%async_computation | async-start | bytes 8388608
  10.2 8.6 %copy-start.3 = (s32[224]{0:T(256)S(1)}, s32[224]{0:T(256)}, u32[]{:S(2)}) copy-start(s32[224]{0:T(256)} %param.9) | copy-start | bytes 2692
  10.2 8.7 %slice-start.1 = ((s8[5160960]{0:T(1024)(128)(4,1)}), s8[966656]{0:T(1024)(128)(4,1)S(1)}, s32[]{:S(2)}) async-start(s8[5160960]{0:T(1024)(128)(4,1)} %bitcast.42), calls=%async_computation.1 | async-start | bytes 1933312
  10.2 20.5 %collective-permute-start = (f32[32,5,1,8,128]{4,0,3,1,2:T(8,128)S(1)}, f32[32,5,1,8,128]{4,0,3,1,2:T(8,128)S(1)}, u32[]{:S(2)}, u32[]{:S(2)}) collective-permute-start(f32[32,5,1,8,128]{4,0,3,1,2:T(8,128)S(1)} %get-tuple-element.9), channel_id=1, source_target_pairs={{0,1},{1,2},{2,3},{3,4},{4,5},{5,6},{6,7},{7,8},{8,9},{9,10},{10,1... | collective-permute-start | bytes 1966088 | tf_op jit(solution)/shard_map/ppermute | solution.py:88
  33.0 43.1 %copy-start.2 = (s32[528]{0:T(1024)S(1)}, s32[528]{0:T(1024)}, u32[]{:S(2)}) copy-start(s32[528]{0:T(1024)} %constant.127) | copy-start | bytes 6340
  33.0 43.1 %copy-start.1 = (s32[528]{0:T(1024)S(1)}, s32[528]{0:T(1024)}, u32[]{:S(2)}) copy-start(s32[528]{0:T(1024)} %constant.128) | copy-start | bytes 6340
  33.9 4.9 %collective-permute-start.2 = (f32[32,224]{0,1:T(8,128)S(1)}, f32[32,224]{0,1:T(8,128)S(1)}, u32[]{:S(2)}, u32[]{:S(2)}) collective-permute-start(f32[32,224]{0,1:T(8,128)S(1)} %select_bitcast_fusion), channel_id=1, source_target_pairs={{0,1},{1,0},{2,3},{3,2},{4,5},{5,4},{6,7},{7,6},{8,9},{9,8},{10,11... | collective-permute-start | bytes 86024 | tf_op jit(solution)/shard_map/ppermute | solution.py:110
  38.9 7.7 %collective-permute-start.3 = (f32[32,224]{0,1:T(8,128)S(1)}, f32[32,224]{0,1:T(8,128)S(1)}, u32[]{:S(2)}, u32[]{:S(2)}) collective-permute-start(f32[32,224]{0,1:T(8,128)S(1)} %fusion.35), channel_id=1, source_target_pairs={{0,2},{1,3},{2,0},{3,1},{4,6},{5,7},{6,4},{7,5},{8,10},{9,11},{10,... | collective-permute-start | bytes 86024 | tf_op jit(solution)/shard_map/ppermute | solution.py:110
  46.6 8.8 %collective-permute-start.4 = (f32[32,224]{0,1:T(8,128)S(1)}, f32[32,224]{0,1:T(8,128)S(1)}, u32[]{:S(2)}, u32[]{:S(2)}) collective-permute-start(f32[32,224]{0,1:T(8,128)S(1)} %add.84), channel_id=1, source_target_pairs={{0,4},{1,5},{2,6},{3,7},{4,0},{5,1},{6,2},{7,3},{8,12},{9,13},{10,... | collective-permute-start | bytes 86024 | tf_op jit(solution)/shard_map/ppermute | solution.py:110
  55.4 4.9 %collective-permute-start.5 = (f32[32,224]{0,1:T(8,128)S(1)}, f32[32,224]{0,1:T(8,128)S(1)}, u32[]{:S(2)}, u32[]{:S(2)}) collective-permute-start(f32[32,224]{0,1:T(8,128)S(1)} %add.85), channel_id=1, source_target_pairs={{0,8},{1,9},{2,10},{3,11},{4,12},{5,13},{6,14},{7,15},{8,0},{9,1},... | collective-permute-start | bytes 86024 | tf_op jit(solution)/shard_map/ppermute | solution.py:110
  60.3 6.4 %collective-permute-start.6 = (f32[32,224]{0,1:T(8,128)S(1)}, f32[32,224]{0,1:T(8,128)S(1)}, u32[]{:S(2)}, u32[]{:S(2)}) collective-permute-start(f32[32,224]{0,1:T(8,128)S(1)} %add.86), channel_id=1, source_target_pairs={{0,16},{1,17},{2,18},{3,19},{4,20},{5,21},{6,22},{7,23},{8,24},{9,... | collective-permute-start | bytes 86024 | tf_op jit(solution)/shard_map/ppermute | solution.py:110
  66.7 1.4 collective-permute-start.7
  68.3 4.4 %collective-permute-start.8 = (f32[32,448]{1,0:T(8,128)S(1)}, f32[32,448]{1,0:T(8,128)S(1)}, u32[]{:S(2)}, u32[]{:S(2)}) collective-permute-start(f32[32,448]{1,0:T(8,128)S(1)} %maximum_select_fusion.2), channel_id=1, source_target_pairs={{0,64},{32,96},{64,0},{96,32},{128,192},{160,224},{192,128},{224,1... | collective-permute-start | bytes 172040 | tf_op jit(solution)/shard_map/ppermute | solution.py:122
  72.8 6.6 %collective-permute-start.9 = (f32[32,896]{1,0:T(8,128)S(1)}, f32[32,896]{1,0:T(8,128)S(1)}, u32[]{:S(2)}, u32[]{:S(2)}) collective-permute-start(f32[32,896]{1,0:T(8,128)S(1)} %maximum_select_fusion.1), channel_id=1, source_target_pairs={{0,128},{32,160},{64,192},{96,224},{128,0},{160,32},{192,64},{224,... | collective-permute-start | bytes 344072 | tf_op jit(solution)/shard_map/ppermute | solution.py:122

commit v5 on v4

--- a/solution.py
+++ b/solution.py
@@ -43,19 +43,25 @@
         blk_ref[:, :PANEL] = w_ref[c0:c1, c0:c1]
         blk_ref[:, PANEL:] = eye
 
-        def step(j, carry):
-            row = blk_ref[pl.ds(j, 1), :]
-            pivot = jnp.sum(jnp.where(row_lanes[:, :PANEL] == j, row[:, :PANEL], 0.0), axis=1, keepdims=True)
-            scale = lax.rsqrt(pivot)
-            scaled = row * scale
-            block = blk_ref[...]
-            column = jnp.sum(jnp.where(lanes[:, :PANEL] == j, block[:, :PANEL], 0.0), axis=1, keepdims=True)
-            coef = jnp.where(col_rows > j, column * scale, 0.0)
-            blk_ref[...] = block - coef * scaled
-            blk_ref[pl.ds(j, 1), :] = scaled
-            return carry
+        for first in range(0, steps, 16):
+            top = (first // 8) * 8
+            height = PANEL - top
+            seg_rows = lax.broadcasted_iota(jnp.int32, (height, 1), 0) + top
+            seg_lanes = lax.broadcasted_iota(jnp.int32, (height, PANEL), 1)
 
-        lax.fori_loop(0, steps, step, 0)
+            def step(j, carry, top=top, seg_rows=seg_rows, seg_lanes=seg_lanes):
+                row = blk_ref[pl.ds(j, 1), :]
+                pivot = jnp.sum(jnp.where(row_lanes[:, :PANEL] == j, row[:, :PANEL], 0.0), axis=1, keepdims=True)
+                scale = lax.rsqrt(pivot)
+                scaled = row * scale
+                block = blk_ref[top:, :]
+                column = jnp.sum(jnp.where(seg_lanes == j, block[:, :PANEL], 0.0), axis=1, keepdims=True)
+                coef = jnp.where(seg_rows > j, column * scale, 0.0)
+                blk_ref[top:, :] = block - coef * scaled
+                blk_ref[pl.ds(j, 1), :] = scaled
+                return carry
+
+            lax.fori_loop(first, min(first + 16, steps), step, 0)
         block = blk_ref[...]
         upper = jnp.where(lanes[:, :PANEL] >= rows[:, :PANEL], block[:, :PANEL], 0.0)
         r_ref[c0:c1, c0:c1] = upper

time: 174 us -> 170 us (0.977)
  Pallas kernels: 67.8 us -> 63.6 us
    pallas_call x1, Pallas kernels: 67.8 us -> 63.6 us  [cholesky_upper(): pl.pallas_call(functools.partial(chol_kernel, size=size, valid=n), out_sh...]
where the time goes in v5:
time: 170 us
  Pallas kernels  63.6 us (37%)
  waiting for transfers between devices  46.5 us (27%)
  matrix products  21.4 us (13%)
  starting transfers between devices  16.1 us (9%)
  local copies, waits for them, and re-layouts  14 us (8%)
  other arithmetic  6.84 us (4%)
    pallas_call x1, Pallas kernels, cholesky_upper(): pl.pallas_call(functools.partial(chol_kernel, size=size, valid=n), out_sh...  63.6 us
    ppermute x5, waiting for transfers between devices, butterfly_sum(): x = x + lax.ppermute(x, axis, [(i, i ^ step) for i in range(count)])  31.5 us
    dot_general x3, matrix products, project(): lax.dot_general(left, right, (((1,), (1,)), ((), ())), precision=lax.Prec...  11.1 us
    dot_general x1, matrix products, body(): lax.dot_general(features_t, features_t, (((1,), (1,)), ((), ())), precisi...  10.3 us
    ppermute x1, starting transfers between devices, neighbour_planes(): high = lax.ppermute(lax.slice_in_dim(block, 0, 1, axis=dim), axis, backward)  8.08 us
    ppermute x3, waiting for transfers between devices, butterfly_gather(): other = lax.ppermute(x, axis, [(i, i ^ step) for i in range(count)])  6.49 us
    ppermute x3, starting transfers between devices, butterfly_gather(): other = lax.ppermute(x, axis, [(i, i ^ step) for i in range(count)])  4.78 us
    gather x1, local copies, waits for them, and re-layouts, expand_rows(): jnp.take(coeffs_t, first, axis=0) * jnp.take(coeffs_t, second, axis=0)  4.49 us
  transfers between devices with their start and end apart: 10, of which 10 were waited for; matrix products, arithmetic and copies ran while one was open for 6% of the time, Pallas kernels for 0%

profile of v5, /device:TPU:24, one launch (start us, length us, event | category | flops | bytes accessed | tf_op | source)
XLA Modules:
  0.0 169.5 jit_solution(10211888458752845280)
XLA Ops:
  0.6 1.3 convert_multiply_fusion
  2.1 8.1 %collective-permute-start.1 = (f32[32,5,1,8,128]{4,0,3,1,2:T(8,128)S(1)}, f32[32,5,1,8,128]{4,0,3,1,2:T(8,128)S(1)}, u32[]{:S(2)}, u32[]{:S(2)}) collective-permute-start(f32[32,5,1,8,128]{4,0,3,1,2:T(8,128)S(1)} %get-tuple-element.10), channel_id=1, source_target_pairs={{1,0},{2,1},{3,2},{4,3},{5,4},{6,5},{7,6},{8,7},{9,8},{10,9},{11,1... | collective-permute-start | bytes 1966088 | tf_op jit(solution)/shard_map/ppermute | solution.py:95
  10.2 2.2 %collective-permute-start = (f32[32,5,1,8,128]{4,0,3,1,2:T(8,128)S(1)}, f32[32,5,1,8,128]{4,0,3,1,2:T(8,128)S(1)}, u32[]{:S(2)}, u32[]{:S(2)}) collective-permute-start(f32[32,5,1,8,128]{4,0,3,1,2:T(8,128)S(1)} %get-tuple-element.9), channel_id=1, source_target_pairs={{0,1},{1,2},{2,3},{3,4},{4,5},{5,6},{6,7},{7,8},{8,9},{9,10},{10,1... | collective-permute-start | bytes 1966088 | tf_op jit(solution)/shard_map/ppermute | solution.py:94
  12.4 6.4 %fusion.22 = f32[32,252]{1,0:T(8,128)S(1)} fusion(bf16[252,5,2,8,128]{4,3,2,1,0:T(8,128)(2,1)} %param.8, f32[32,5,2,8,128]{4,0,3,1,2:T(8,128)S(1)} %convert_multiply_fusion, bf16[32,5,2,8,128]{4,3,2,1,0:T(8,128)(2,1)S(1)} %copy-done), kind=kOutput, calls=%fused_computation.35 | convolution fusion | flops 993853440 | bytes 7159296 | tf_op jit(solution)/shard_map/dot_general | solution.py:144
  19.8 4.3 %collective-permute-done.1 = f32[32,5,1,8,128]{4,0,3,1,2:T(8,128)S(1)} collective-permute-done((f32[32,5,1,8,128]{4,0,3,1,2:T(8,128)S(1)}, f32[32,5,1,8,128]{4,0,3,1,2:T(8,128)S(1)}, u32[]{:S(2)}, u32[]{:S(2)}) %collective-permute-start.1) | collective-permute-done | bytes 655392 | tf_op jit(solution)/shard_map/ppermute | solution.py:95
  24.1 2.3 %fusion.21 = f32[32,252]{1,0:T(8,128)S(1)} fusion(bf16[252,5,1,8,128]{4,3,2,1,0:T(8,128)(2,1)S(1)} %get-tuple-element.8, f32[32,5,1,8,128]{4,0,3,1,2:T(8,128)S(1)} %collective-permute-done.1), kind=kOutput, calls=%fused_computation.34 | convolution fusion | flops 495452160 | bytes 3268096 | tf_op jit(solution)/shard_map/dot_general | solution.py:144
  26.5 4.2 %collective-permute-done = f32[32,5,1,8,128]{4,0,3,1,2:T(8,128)S(1)} collective-permute-done((f32[32,5,1,8,128]{4,0,3,1,2:T(8,128)S(1)}, f32[32,5,1,8,128]{4,0,3,1,2:T(8,128)S(1)}, u32[]{:S(2)}, u32[]{:S(2)}) %collective-permute-start) | collective-permute-done | bytes 655392 | tf_op jit(solution)/shard_map/ppermute | solution.py:94
  30.6 2.3 %fusion.28 = f32[32,252]{1,0:T(8,128)S(1)} fusion(f32[32,252]{1,0:T(8,128)S(1)} %fusion.22, f32[32,252]{1,0:T(8,128)S(1)} %fusion.21, bf16[252,5,1,8,128]{4,3,2,1,0:T(8,128)(2,1)S(1)} %get-tuple-element.7, f32[32,5,1,8,128]{4,0,3,1,2:T(8,128)S(1)} %collective-permute-done), kind=kOutput, calls=%fused_computation.37 | convolution fusion | flops 495468288 | bytes 3332608 | tf_op jit(solution)/shard_map/dot_general | solution.py:144
  34.0 4.8 %collective-permute-done.2 = f32[32,224]{0,1:T(8,128)S(1)} collective-permute-done((f32[32,224]{0,1:T(8,128)S(1)}, f32[32,224]{0,1:T(8,128)S(1)}, u32[]{:S(2)}, u32[]{:S(2)}) %collective-permute-start.2) | collective-permute-done | bytes 28704 | tf_op jit(solution)/shard_map/ppermute | solution.py:116
  39.0 7.6 %collective-permute-done.3 = f32[32,224]{0,1:T(8,128)S(1)} collective-permute-done((f32[32,224]{0,1:T(8,128)S(1)}, f32[32,224]{0,1:T(8,128)S(1)}, u32[]{:S(2)}, u32[]{:S(2)}) %collective-permute-start.3) | collective-permute-done | bytes 28704 | tf_op jit(solution)/shard_map/ppermute | solution.py:116
  46.7 8.7 %collective-permute-done.4 = f32[32,224]{0,1:T(8,128)S(1)} collective-permute-done((f32[32,224]{0,1:T(8,128)S(1)}, f32[32,224]{0,1:T(8,128)S(1)}, u32[]{:S(2)}, u32[]{:S(2)}) %collective-permute-start.4) | collective-permute-done | bytes 28704 | tf_op jit(solution)/shard_map/ppermute | solution.py:116
  55.5 4.8 %collective-permute-done.5 = f32[32,224]{0,1:T(8,128)S(1)} collective-permute-done((f32[32,224]{0,1:T(8,128)S(1)}, f32[32,224]{0,1:T(8,128)S(1)}, u32[]{:S(2)}, u32[]{:S(2)}) %collective-permute-start.5) | collective-permute-done | bytes 28704 | tf_op jit(solution)/shard_map/ppermute | solution.py:116
  61.1 5.6 %collective-permute-done.6 = f32[32,224]{0,1:T(8,128)S(1)} collective-permute-done((f32[32,224]{0,1:T(8,128)S(1)}, f32[32,224]{0,1:T(8,128)S(1)}, u32[]{:S(2)}, u32[]{:S(2)}) %collective-permute-start.6) | collective-permute-done | bytes 28704 | tf_op jit(solution)/shard_map/ppermute | solution.py:116
  68.3 1.6 collective-permute-start.8
  69.9 2.8 %collective-permute-done.8 = f32[32,448]{1,0:T(8,128)S(1)} collective-permute-done((f32[32,448]{1,0:T(8,128)S(1)}, f32[32,448]{1,0:T(8,128)S(1)}, u32[]{:S(2)}, u32[]{:S(2)}) %collective-permute-start.8) | collective-permute-done | bytes 57376 | tf_op jit(solution)/shard_map/ppermute | solution.py:128
  72.8 3.1 %collective-permute-start.9 = (f32[32,896]{1,0:T(8,128)S(1)}, f32[32,896]{1,0:T(8,128)S(1)}, u32[]{:S(2)}, u32[]{:S(2)}) collective-permute-start(f32[32,896]{1,0:T(8,128)S(1)} %maximum_select_fusion.1), channel_id=1, source_target_pairs={{0,128},{32,160},{64,192},{96,224},{128,0},{160,32},{192,64},{224,... | collective-permute-start | bytes 344072 | tf_op jit(solution)/shard_map/ppermute | solution.py:128
  76.6 2.5 %collective-permute-done.9 = f32[32,896]{1,0:T(8,128)S(1)} collective-permute-done((f32[32,896]{1,0:T(8,128)S(1)}, f32[32,896]{1,0:T(8,128)S(1)}, u32[]{:S(2)}, u32[]{:S(2)}) %collective-permute-start.9) | collective-permute-done | bytes 114720 | tf_op jit(solution)/shard_map/ppermute | solution.py:128
  79.2 4.5 %gather_fusion.1 = f32[528,1792]{1,0:T(8,128)} fusion(f32[32,1792]{1,0:T(8,128)S(1)} %maximum_select_fusion, s32[1024]{0:T(1024)S(1)} %pad_clamp_fusion.1), kind=kCustom, calls=%fused_computation.clone | custom fusion | bytes 7571520 | tf_op jit(solution)/shard_map/jit(_take)/gather | solution.py:138
  83.7 4.3 %gather_fusion.2 = f32[528,1792]{1,0:T(8,128)} fusion(f32[32,1792]{1,0:T(8,128)S(1)} %maximum_select_fusion, s32[1024]{0:T(1024)S(1)} %pad_clamp_fusion), kind=kCustom, calls=%fused_computation.1.clone | custom fusion | bytes 7571520 | tf_op jit(solution)/shard_map/jit(_take)/gather | solution.py:138
  87.9 3.7 %mul.21 = f32[528,1792]{1,0:T(8,128)S(1)} multiply(f32[528,1792]{1,0:T(8,128)} %gather_fusion.1, f32[528,1792]{1,0:T(8,128)} %gather_fusion.2) | non-fusion elementwise | flops 946176 | bytes 11354112 | tf_op jit(solution)/shard_map/mul | solution.py:138
  91.6 10.3 %fusion.10 = f32[561,561]{1,0:T(8,128)S(1)} fusion(f32[528,1792]{1,0:T(8,128)S(1)} %mul.21, f32[32,1792]{1,0:T(8,128)S(1)} %maximum_select_fusion, f32[561]{0:T(1024)S(1)} %pad.10.clone), kind=kOutput, calls=%fused_computation.25 | convolution fusion | flops 6770085888 | bytes 5275208 | tf_op jit(solution)/shard_map/dot_general | solution.py:168
  102.0 1.4 select_add_fusion.a_ref
  103.3 63.6 %shard_map.77 = f32[640,640]{1,0:T(8,128)} custom-call(f32[640,640]{1,0:T(8,128)} %select_add_fusion.a_ref), custom_call_target="tpu_custom_call" | custom-call | tf_op jit(solution)/shard_map/pallas_call | solution.py:81
  167.0 2.6 %slice.53 = f32[561,561]{1,0:T(8,128)} slice(f32[640,640]{1,0:T(8,128)} %shard_map.77), slice={[0:561], [0:561]} | slice | bytes 2517768 | tf_op jit(solution)/shard_map/slice | solution.py:86
  (43 shorter events, 5.6 us)
Async XLA Ops:
  1.9 10.4 %copy-start = (bf16[32,5,2,8,128]{4,3,2,1,0:T(8,128)(2,1)S(1)}, bf16[32,5,2,8,128]{4,3,2,1,0:T(8,128)(2,1)}, u32[]{:S(2)}) copy-start(bf16[32,5,2,8,128]{4,3,2,1,0:T(8,128)(2,1)} %param.10) | copy-start | bytes 1966084
  2.1 22.1 %collective-permute-start.1 = (f32[32,5,1,8,128]{4,0,3,1,2:T(8,128)S(1)}, f32[32,5,1,8,128]{4,0,3,1,2:T(8,128)S(1)}, u32[]{:S(2)}, u32[]{:S(2)}) collective-permute-start(f32[32,5,1,8,128]{4,0,3,1,2:T(8,128)S(1)} %get-tuple-element.10), channel_id=1, source_target_pairs={{1,0},{2,1},{3,2},{4,3},{5,4},{6,5},{7,6},{8,7},{9,8},{10,9},{11,1... | collective-permute-start | bytes 1966088 | tf_op jit(solution)/shard_map/ppermute | solution.py:95
  10.1 8.7 %slice-start = ((s8[5160960]{0:T(1024)(128)(4,1)}), s8[4194304]{0:T(1024)(128)(4,1)S(1)}, s32[]{:S(2)}) async-start(s8[5160960]{0:T(1024)(128)(4,1)} %bitcast.42), calls=%async_computation | async-start | bytes 8388608
  10.2 8.6 %copy-start.3 = (s32[224]{0:T(256)S(1)}, s32[224]{0:T(256)}, u32[]{:S(2)}) copy-start(s32[224]{0:T(256)} %param.9) | copy-start | bytes 2692
  10.2 8.7 %slice-start.1 = ((s8[5160960]{0:T(1024)(128)(4,1)}), s8[966656]{0:T(1024)(128)(4,1)S(1)}, s32[]{:S(2)}) async-start(s8[5160960]{0:T(1024)(128)(4,1)} %bitcast.42), calls=%async_computation.1 | async-start | bytes 1933312
  10.2 20.5 %collective-permute-start = (f32[32,5,1,8,128]{4,0,3,1,2:T(8,128)S(1)}, f32[32,5,1,8,128]{4,0,3,1,2:T(8,128)S(1)}, u32[]{:S(2)}, u32[]{:S(2)}) collective-permute-start(f32[32,5,1,8,128]{4,0,3,1,2:T(8,128)S(1)} %get-tuple-element.9), channel_id=1, source_target_pairs={{0,1},{1,2},{2,3},{3,4},{4,5},{5,6},{6,7},{7,8},{8,9},{9,10},{10,1... | collective-permute-start | bytes 1966088 | tf_op jit(solution)/shard_map/ppermute | solution.py:94
  33.0 42.9 %copy-start.2 = (s32[528]{0:T(1024)S(1)}, s32[528]{0:T(1024)}, u32[]{:S(2)}) copy-start(s32[528]{0:T(1024)} %constant.127) | copy-start | bytes 6340
  33.0 42.9 %copy-start.1 = (s32[528]{0:T(1024)S(1)}, s32[528]{0:T(1024)}, u32[]{:S(2)}) copy-start(s32[528]{0:T(1024)} %constant.128) | copy-start | bytes 6340
  33.9 4.9 %collective-permute-start.2 = (f32[32,224]{0,1:T(8,128)S(1)}, f32[32,224]{0,1:T(8,128)S(1)}, u32[]{:S(2)}, u32[]{:S(2)}) collective-permute-start(f32[32,224]{0,1:T(8,128)S(1)} %select_bitcast_fusion), channel_id=1, source_target_pairs={{0,1},{1,0},{2,3},{3,2},{4,5},{5,4},{6,7},{7,6},{8,9},{9,8},{10,11... | collective-permute-start | bytes 86024 | tf_op jit(solution)/shard_map/ppermute | solution.py:116
  38.9 7.7 %collective-permute-start.3 = (f32[32,224]{0,1:T(8,128)S(1)}, f32[32,224]{0,1:T(8,128)S(1)}, u32[]{:S(2)}, u32[]{:S(2)}) collective-permute-start(f32[32,224]{0,1:T(8,128)S(1)} %fusion.35), channel_id=1, source_target_pairs={{0,2},{1,3},{2,0},{3,1},{4,6},{5,7},{6,4},{7,5},{8,10},{9,11},{10,... | collective-permute-start | bytes 86024 | tf_op jit(solution)/shard_map/ppermute | solution.py:116
  46.6 8.8 %collective-permute-start.4 = (f32[32,224]{0,1:T(8,128)S(1)}, f32[32,224]{0,1:T(8,128)S(1)}, u32[]{:S(2)}, u32[]{:S(2)}) collective-permute-start(f32[32,224]{0,1:T(8,128)S(1)} %add.84), channel_id=1, source_target_pairs={{0,4},{1,5},{2,6},{3,7},{4,0},{5,1},{6,2},{7,3},{8,12},{9,13},{10,... | collective-permute-start | bytes 86024 | tf_op jit(solution)/shard_map/ppermute | solution.py:116
  55.4 4.9 %collective-permute-start.5 = (f32[32,224]{0,1:T(8,128)S(1)}, f32[32,224]{0,1:T(8,128)S(1)}, u32[]{:S(2)}, u32[]{:S(2)}) collective-permute-start(f32[32,224]{0,1:T(8,128)S(1)} %add.85), channel_id=1, source_target_pairs={{0,8},{1,9},{2,10},{3,11},{4,12},{5,13},{6,14},{7,15},{8,0},{9,1},... | collective-permute-start | bytes 86024 | tf_op jit(solution)/shard_map/ppermute | solution.py:116
  60.3 6.4 %collective-permute-start.6 = (f32[32,224]{0,1:T(8,128)S(1)}, f32[32,224]{0,1:T(8,128)S(1)}, u32[]{:S(2)}, u32[]{:S(2)}) collective-permute-start(f32[32,224]{0,1:T(8,128)S(1)} %add.86), channel_id=1, source_target_pairs={{0,16},{1,17},{2,18},{3,19},{4,20},{5,21},{6,22},{7,23},{8,24},{9,... | collective-permute-start | bytes 86024 | tf_op jit(solution)/shard_map/ppermute | solution.py:116
  66.7 1.4 collective-permute-start.7
  68.3 4.4 %collective-permute-start.8 = (f32[32,448]{1,0:T(8,128)S(1)}, f32[32,448]{1,0:T(8,128)S(1)}, u32[]{:S(2)}, u32[]{:S(2)}) collective-permute-start(f32[32,448]{1,0:T(8,128)S(1)} %maximum_select_fusion.2), channel_id=1, source_target_pairs={{0,64},{32,96},{64,0},{96,32},{128,192},{160,224},{192,128},{224,1... | collective-permute-start | bytes 172040 | tf_op jit(solution)/shard_map/ppermute | solution.py:128
  72.8 6.4 %collective-permute-start.9 = (f32[32,896]{1,0:T(8,128)S(1)}, f32[32,896]{1,0:T(8,128)S(1)}, u32[]{:S(2)}, u32[]{:S(2)}) collective-permute-start(f32[32,896]{1,0:T(8,128)S(1)} %maximum_select_fusion.1), channel_id=1, source_target_pairs={{0,128},{32,160},{64,192},{96,224},{128,0},{160,32},{192,64},{224,... | collective-permute-start | bytes 344072 | tf_op jit(solution)/shard_map/ppermute | solution.py:128

commit v6 on v4

--- a/solution.py
+++ b/solution.py
@@ -9,6 +9,7 @@
 from jax.sharding import PartitionSpec as P
 
 PANEL = 128
+UNROLLED = 2
 
 
 def split3(x):
@@ -34,28 +35,51 @@
     rows = lax.broadcasted_iota(jnp.int32, (PANEL, 2 * PANEL), 0)
     lanes = lax.broadcasted_iota(jnp.int32, (PANEL, 2 * PANEL), 1)
     eye = (rows[:, :PANEL] == lanes[:, :PANEL]).astype(jnp.float32)
+    group_rows = lax.broadcasted_iota(jnp.int32, (8, 1), 0)
     row_lanes = lax.broadcasted_iota(jnp.int32, (1, 2 * PANEL), 1)
-    col_rows = lax.broadcasted_iota(jnp.int32, (PANEL, 1), 0)
     for p in range(panels):
         c0 = p * PANEL
         c1 = c0 + PANEL
         steps = min(PANEL, valid - c0)
         blk_ref[:, :PANEL] = w_ref[c0:c1, c0:c1]
         blk_ref[:, PANEL:] = eye
-
-        def step(j, carry):
-            row = blk_ref[pl.ds(j, 1), :]
-            pivot = jnp.sum(jnp.where(row_lanes[:, :PANEL] == j, row[:, :PANEL], 0.0), axis=1, keepdims=True)
-            scale = lax.rsqrt(pivot)
-            scaled = row * scale
-            block = blk_ref[...]
-            column = jnp.sum(jnp.where(lanes[:, :PANEL] == j, block[:, :PANEL], 0.0), axis=1, keepdims=True)
-            coef = jnp.where(col_rows > j, column * scale, 0.0)
-            blk_ref[...] = block - coef * scaled
-            blk_ref[pl.ds(j, 1), :] = scaled
-            return carry
-
-        lax.fori_loop(0, steps, step, 0)
+        if p < UNROLLED:
+            groups = [blk_ref[8 * g : 8 * g + 8, :] for g in range(PANEL // 8)]
+            for j in range(steps):
+                own, at = divmod(j, 8)
+                row = groups[own][at : at + 1, :]
+                scale = lax.rsqrt(row[:, j : j + 1])
+                scaled = row * scale
+                for g in range(own, PANEL // 8):
+                    column = groups[g][:, j : j + 1]
+                    if g == own:
+                        coef = jnp.where(group_rows > at, column * scale, 0.0)
+                        updated = groups[g] - coef * scaled
+                        groups[g] = jnp.where(group_rows == at, scaled, updated)
+                    else:
+                        groups[g] = groups[g] - (column * scale) * scaled
+            for g in range(PANEL // 8):
+                blk_ref[8 * g : 8 * g + 8, :] = groups[g]
+        else:
+            for first in range(0, steps, 16):
+                top = (first // 8) * 8
+                height = PANEL - top
+                seg_rows = lax.broadcasted_iota(jnp.int32, (height, 1), 0) + top
+                seg_lanes = lax.broadcasted_iota(jnp.int32, (height, PANEL), 1)
+
+                def step(j, carry, top=top, seg_rows=seg_rows, seg_lanes=seg_lanes):
+                    row = blk_ref[pl.ds(j, 1), :]
+                    pivot = jnp.sum(jnp.where(row_lanes[:, :PANEL] == j, row[:, :PANEL], 0.0), axis=1, keepdims=True)
+                    scale = lax.rsqrt(pivot)
+                    scaled = row * scale
+                    block = blk_ref[top:, :]
+                    column = jnp.sum(jnp.where(seg_lanes == j, block[:, :PANEL], 0.0), axis=1, keepdims=True)
+                    coef = jnp.where(seg_rows > j, column * scale, 0.0)
+                    blk_ref[top:, :] = block - coef * scaled
+                    blk_ref[pl.ds(j, 1), :] = scaled
+                    return carry
+
+                lax.fori_loop(first, min(first + 16, steps), step, 0)
         block = blk_ref[...]
         upper = jnp.where(lanes[:, :PANEL] >= rows[:, :PANEL], block[:, :PANEL], 0.0)
         r_ref[c0:c1, c0:c1] = upper

time: 174 us -> 165 us (0.948)
  Pallas kernels: 67.8 us -> 59 us
    pallas_call x1, Pallas kernels: 67.8 us -> 59 us  [cholesky_upper(): pl.pallas_call(functools.partial(chol_kernel, size=size, valid=n), out_sh...]
where the time goes in v6:
time: 165 us
  Pallas kernels  59 us (36%)
  waiting for transfers between devices  46.5 us (28%)
  matrix products  21.4 us (13%)
  starting transfers between devices  16.2 us (10%)
  local copies, waits for them, and re-layouts  13.8 us (8%)
  other arithmetic  6.84 us (4%)
    pallas_call x1, Pallas kernels, cholesky_upper(): pl.pallas_call(functools.partial(chol_kernel, size=size, valid=n), out_sh...  59 us
    ppermute x5, waiting for transfers between devices, butterfly_sum(): x = x + lax.ppermute(x, axis, [(i, i ^ step) for i in range(count)])  31.5 us
    dot_general x3, matrix products, project(): lax.dot_general(left, right, (((1,), (1,)), ((), ())), precision=lax.Prec...  11.1 us
    dot_general x1, matrix products, body(): lax.dot_general(features_t, features_t, (((1,), (1,)), ((), ())), precisi...  10.3 us
    ppermute x1, starting transfers between devices, neighbour_planes(): high = lax.ppermute(lax.slice_in_dim(block, 0, 1, axis=dim), axis, backward)  8.08 us
    ppermute x3, waiting for transfers between devices, butterfly_gather(): other = lax.ppermute(x, axis, [(i, i ^ step) for i in range(count)])  6.48 us
    ppermute x3, starting transfers between devices, butterfly_gather(): other = lax.ppermute(x, axis, [(i, i ^ step) for i in range(count)])  4.78 us
    ppermute x1, waiting for transfers between devices, neighbour_planes(): high = lax.ppermute(lax.slice_in_dim(block, 0, 1, axis=dim), axis, backward)  4.34 us
  transfers between devices with their start and end apart: 10, of which 10 were waited for; matrix products, arithmetic and copies ran while one was open for 6% of the time, Pallas kernels for 0%

profile of v6, /device:TPU:24, one launch (start us, length us, event | category | flops | bytes accessed | tf_op | source)
XLA Modules:
  0.0 164.7 jit_solution(8679364049548205463)
XLA Ops:
  0.6 1.3 convert_multiply_fusion
  2.1 8.1 %collective-permute-start.1 = (f32[32,5,1,8,128]{4,0,3,1,2:T(8,128)S(1)}, f32[32,5,1,8,128]{4,0,3,1,2:T(8,128)S(1)}, u32[]{:S(2)}, u32[]{:S(2)}) collective-permute-start(f32[32,5,1,8,128]{4,0,3,1,2:T(8,128)S(1)} %get-tuple-element.10), channel_id=1, source_target_pairs={{1,0},{2,1},{3,2},{4,3},{5,4},{6,5},{7,6},{8,7},{9,8},{10,9},{11,1... | collective-permute-start | bytes 1966088 | tf_op jit(solution)/shard_map/ppermute | solution.py:113
  10.2 2.2 %collective-permute-start = (f32[32,5,1,8,128]{4,0,3,1,2:T(8,128)S(1)}, f32[32,5,1,8,128]{4,0,3,1,2:T(8,128)S(1)}, u32[]{:S(2)}, u32[]{:S(2)}) collective-permute-start(f32[32,5,1,8,128]{4,0,3,1,2:T(8,128)S(1)} %get-tuple-element.9), channel_id=1, source_target_pairs={{0,1},{1,2},{2,3},{3,4},{4,5},{5,6},{6,7},{7,8},{8,9},{9,10},{10,1... | collective-permute-start | bytes 1966088 | tf_op jit(solution)/shard_map/ppermute | solution.py:112
  12.4 6.4 %fusion.22 = f32[32,252]{1,0:T(8,128)S(1)} fusion(bf16[252,5,2,8,128]{4,3,2,1,0:T(8,128)(2,1)} %param.8, f32[32,5,2,8,128]{4,0,3,1,2:T(8,128)S(1)} %convert_multiply_fusion, bf16[32,5,2,8,128]{4,3,2,1,0:T(8,128)(2,1)S(1)} %copy-done), kind=kOutput, calls=%fused_computation.35 | convolution fusion | flops 993853440 | bytes 7159296 | tf_op jit(solution)/shard_map/dot_general | solution.py:162
  19.8 4.3 %collective-permute-done.1 = f32[32,5,1,8,128]{4,0,3,1,2:T(8,128)S(1)} collective-permute-done((f32[32,5,1,8,128]{4,0,3,1,2:T(8,128)S(1)}, f32[32,5,1,8,128]{4,0,3,1,2:T(8,128)S(1)}, u32[]{:S(2)}, u32[]{:S(2)}) %collective-permute-start.1) | collective-permute-done | bytes 655392 | tf_op jit(solution)/shard_map/ppermute | solution.py:113
  24.1 2.3 %fusion.21 = f32[32,252]{1,0:T(8,128)S(1)} fusion(bf16[252,5,1,8,128]{4,3,2,1,0:T(8,128)(2,1)S(1)} %get-tuple-element.8, f32[32,5,1,8,128]{4,0,3,1,2:T(8,128)S(1)} %collective-permute-done.1), kind=kOutput, calls=%fused_computation.34 | convolution fusion | flops 495452160 | bytes 3268096 | tf_op jit(solution)/shard_map/dot_general | solution.py:162
  26.5 4.2 %collective-permute-done = f32[32,5,1,8,128]{4,0,3,1,2:T(8,128)S(1)} collective-permute-done((f32[32,5,1,8,128]{4,0,3,1,2:T(8,128)S(1)}, f32[32,5,1,8,128]{4,0,3,1,2:T(8,128)S(1)}, u32[]{:S(2)}, u32[]{:S(2)}) %collective-permute-start) | collective-permute-done | bytes 655392 | tf_op jit(solution)/shard_map/ppermute | solution.py:112
  30.6 2.3 %fusion.28 = f32[32,252]{1,0:T(8,128)S(1)} fusion(f32[32,252]{1,0:T(8,128)S(1)} %fusion.22, f32[32,252]{1,0:T(8,128)S(1)} %fusion.21, bf16[252,5,1,8,128]{4,3,2,1,0:T(8,128)(2,1)S(1)} %get-tuple-element.7, f32[32,5,1,8,128]{4,0,3,1,2:T(8,128)S(1)} %collective-permute-done), kind=kOutput, calls=%fused_computation.37 | convolution fusion | flops 495468288 | bytes 3332608 | tf_op jit(solution)/shard_map/dot_general | solution.py:162
  34.0 4.8 %collective-permute-done.2 = f32[32,224]{0,1:T(8,128)S(1)} collective-permute-done((f32[32,224]{0,1:T(8,128)S(1)}, f32[32,224]{0,1:T(8,128)S(1)}, u32[]{:S(2)}, u32[]{:S(2)}) %collective-permute-start.2) | collective-permute-done | bytes 28704 | tf_op jit(solution)/shard_map/ppermute | solution.py:134
  39.0 7.6 %collective-permute-done.3 = f32[32,224]{0,1:T(8,128)S(1)} collective-permute-done((f32[32,224]{0,1:T(8,128)S(1)}, f32[32,224]{0,1:T(8,128)S(1)}, u32[]{:S(2)}, u32[]{:S(2)}) %collective-permute-start.3) | collective-permute-done | bytes 28704 | tf_op jit(solution)/shard_map/ppermute | solution.py:134
  46.7 8.7 %collective-permute-done.4 = f32[32,224]{0,1:T(8,128)S(1)} collective-permute-done((f32[32,224]{0,1:T(8,128)S(1)}, f32[32,224]{0,1:T(8,128)S(1)}, u32[]{:S(2)}, u32[]{:S(2)}) %collective-permute-start.4) | collective-permute-done | bytes 28704 | tf_op jit(solution)/shard_map/ppermute | solution.py:134
  55.5 4.8 %collective-permute-done.5 = f32[32,224]{0,1:T(8,128)S(1)} collective-permute-done((f32[32,224]{0,1:T(8,128)S(1)}, f32[32,224]{0,1:T(8,128)S(1)}, u32[]{:S(2)}, u32[]{:S(2)}) %collective-permute-start.5) | collective-permute-done | bytes 28704 | tf_op jit(solution)/shard_map/ppermute | solution.py:134
  61.0 5.6 %collective-permute-done.6 = f32[32,224]{0,1:T(8,128)S(1)} collective-permute-done((f32[32,224]{0,1:T(8,128)S(1)}, f32[32,224]{0,1:T(8,128)S(1)}, u32[]{:S(2)}, u32[]{:S(2)}) %collective-permute-start.6) | collective-permute-done | bytes 28704 | tf_op jit(solution)/shard_map/ppermute | solution.py:134
  68.3 1.6 collective-permute-start.8
  69.9 2.8 %collective-permute-done.8 = f32[32,448]{1,0:T(8,128)S(1)} collective-permute-done((f32[32,448]{1,0:T(8,128)S(1)}, f32[32,448]{1,0:T(8,128)S(1)}, u32[]{:S(2)}, u32[]{:S(2)}) %collective-permute-start.8) | collective-permute-done | bytes 57376 | tf_op jit(solution)/shard_map/ppermute | solution.py:146
  72.8 3.1 %collective-permute-start.9 = (f32[32,896]{1,0:T(8,128)S(1)}, f32[32,896]{1,0:T(8,128)S(1)}, u32[]{:S(2)}, u32[]{:S(2)}) collective-permute-start(f32[32,896]{1,0:T(8,128)S(1)} %maximum_select_fusion.1), channel_id=1, source_target_pairs={{0,128},{32,160},{64,192},{96,224},{128,0},{160,32},{192,64},{224,... | collective-permute-start | bytes 344072 | tf_op jit(solution)/shard_map/ppermute | solution.py:146
  76.6 2.5 %collective-permute-done.9 = f32[32,896]{1,0:T(8,128)S(1)} collective-permute-done((f32[32,896]{1,0:T(8,128)S(1)}, f32[32,896]{1,0:T(8,128)S(1)}, u32[]{:S(2)}, u32[]{:S(2)}) %collective-permute-start.9) | collective-permute-done | bytes 114720 | tf_op jit(solution)/shard_map/ppermute | solution.py:146
  79.2 4.3 %gather_fusion.1 = f32[528,1792]{1,0:T(8,128)} fusion(f32[32,1792]{1,0:T(8,128)S(1)} %maximum_select_fusion, s32[1024]{0:T(1024)S(1)} %pad_clamp_fusion.1), kind=kCustom, calls=%fused_computation.clone | custom fusion | bytes 7571520 | tf_op jit(solution)/shard_map/jit(_take)/gather | solution.py:156
  83.5 4.3 %gather_fusion.2 = f32[528,1792]{1,0:T(8,128)} fusion(f32[32,1792]{1,0:T(8,128)S(1)} %maximum_select_fusion, s32[1024]{0:T(1024)S(1)} %pad_clamp_fusion), kind=kCustom, calls=%fused_computation.1.clone | custom fusion | bytes 7571520 | tf_op jit(solution)/shard_map/jit(_take)/gather | solution.py:156
  87.8 3.7 %mul.21 = f32[528,1792]{1,0:T(8,128)S(1)} multiply(f32[528,1792]{1,0:T(8,128)} %gather_fusion.1, f32[528,1792]{1,0:T(8,128)} %gather_fusion.2) | non-fusion elementwise | flops 946176 | bytes 11354112 | tf_op jit(solution)/shard_map/mul | solution.py:156
  91.4 10.3 %fusion.10 = f32[561,561]{1,0:T(8,128)S(1)} fusion(f32[528,1792]{1,0:T(8,128)S(1)} %mul.21, f32[32,1792]{1,0:T(8,128)S(1)} %maximum_select_fusion, f32[561]{0:T(1024)S(1)} %pad.10.clone), kind=kOutput, calls=%fused_computation.25 | convolution fusion | flops 6770085888 | bytes 5275208 | tf_op jit(solution)/shard_map/dot_general | solution.py:186
  101.8 1.4 select_add_fusion.a_ref
  103.1 59.0 %shard_map.77 = f32[640,640]{1,0:T(8,128)} custom-call(f32[640,640]{1,0:T(8,128)} %select_add_fusion.a_ref), custom_call_target="tpu_custom_call" | custom-call | tf_op jit(solution)/shard_map/pallas_call | solution.py:99
  162.2 2.6 %slice.53 = f32[561,561]{1,0:T(8,128)} slice(f32[640,640]{1,0:T(8,128)} %shard_map.77), slice={[0:561], [0:561]} | slice | bytes 2517768 | tf_op jit(solution)/shard_map/slice | solution.py:104
  (43 shorter events, 5.6 us)
Async XLA Ops:
  1.9 10.4 %copy-start = (bf16[32,5,2,8,128]{4,3,2,1,0:T(8,128)(2,1)S(1)}, bf16[32,5,2,8,128]{4,3,2,1,0:T(8,128)(2,1)}, u32[]{:S(2)}) copy-start(bf16[32,5,2,8,128]{4,3,2,1,0:T(8,128)(2,1)} %param.10) | copy-start | bytes 1966084
  2.1 22.1 %collective-permute-start.1 = (f32[32,5,1,8,128]{4,0,3,1,2:T(8,128)S(1)}, f32[32,5,1,8,128]{4,0,3,1,2:T(8,128)S(1)}, u32[]{:S(2)}, u32[]{:S(2)}) collective-permute-start(f32[32,5,1,8,128]{4,0,3,1,2:T(8,128)S(1)} %get-tuple-element.10), channel_id=1, source_target_pairs={{1,0},{2,1},{3,2},{4,3},{5,4},{6,5},{7,6},{8,7},{9,8},{10,9},{11,1... | collective-permute-start | bytes 1966088 | tf_op jit(solution)/shard_map/ppermute | solution.py:113
  10.1 8.7 %slice-start = ((s8[5160960]{0:T(1024)(128)(4,1)}), s8[4194304]{0:T(1024)(128)(4,1)S(1)}, s32[]{:S(2)}) async-start(s8[5160960]{0:T(1024)(128)(4,1)} %bitcast.42), calls=%async_computation | async-start | bytes 8388608
  10.2 8.6 %copy-start.3 = (s32[224]{0:T(256)S(1)}, s32[224]{0:T(256)}, u32[]{:S(2)}) copy-start(s32[224]{0:T(256)} %param.9) | copy-start | bytes 2692
  10.2 8.7 %slice-start.1 = ((s8[5160960]{0:T(1024)(128)(4,1)}), s8[966656]{0:T(1024)(128)(4,1)S(1)}, s32[]{:S(2)}) async-start(s8[5160960]{0:T(1024)(128)(4,1)} %bitcast.42), calls=%async_computation.1 | async-start | bytes 1933312
  10.2 20.5 %collective-permute-start = (f32[32,5,1,8,128]{4,0,3,1,2:T(8,128)S(1)}, f32[32,5,1,8,128]{4,0,3,1,2:T(8,128)S(1)}, u32[]{:S(2)}, u32[]{:S(2)}) collective-permute-start(f32[32,5,1,8,128]{4,0,3,1,2:T(8,128)S(1)} %get-tuple-element.9), channel_id=1, source_target_pairs={{0,1},{1,2},{2,3},{3,4},{4,5},{5,6},{6,7},{7,8},{8,9},{9,10},{10,1... | collective-permute-start | bytes 1966088 | tf_op jit(solution)/shard_map/ppermute | solution.py:112
  33.0 42.9 %copy-start.2 = (s32[528]{0:T(1024)S(1)}, s32[528]{0:T(1024)}, u32[]{:S(2)}) copy-start(s32[528]{0:T(1024)} %constant.127) | copy-start | bytes 6340
  33.0 42.9 %copy-start.1 = (s32[528]{0:T(1024)S(1)}, s32[528]{0:T(1024)}, u32[]{:S(2)}) copy-start(s32[528]{0:T(1024)} %constant.128) | copy-start | bytes 6340
  33.9 4.9 %collective-permute-start.2 = (f32[32,224]{0,1:T(8,128)S(1)}, f32[32,224]{0,1:T(8,128)S(1)}, u32[]{:S(2)}, u32[]{:S(2)}) collective-permute-start(f32[32,224]{0,1:T(8,128)S(1)} %select_bitcast_fusion), channel_id=1, source_target_pairs={{0,1},{1,0},{2,3},{3,2},{4,5},{5,4},{6,7},{7,6},{8,9},{9,8},{10,11... | collective-permute-start | bytes 86024 | tf_op jit(solution)/shard_map/ppermute | solution.py:134
  38.9 7.7 %collective-permute-start.3 = (f32[32,224]{0,1:T(8,128)S(1)}, f32[32,224]{0,1:T(8,128)S(1)}, u32[]{:S(2)}, u32[]{:S(2)}) collective-permute-start(f32[32,224]{0,1:T(8,128)S(1)} %fusion.35), channel_id=1, source_target_pairs={{0,2},{1,3},{2,0},{3,1},{4,6},{5,7},{6,4},{7,5},{8,10},{9,11},{10,... | collective-permute-start | bytes 86024 | tf_op jit(solution)/shard_map/ppermute | solution.py:134
  46.6 8.8 %collective-permute-start.4 = (f32[32,224]{0,1:T(8,128)S(1)}, f32[32,224]{0,1:T(8,128)S(1)}, u32[]{:S(2)}, u32[]{:S(2)}) collective-permute-start(f32[32,224]{0,1:T(8,128)S(1)} %add.84), channel_id=1, source_target_pairs={{0,4},{1,5},{2,6},{3,7},{4,0},{5,1},{6,2},{7,3},{8,12},{9,13},{10,... | collective-permute-start | bytes 86024 | tf_op jit(solution)/shard_map/ppermute | solution.py:134
  55.4 4.9 %collective-permute-start.5 = (f32[32,224]{0,1:T(8,128)S(1)}, f32[32,224]{0,1:T(8,128)S(1)}, u32[]{:S(2)}, u32[]{:S(2)}) collective-permute-start(f32[32,224]{0,1:T(8,128)S(1)} %add.85), channel_id=1, source_target_pairs={{0,8},{1,9},{2,10},{3,11},{4,12},{5,13},{6,14},{7,15},{8,0},{9,1},... | collective-permute-start | bytes 86024 | tf_op jit(solution)/shard_map/ppermute | solution.py:134
  60.3 6.4 %collective-permute-start.6 = (f32[32,224]{0,1:T(8,128)S(1)}, f32[32,224]{0,1:T(8,128)S(1)}, u32[]{:S(2)}, u32[]{:S(2)}) collective-permute-start(f32[32,224]{0,1:T(8,128)S(1)} %add.86), channel_id=1, source_target_pairs={{0,16},{1,17},{2,18},{3,19},{4,20},{5,21},{6,22},{7,23},{8,24},{9,... | collective-permute-start | bytes 86024 | tf_op jit(solution)/shard_map/ppermute | solution.py:134
  66.7 1.4 collective-permute-start.7
  68.3 4.4 %collective-permute-start.8 = (f32[32,448]{1,0:T(8,128)S(1)}, f32[32,448]{1,0:T(8,128)S(1)}, u32[]{:S(2)}, u32[]{:S(2)}) collective-permute-start(f32[32,448]{1,0:T(8,128)S(1)} %maximum_select_fusion.2), channel_id=1, source_target_pairs={{0,64},{32,96},{64,0},{96,32},{128,192},{160,224},{192,128},{224,1... | collective-permute-start | bytes 172040 | tf_op jit(solution)/shard_map/ppermute | solution.py:146
  72.8 6.4 %collective-permute-start.9 = (f32[32,896]{1,0:T(8,128)S(1)}, f32[32,896]{1,0:T(8,128)S(1)}, u32[]{:S(2)}, u32[]{:S(2)}) collective-permute-start(f32[32,896]{1,0:T(8,128)S(1)} %maximum_select_fusion.1), channel_id=1, source_target_pairs={{0,128},{32,160},{64,192},{96,224},{128,0},{160,32},{192,64},{224,... | collective-permute-start | bytes 344072 | tf_op jit(solution)/shard_map/ppermute | solution.py:146

commit v7 on v6

--- a/solution.py
+++ b/solution.py
@@ -30,8 +30,11 @@
 
 def chol_kernel(a_ref, r_ref, w_ref, blk_ref, *, size, valid):
     panels = size // PANEL
-    r_ref[...] = jnp.zeros((size, size), jnp.float32)
-    w_ref[...] = a_ref[...]
+    r_ref[...] = jnp.zeros((valid, valid), jnp.float32)
+    fill_rows = lax.broadcasted_iota(jnp.int32, (size, size), 0)
+    fill_cols = lax.broadcasted_iota(jnp.int32, (size, size), 1)
+    w_ref[...] = jnp.where((fill_rows == fill_cols) & (fill_rows >= valid), 1.0, 0.0).astype(jnp.float32)
+    w_ref[0:valid, 0:valid] = a_ref[...]
     rows = lax.broadcasted_iota(jnp.int32, (PANEL, 2 * PANEL), 0)
     lanes = lax.broadcasted_iota(jnp.int32, (PANEL, 2 * PANEL), 1)
     eye = (rows[:, :PANEL] == lanes[:, :PANEL]).astype(jnp.float32)
@@ -82,26 +85,23 @@
                 lax.fori_loop(first, min(first + 16, steps), step, 0)
         block = blk_ref[...]
         upper = jnp.where(lanes[:, :PANEL] >= rows[:, :PANEL], block[:, :PANEL], 0.0)
-        r_ref[c0:c1, c0:c1] = upper
+        end = min(c1, valid)
+        r_ref[c0:end, c0:end] = upper[: end - c0, : end - c0]
         if p + 1 < panels:
             inv_t = block[:, PANEL:]
             right = dot3(inv_t, w_ref[c0:c1, c1:size])
-            r_ref[c0:c1, c1:size] = right
+            r_ref[c0:c1, c1:valid] = right[:, : valid - c1]
             w_ref[c1:size, c1:size] = w_ref[c1:size, c1:size] - dot3(right.T, right)
 
 
 def cholesky_upper(gram):
     n = gram.shape[0]
     size = -(-n // PANEL) * PANEL
-    padded = jnp.pad(gram, ((0, size - n), (0, size - n)))
-    fill = (jnp.arange(size) >= n).astype(jnp.float32)
-    padded = padded + jnp.diag(fill)
-    out = pl.pallas_call(
+    return pl.pallas_call(
         functools.partial(chol_kernel, size=size, valid=n),
-        out_shape=jax.ShapeDtypeStruct((size, size), jnp.float32),
+        out_shape=jax.ShapeDtypeStruct((n, n), jnp.float32),
         scratch_shapes=[pltpu.VMEM((size, size), jnp.float32), pltpu.VMEM((PANEL, 2 * PANEL), jnp.float32)],
-    )(padded)
-    return out[:n, :n]
+    )(gram)
 
 
 def neighbour_planes(block, axis, dim):

time: 165 us -> 162 us (0.982)
  local copies, waits for them, and re-layouts: 13.8 us -> 11.2 us
    slice x1 -> x0, local copies, waits for them, and re-layouts: 2.56 us -> none  [cholesky_upper(): return out[:n, :n]]
where the time goes in v7:
time: 162 us
  Pallas kernels  58.9 us (36%)
  waiting for transfers between devices  46.5 us (29%)
  matrix products  22.6 us (14%)
  starting transfers between devices  16 us (10%)
  local copies, waits for them, and re-layouts  11.2 us (7%)
  other arithmetic  5.54 us (3%)
    pallas_call x1, Pallas kernels, cholesky_upper(): pl.pallas_call(functools.partial(chol_kernel, size=size, valid=n), out_sh...  58.9 us
    ppermute x5, waiting for transfers between devices, butterfly_sum(): x = x + lax.ppermute(x, axis, [(i, i ^ step) for i in range(count)])  31.5 us
    dot_general x1, matrix products, body(): lax.dot_general(features_t, features_t, (((1,), (1,)), ((), ())), precisi...  11.5 us
    dot_general x3, matrix products, project(): lax.dot_general(left, right, (((1,), (1,)), ((), ())), precision=lax.Prec...  11.1 us
    ppermute x1, starting transfers between devices, neighbour_planes(): high = lax.ppermute(lax.slice_in_dim(block, 0, 1, axis=dim), axis, backward)  7.94 us
    ppermute x3, waiting for transfers between devices, butterfly_gather(): other = lax.ppermute(x, axis, [(i, i ^ step) for i in range(count)])  6.51 us
    ppermute x3, starting transfers between devices, butterfly_gather(): other = lax.ppermute(x, axis, [(i, i ^ step) for i in range(count)])  4.78 us
    ppermute x1, waiting for transfers between devices, neighbour_planes(): high = lax.ppermute(lax.slice_in_dim(block, 0, 1, axis=dim), axis, backward)  4.34 us
  transfers between devices with their start and end apart: 10, of which 10 were waited for; matrix products, arithmetic and copies ran while one was open for 6% of the time, Pallas kernels for 0%

profile of v7, /device:TPU:24, one launch (start us, length us, event | category | flops | bytes accessed | tf_op | source)
XLA Modules:
  0.0 161.8 jit_solution(15148362576626491123)
XLA Ops:
  0.6 1.4 convert_multiply_fusion
  2.1 7.9 %collective-permute-start.1 = (f32[32,5,1,8,128]{4,0,3,1,2:T(8,128)S(1)}, f32[32,5,1,8,128]{4,0,3,1,2:T(8,128)S(1)}, u32[]{:S(2)}, u32[]{:S(2)}) collective-permute-start(f32[32,5,1,8,128]{4,0,3,1,2:T(8,128)S(1)} %get-tuple-element.10), channel_id=1, source_target_pairs={{1,0},{2,1},{3,2},{4,3},{5,4},{6,5},{7,6},{8,7},{9,8},{10,9},{11,1... | collective-permute-start | bytes 1966088 | tf_op jit(solution)/shard_map/ppermute | solution.py:113
  10.1 2.2 %collective-permute-start = (f32[32,5,1,8,128]{4,0,3,1,2:T(8,128)S(1)}, f32[32,5,1,8,128]{4,0,3,1,2:T(8,128)S(1)}, u32[]{:S(2)}, u32[]{:S(2)}) collective-permute-start(f32[32,5,1,8,128]{4,0,3,1,2:T(8,128)S(1)} %get-tuple-element.9), channel_id=1, source_target_pairs={{0,1},{1,2},{2,3},{3,4},{4,5},{5,6},{6,7},{7,8},{8,9},{9,10},{10,1... | collective-permute-start | bytes 1966088 | tf_op jit(solution)/shard_map/ppermute | solution.py:112
  12.3 6.4 %fusion.22 = f32[32,252]{1,0:T(8,128)S(1)} fusion(bf16[252,5,2,8,128]{4,3,2,1,0:T(8,128)(2,1)} %param.8, f32[32,5,2,8,128]{4,0,3,1,2:T(8,128)S(1)} %convert_multiply_fusion, bf16[32,5,2,8,128]{4,3,2,1,0:T(8,128)(2,1)S(1)} %copy-done), kind=kOutput, calls=%fused_computation.33 | convolution fusion | flops 993853440 | bytes 7159296 | tf_op jit(solution)/shard_map/dot_general | solution.py:162
  18.8 0.9 fusion.32
  19.7 4.3 %collective-permute-done.1 = f32[32,5,1,8,128]{4,0,3,1,2:T(8,128)S(1)} collective-permute-done((f32[32,5,1,8,128]{4,0,3,1,2:T(8,128)S(1)}, f32[32,5,1,8,128]{4,0,3,1,2:T(8,128)S(1)}, u32[]{:S(2)}, u32[]{:S(2)}) %collective-permute-start.1) | collective-permute-done | bytes 655392 | tf_op jit(solution)/shard_map/ppermute | solution.py:113
  24.0 2.3 %fusion.21 = f32[32,252]{1,0:T(8,128)S(1)} fusion(bf16[252,5,1,8,128]{4,3,2,1,0:T(8,128)(2,1)S(1)} %get-tuple-element.8, f32[32,5,1,8,128]{4,0,3,1,2:T(8,128)S(1)} %collective-permute-done.1), kind=kOutput, calls=%fused_computation.32 | convolution fusion | flops 495452160 | bytes 3268096 | tf_op jit(solution)/shard_map/dot_general | solution.py:162
  26.4 4.2 %collective-permute-done = f32[32,5,1,8,128]{4,0,3,1,2:T(8,128)S(1)} collective-permute-done((f32[32,5,1,8,128]{4,0,3,1,2:T(8,128)S(1)}, f32[32,5,1,8,128]{4,0,3,1,2:T(8,128)S(1)}, u32[]{:S(2)}, u32[]{:S(2)}) %collective-permute-start) | collective-permute-done | bytes 655392 | tf_op jit(solution)/shard_map/ppermute | solution.py:112
  30.6 2.3 %fusion.28 = f32[32,252]{1,0:T(8,128)S(1)} fusion(f32[32,252]{1,0:T(8,128)S(1)} %fusion.22, f32[32,252]{1,0:T(8,128)S(1)} %fusion.21, bf16[252,5,1,8,128]{4,3,2,1,0:T(8,128)(2,1)S(1)} %get-tuple-element.7, f32[32,5,1,8,128]{4,0,3,1,2:T(8,128)S(1)} %collective-permute-done), kind=kOutput, calls=%fused_computation.35 | convolution fusion | flops 495468288 | bytes 3332608 | tf_op jit(solution)/shard_map/dot_general | solution.py:162
  33.9 4.8 %collective-permute-done.2 = f32[32,224]{0,1:T(8,128)S(1)} collective-permute-done((f32[32,224]{0,1:T(8,128)S(1)}, f32[32,224]{0,1:T(8,128)S(1)}, u32[]{:S(2)}, u32[]{:S(2)}) %collective-permute-start.2) | collective-permute-done | bytes 28704 | tf_op jit(solution)/shard_map/ppermute | solution.py:134
  38.9 7.6 %collective-permute-done.3 = f32[32,224]{0,1:T(8,128)S(1)} collective-permute-done((f32[32,224]{0,1:T(8,128)S(1)}, f32[32,224]{0,1:T(8,128)S(1)}, u32[]{:S(2)}, u32[]{:S(2)}) %collective-permute-start.3) | collective-permute-done | bytes 28704 | tf_op jit(solution)/shard_map/ppermute | solution.py:134
  46.6 8.7 %collective-permute-done.4 = f32[32,224]{0,1:T(8,128)S(1)} collective-permute-done((f32[32,224]{0,1:T(8,128)S(1)}, f32[32,224]{0,1:T(8,128)S(1)}, u32[]{:S(2)}, u32[]{:S(2)}) %collective-permute-start.4) | collective-permute-done | bytes 28704 | tf_op jit(solution)/shard_map/ppermute | solution.py:134
  55.4 4.8 %collective-permute-done.5 = f32[32,224]{0,1:T(8,128)S(1)} collective-permute-done((f32[32,224]{0,1:T(8,128)S(1)}, f32[32,224]{0,1:T(8,128)S(1)}, u32[]{:S(2)}, u32[]{:S(2)}) %collective-permute-start.5) | collective-permute-done | bytes 28704 | tf_op jit(solution)/shard_map/ppermute | solution.py:134
  60.9 5.7 %collective-permute-done.6 = f32[32,224]{0,1:T(8,128)S(1)} collective-permute-done((f32[32,224]{0,1:T(8,128)S(1)}, f32[32,224]{0,1:T(8,128)S(1)}, u32[]{:S(2)}, u32[]{:S(2)}) %collective-permute-start.6) | collective-permute-done | bytes 28704 | tf_op jit(solution)/shard_map/ppermute | solution.py:134
  66.8 1.2 collective-permute-done.7
  68.2 1.6 collective-permute-start.8
  69.8 2.8 %collective-permute-done.8 = f32[32,448]{1,0:T(8,128)S(1)} collective-permute-done((f32[32,448]{1,0:T(8,128)S(1)}, f32[32,448]{1,0:T(8,128)S(1)}, u32[]{:S(2)}, u32[]{:S(2)}) %collective-permute-start.8) | collective-permute-done | bytes 57376 | tf_op jit(solution)/shard_map/ppermute | solution.py:146
  72.7 3.1 %collective-permute-start.9 = (f32[32,896]{1,0:T(8,128)S(1)}, f32[32,896]{1,0:T(8,128)S(1)}, u32[]{:S(2)}, u32[]{:S(2)}) collective-permute-start(f32[32,896]{1,0:T(8,128)S(1)} %maximum_select_fusion.1), channel_id=1, source_target_pairs={{0,128},{32,160},{64,192},{96,224},{128,0},{160,32},{192,64},{224,... | collective-permute-start | bytes 344072 | tf_op jit(solution)/shard_map/ppermute | solution.py:146
  76.5 2.5 %collective-permute-done.9 = f32[32,896]{1,0:T(8,128)S(1)} collective-permute-done((f32[32,896]{1,0:T(8,128)S(1)}, f32[32,896]{1,0:T(8,128)S(1)}, u32[]{:S(2)}, u32[]{:S(2)}) %collective-permute-start.9) | collective-permute-done | bytes 114720 | tf_op jit(solution)/shard_map/ppermute | solution.py:146
  79.1 4.3 %gather_fusion.1 = f32[528,1792]{1,0:T(8,128)} fusion(f32[32,1792]{1,0:T(8,128)S(1)} %maximum_select_fusion, s32[1024]{0:T(1024)S(1)} %pad_clamp_fusion.1), kind=kCustom, calls=%fused_computation.clone | custom fusion | bytes 7571520 | tf_op jit(solution)/shard_map/jit(_take)/gather | solution.py:156
  83.4 4.3 %gather_fusion.2 = f32[528,1792]{1,0:T(8,128)} fusion(f32[32,1792]{1,0:T(8,128)S(1)} %maximum_select_fusion, s32[1024]{0:T(1024)S(1)} %pad_clamp_fusion), kind=kCustom, calls=%fused_computation.1.clone | custom fusion | bytes 7571520 | tf_op jit(solution)/shard_map/jit(_take)/gather | solution.py:156
  87.7 3.7 %mul.21 = f32[528,1792]{1,0:T(8,128)S(1)} multiply(f32[528,1792]{1,0:T(8,128)} %gather_fusion.1, f32[528,1792]{1,0:T(8,128)} %gather_fusion.2) | non-fusion elementwise | flops 946176 | bytes 11354112 | tf_op jit(solution)/shard_map/mul | solution.py:156
  91.3 11.5 %fusion.10.a_ref = f32[561,561]{1,0:T(8,128)} fusion(f32[528,1792]{1,0:T(8,128)S(1)} %mul.21, f32[32,1792]{1,0:T(8,128)S(1)} %maximum_select_fusion, f32[561]{0:T(1024)S(1)} %pad.5.clone), kind=kOutput, calls=%fused_computation.23 | convolution fusion | flops 6770085888 | bytes 5275208 | tf_op jit(solution)/shard_map/dot_general | solution.py:186
  102.8 58.9 %shard_map.77 = f32[561,561]{1,0:T(8,128)} custom-call(f32[561,561]{1,0:T(8,128)} %fusion.10.a_ref), custom_call_target="tpu_custom_call" | custom-call | tf_op jit(solution)/shard_map/pallas_call | solution.py:100
  (40 shorter events, 3.4 us)
Async XLA Ops:
  0.6 11.7 %copy-start = (bf16[32,5,2,8,128]{4,3,2,1,0:T(8,128)(2,1)S(1)}, bf16[32,5,2,8,128]{4,3,2,1,0:T(8,128)(2,1)}, u32[]{:S(2)}) copy-start(bf16[32,5,2,8,128]{4,3,2,1,0:T(8,128)(2,1)} %param.10) | copy-start | bytes 1966084
  2.1 21.9 %collective-permute-start.1 = (f32[32,5,1,8,128]{4,0,3,1,2:T(8,128)S(1)}, f32[32,5,1,8,128]{4,0,3,1,2:T(8,128)S(1)}, u32[]{:S(2)}, u32[]{:S(2)}) collective-permute-start(f32[32,5,1,8,128]{4,0,3,1,2:T(8,128)S(1)} %get-tuple-element.10), channel_id=1, source_target_pairs={{1,0},{2,1},{3,2},{4,3},{5,4},{6,5},{7,6},{8,7},{9,8},{10,9},{11,1... | collective-permute-start | bytes 1966088 | tf_op jit(solution)/shard_map/ppermute | solution.py:113
  10.1 8.7 %slice-start = ((s8[5160960]{0:T(1024)(128)(4,1)}), s8[4194304]{0:T(1024)(128)(4,1)S(1)}, s32[]{:S(2)}) async-start(s8[5160960]{0:T(1024)(128)(4,1)} %bitcast.42), calls=%async_computation | async-start | bytes 8388608
  10.1 8.6 %copy-start.3 = (s32[224]{0:T(256)S(1)}, s32[224]{0:T(256)}, u32[]{:S(2)}) copy-start(s32[224]{0:T(256)} %param.9) | copy-start | bytes 2692
  10.1 8.7 %slice-start.1 = ((s8[5160960]{0:T(1024)(128)(4,1)}), s8[966656]{0:T(1024)(128)(4,1)S(1)}, s32[]{:S(2)}) async-start(s8[5160960]{0:T(1024)(128)(4,1)} %bitcast.42), calls=%async_computation.1 | async-start | bytes 1933312
  10.1 20.5 %collective-permute-start = (f32[32,5,1,8,128]{4,0,3,1,2:T(8,128)S(1)}, f32[32,5,1,8,128]{4,0,3,1,2:T(8,128)S(1)}, u32[]{:S(2)}, u32[]{:S(2)}) collective-permute-start(f32[32,5,1,8,128]{4,0,3,1,2:T(8,128)S(1)} %get-tuple-element.9), channel_id=1, source_target_pairs={{0,1},{1,2},{2,3},{3,4},{4,5},{5,6},{6,7},{7,8},{8,9},{9,10},{10,1... | collective-permute-start | bytes 1966088 | tf_op jit(solution)/shard_map/ppermute | solution.py:112
  30.6 45.2 %copy-start.2 = (s32[528]{0:T(1024)S(1)}, s32[528]{0:T(1024)}, u32[]{:S(2)}) copy-start(s32[528]{0:T(1024)} %constant.121) | copy-start | bytes 6340
  30.6 45.3 %copy-start.1 = (s32[528]{0:T(1024)S(1)}, s32[528]{0:T(1024)}, u32[]{:S(2)}) copy-start(s32[528]{0:T(1024)} %constant.122) | copy-start | bytes 6340
  33.8 4.9 %collective-permute-start.2 = (f32[32,224]{0,1:T(8,128)S(1)}, f32[32,224]{0,1:T(8,128)S(1)}, u32[]{:S(2)}, u32[]{:S(2)}) collective-permute-start(f32[32,224]{0,1:T(8,128)S(1)} %select_bitcast_fusion), channel_id=1, source_target_pairs={{0,1},{1,0},{2,3},{3,2},{4,5},{5,4},{6,7},{7,6},{8,9},{9,8},{10,11... | collective-permute-start | bytes 86024 | tf_op jit(solution)/shard_map/ppermute | solution.py:134
  38.8 7.7 %collective-permute-start.3 = (f32[32,224]{0,1:T(8,128)S(1)}, f32[32,224]{0,1:T(8,128)S(1)}, u32[]{:S(2)}, u32[]{:S(2)}) collective-permute-start(f32[32,224]{0,1:T(8,128)S(1)} %fusion.34), channel_id=1, source_target_pairs={{0,2},{1,3},{2,0},{3,1},{4,6},{5,7},{6,4},{7,5},{8,10},{9,11},{10,... | collective-permute-start | bytes 86024 | tf_op jit(solution)/shard_map/ppermute | solution.py:134
  46.5 8.8 %collective-permute-start.4 = (f32[32,224]{0,1:T(8,128)S(1)}, f32[32,224]{0,1:T(8,128)S(1)}, u32[]{:S(2)}, u32[]{:S(2)}) collective-permute-start(f32[32,224]{0,1:T(8,128)S(1)} %add.79), channel_id=1, source_target_pairs={{0,4},{1,5},{2,6},{3,7},{4,0},{5,1},{6,2},{7,3},{8,12},{9,13},{10,... | collective-permute-start | bytes 86024 | tf_op jit(solution)/shard_map/ppermute | solution.py:134
  55.3 4.9 %collective-permute-start.5 = (f32[32,224]{0,1:T(8,128)S(1)}, f32[32,224]{0,1:T(8,128)S(1)}, u32[]{:S(2)}, u32[]{:S(2)}) collective-permute-start(f32[32,224]{0,1:T(8,128)S(1)} %add.80), channel_id=1, source_target_pairs={{0,8},{1,9},{2,10},{3,11},{4,12},{5,13},{6,14},{7,15},{8,0},{9,1},... | collective-permute-start | bytes 86024 | tf_op jit(solution)/shard_map/ppermute | solution.py:134
  60.2 6.4 %collective-permute-start.6 = (f32[32,224]{0,1:T(8,128)S(1)}, f32[32,224]{0,1:T(8,128)S(1)}, u32[]{:S(2)}, u32[]{:S(2)}) collective-permute-start(f32[32,224]{0,1:T(8,128)S(1)} %add.81), channel_id=1, source_target_pairs={{0,16},{1,17},{2,18},{3,19},{4,20},{5,21},{6,22},{7,23},{8,24},{9,... | collective-permute-start | bytes 86024 | tf_op jit(solution)/shard_map/ppermute | solution.py:134
  66.6 1.4 collective-permute-start.7
  68.2 4.4 %collective-permute-start.8 = (f32[32,448]{1,0:T(8,128)S(1)}, f32[32,448]{1,0:T(8,128)S(1)}, u32[]{:S(2)}, u32[]{:S(2)}) collective-permute-start(f32[32,448]{1,0:T(8,128)S(1)} %maximum_select_fusion.2), channel_id=1, source_target_pairs={{0,64},{32,96},{64,0},{96,32},{128,192},{160,224},{192,128},{224,1... | collective-permute-start | bytes 172040 | tf_op jit(solution)/shard_map/ppermute | solution.py:146
  72.7 6.4 %collective-permute-start.9 = (f32[32,896]{1,0:T(8,128)S(1)}, f32[32,896]{1,0:T(8,128)S(1)}, u32[]{:S(2)}, u32[]{:S(2)}) collective-permute-start(f32[32,896]{1,0:T(8,128)S(1)} %maximum_select_fusion.1), channel_id=1, source_target_pairs={{0,128},{32,160},{64,192},{96,224},{128,0},{160,32},{192,64},{224,... | collective-permute-start | bytes 344072 | tf_op jit(solution)/shard_map/ppermute | solution.py:146

commit v8 on v7

--- a/solution.py
+++ b/solution.py
@@ -153,7 +153,8 @@
 def expand_rows(coeffs_t):
     count = coeffs_t.shape[0]
     first, second = np.triu_indices(count)
-    quad = jnp.take(coeffs_t, first, axis=0) * jnp.take(coeffs_t, second, axis=0)
+    outer = (coeffs_t[:, None, :] * coeffs_t[None, :, :]).reshape(count * count, coeffs_t.shape[1])
+    quad = jnp.take(outer, first * count + second, axis=0)
     ones = jnp.ones((1, coeffs_t.shape[1]), coeffs_t.dtype)
     return jnp.concatenate([ones, coeffs_t, quad], axis=0)
 

time: 162 us -> 166 us (1.025)
  matrix products: 22.6 us -> 26.5 us
    dot_general x1, matrix products: 11.5 us -> 15.4 us  [body(): lax.dot_general(features_t, features_t, (((1,), (1,)), ((), ())), precisi...]
    gather x2 -> x1, local copies, waits for them, and re-layouts: 8.6 us -> 8.99 us  [expand_rows(): quad = jnp.take(outer, first * count + second, axis=0)]
where the time goes in v8:
time: 166 us
  Pallas kernels  58.7 us (35%)
  waiting for transfers between devices  46.6 us (28%)
  matrix products  26.5 us (16%)
  starting transfers between devices  16.2 us (10%)
  local copies, waits for them, and re-layouts  11.7 us (7%)
  other arithmetic  5.64 us (3%)
    pallas_call x1, Pallas kernels, cholesky_upper(): pl.pallas_call(functools.partial(chol_kernel, size=size, valid=n), out_sh...  58.7 us
    ppermute x5, waiting for transfers between devices, butterfly_sum(): x = x + lax.ppermute(x, axis, [(i, i ^ step) for i in range(count)])  31.5 us
    dot_general x1, matrix products, body(): lax.dot_general(features_t, features_t, (((1,), (1,)), ((), ())), precisi...  15.4 us
    dot_general x3, matrix products, project(): lax.dot_general(left, right, (((1,), (1,)), ((), ())), precision=lax.Prec...  11.1 us
    gather x1, local copies, waits for them, and re-layouts, expand_rows(): quad = jnp.take(outer, first * count + second, axis=0)  8.99 us
    ppermute x1, starting transfers between devices, neighbour_planes(): high = lax.ppermute(lax.slice_in_dim(block, 0, 1, axis=dim), axis, backward)  7.94 us
    ppermute x3, waiting for transfers between devices, butterfly_gather(): other = lax.ppermute(x, axis, [(i, i ^ step) for i in range(count)])  6.58 us
    ppermute x3, starting transfers between devices, butterfly_gather(): other = lax.ppermute(x, axis, [(i, i ^ step) for i in range(count)])  4.96 us
  transfers between devices with their start and end apart: 10, of which 10 were waited for; matrix products, arithmetic and copies ran while one was open for 6% of the time, Pallas kernels for 0%

profile of v8, /device:TPU:24, one launch (start us, length us, event | category | flops | bytes accessed | tf_op | source)
XLA Modules:
  0.0 166.2 jit_solution(553951502273404439)
XLA Ops:
  0.6 1.4 convert_multiply_fusion
  2.2 7.9 %collective-permute-start.1 = (f32[32,5,1,8,128]{4,0,3,1,2:T(8,128)S(1)}, f32[32,5,1,8,128]{4,0,3,1,2:T(8,128)S(1)}, u32[]{:S(2)}, u32[]{:S(2)}) collective-permute-start(f32[32,5,1,8,128]{4,0,3,1,2:T(8,128)S(1)} %get-tuple-element.9), channel_id=1, source_target_pairs={{1,0},{2,1},{3,2},{4,3},{5,4},{6,5},{7,6},{8,7},{9,8},{10,9},{11,1... | collective-permute-start | bytes 1966088 | tf_op jit(solution)/shard_map/ppermute | solution.py:113
  10.2 2.2 %collective-permute-start = (f32[32,5,1,8,128]{4,0,3,1,2:T(8,128)S(1)}, f32[32,5,1,8,128]{4,0,3,1,2:T(8,128)S(1)}, u32[]{:S(2)}, u32[]{:S(2)}) collective-permute-start(f32[32,5,1,8,128]{4,0,3,1,2:T(8,128)S(1)} %get-tuple-element.8), channel_id=1, source_target_pairs={{0,1},{1,2},{2,3},{3,4},{4,5},{5,6},{6,7},{7,8},{8,9},{9,10},{10,1... | collective-permute-start | bytes 1966088 | tf_op jit(solution)/shard_map/ppermute | solution.py:112
  12.4 6.4 %fusion.22 = f32[32,252]{1,0:T(8,128)S(1)} fusion(bf16[252,5,2,8,128]{4,3,2,1,0:T(8,128)(2,1)} %param.5, f32[32,5,2,8,128]{4,0,3,1,2:T(8,128)S(1)} %convert_multiply_fusion, bf16[32,5,2,8,128]{4,3,2,1,0:T(8,128)(2,1)S(1)} %copy-done), kind=kOutput, calls=%fused_computation.33 | convolution fusion | flops 993853440 | bytes 7159296 | tf_op jit(solution)/shard_map/dot_general | solution.py:163
  18.9 0.9 fusion.32
  19.7 4.3 %collective-permute-done.1 = f32[32,5,1,8,128]{4,0,3,1,2:T(8,128)S(1)} collective-permute-done((f32[32,5,1,8,128]{4,0,3,1,2:T(8,128)S(1)}, f32[32,5,1,8,128]{4,0,3,1,2:T(8,128)S(1)}, u32[]{:S(2)}, u32[]{:S(2)}) %collective-permute-start.1) | collective-permute-done | bytes 655392 | tf_op jit(solution)/shard_map/ppermute | solution.py:113
  24.1 2.3 %fusion.21 = f32[32,252]{1,0:T(8,128)S(1)} fusion(bf16[252,5,1,8,128]{4,3,2,1,0:T(8,128)(2,1)S(1)} %get-tuple-element.7, f32[32,5,1,8,128]{4,0,3,1,2:T(8,128)S(1)} %collective-permute-done.1), kind=kOutput, calls=%fused_computation.32 | convolution fusion | flops 495452160 | bytes 3268096 | tf_op jit(solution)/shard_map/dot_general | solution.py:163
  26.4 4.2 %collective-permute-done = f32[32,5,1,8,128]{4,0,3,1,2:T(8,128)S(1)} collective-permute-done((f32[32,5,1,8,128]{4,0,3,1,2:T(8,128)S(1)}, f32[32,5,1,8,128]{4,0,3,1,2:T(8,128)S(1)}, u32[]{:S(2)}, u32[]{:S(2)}) %collective-permute-start) | collective-permute-done | bytes 655392 | tf_op jit(solution)/shard_map/ppermute | solution.py:112
  30.6 2.3 %fusion.28 = f32[32,252]{1,0:T(8,128)S(1)} fusion(f32[32,252]{1,0:T(8,128)S(1)} %fusion.22, f32[32,252]{1,0:T(8,128)S(1)} %fusion.21, bf16[252,5,1,8,128]{4,3,2,1,0:T(8,128)(2,1)S(1)} %get-tuple-element.6, f32[32,5,1,8,128]{4,0,3,1,2:T(8,128)S(1)} %collective-permute-done), kind=kOutput, calls=%fused_computation.35 | convolution fusion | flops 495468288 | bytes 3332608 | tf_op jit(solution)/shard_map/dot_general | solution.py:163
  34.0 4.8 %collective-permute-done.2 = f32[32,224]{0,1:T(8,128)S(1)} collective-permute-done((f32[32,224]{0,1:T(8,128)S(1)}, f32[32,224]{0,1:T(8,128)S(1)}, u32[]{:S(2)}, u32[]{:S(2)}) %collective-permute-start.2) | collective-permute-done | bytes 28704 | tf_op jit(solution)/shard_map/ppermute | solution.py:134
  39.0 7.6 %collective-permute-done.3 = f32[32,224]{0,1:T(8,128)S(1)} collective-permute-done((f32[32,224]{0,1:T(8,128)S(1)}, f32[32,224]{0,1:T(8,128)S(1)}, u32[]{:S(2)}, u32[]{:S(2)}) %collective-permute-start.3) | collective-permute-done | bytes 28704 | tf_op jit(solution)/shard_map/ppermute | solution.py:134
  46.7 8.7 %collective-permute-done.4 = f32[32,224]{0,1:T(8,128)S(1)} collective-permute-done((f32[32,224]{0,1:T(8,128)S(1)}, f32[32,224]{0,1:T(8,128)S(1)}, u32[]{:S(2)}, u32[]{:S(2)}) %collective-permute-start.4) | collective-permute-done | bytes 28704 | tf_op jit(solution)/shard_map/ppermute | solution.py:134
  55.5 4.8 %collective-permute-done.5 = f32[32,224]{0,1:T(8,128)S(1)} collective-permute-done((f32[32,224]{0,1:T(8,128)S(1)}, f32[32,224]{0,1:T(8,128)S(1)}, u32[]{:S(2)}, u32[]{:S(2)}) %collective-permute-start.5) | collective-permute-done | bytes 28704 | tf_op jit(solution)/shard_map/ppermute | solution.py:134
  60.3 0.7 collective-permute-start.6
  61.0 5.7 %collective-permute-done.6 = f32[32,224]{0,1:T(8,128)S(1)} collective-permute-done((f32[32,224]{0,1:T(8,128)S(1)}, f32[32,224]{0,1:T(8,128)S(1)}, u32[]{:S(2)}, u32[]{:S(2)}) %collective-permute-start.6) | collective-permute-done | bytes 28704 | tf_op jit(solution)/shard_map/ppermute | solution.py:134
  66.8 1.2 collective-permute-done.7
  68.3 1.6 collective-permute-start.8
  69.8 2.8 %collective-permute-done.8 = f32[32,448]{1,0:T(8,128)S(1)} collective-permute-done((f32[32,448]{1,0:T(8,128)S(1)}, f32[32,448]{1,0:T(8,128)S(1)}, u32[]{:S(2)}, u32[]{:S(2)}) %collective-permute-start.8) | collective-permute-done | bytes 57376 | tf_op jit(solution)/shard_map/ppermute | solution.py:146
  72.7 3.3 %collective-permute-start.9 = (f32[32,896]{1,0:T(8,128)S(1)}, f32[32,896]{1,0:T(8,128)S(1)}, u32[]{:S(2)}, u32[]{:S(2)}) collective-permute-start(f32[32,896]{1,0:T(8,128)S(1)} %maximum_select_fusion.1), channel_id=1, source_target_pairs={{0,128},{32,160},{64,192},{96,224},{128,0},{160,32},{192,64},{224,... | collective-permute-start | bytes 344072 | tf_op jit(solution)/shard_map/ppermute | solution.py:146
  76.7 2.6 %collective-permute-done.9 = f32[32,896]{1,0:T(8,128)S(1)} collective-permute-done((f32[32,896]{1,0:T(8,128)S(1)}, f32[32,896]{1,0:T(8,128)S(1)}, u32[]{:S(2)}, u32[]{:S(2)}) %collective-permute-start.9) | collective-permute-done | bytes 114720 | tf_op jit(solution)/shard_map/ppermute | solution.py:146
  79.3 3.8 %broadcast_multiply_fusion = f32[32,32,1792]{2,1,0:T(8,128)} fusion(f32[32,1792]{1,0:T(8,128)S(1)} %maximum_select_fusion), kind=kLoop, calls=%fused_computation.15 | loop fusion | flops 1835008 | bytes 7569408 | tf_op jit(solution)/shard_map/mul | solution.py:156
  83.1 9.0 %gather_fusion.1 = f32[528,1792]{1,0:T(8,128)} fusion(f32[1024,1792]{1,0:T(8,128)} %bitcast.43, s32[1024]{0:T(1024)S(1)} %pad_clamp_fusion), kind=kCustom, calls=%fused_computation.1 | custom fusion | bytes 7571520 | tf_op jit(solution)/shard_map/jit(_take)/gather | solution.py:157
  92.1 15.4 %fusion.10.a_ref = f32[561,561]{1,0:T(8,128)} fusion(f32[528,1792]{1,0:T(8,128)} %gather_fusion.1, f32[32,1792]{1,0:T(8,128)S(1)} %maximum_select_fusion, f32[561]{0:T(1024)S(1)} %pad.5.clone), kind=kOutput, calls=%fused_computation.23 | convolution fusion | flops 6770085888 | bytes 5275208 | tf_op jit(solution)/shard_map/dot_general | solution.py:187
  107.5 58.7 %shard_map.68 = f32[561,561]{1,0:T(8,128)} custom-call(f32[561,561]{1,0:T(8,128)} %fusion.10.a_ref), custom_call_target="tpu_custom_call" | custom-call | tf_op jit(solution)/shard_map/pallas_call | solution.py:100
  (36 shorter events, 2.8 us)
Async XLA Ops:
  0.6 11.7 %copy-start = (bf16[32,5,2,8,128]{4,3,2,1,0:T(8,128)(2,1)S(1)}, bf16[32,5,2,8,128]{4,3,2,1,0:T(8,128)(2,1)}, u32[]{:S(2)}) copy-start(bf16[32,5,2,8,128]{4,3,2,1,0:T(8,128)(2,1)} %param.7) | copy-start | bytes 1966084
  2.2 21.9 %collective-permute-start.1 = (f32[32,5,1,8,128]{4,0,3,1,2:T(8,128)S(1)}, f32[32,5,1,8,128]{4,0,3,1,2:T(8,128)S(1)}, u32[]{:S(2)}, u32[]{:S(2)}) collective-permute-start(f32[32,5,1,8,128]{4,0,3,1,2:T(8,128)S(1)} %get-tuple-element.9), channel_id=1, source_target_pairs={{1,0},{2,1},{3,2},{4,3},{5,4},{6,5},{7,6},{8,7},{9,8},{10,9},{11,1... | collective-permute-start | bytes 1966088 | tf_op jit(solution)/shard_map/ppermute | solution.py:113
  10.1 8.7 %slice-start = ((s8[5160960]{0:T(1024)(128)(4,1)}), s8[4194304]{0:T(1024)(128)(4,1)S(1)}, s32[]{:S(2)}) async-start(s8[5160960]{0:T(1024)(128)(4,1)} %bitcast.44), calls=%async_computation | async-start | bytes 8388608
  10.1 8.6 %copy-start.2 = (s32[224]{0:T(256)S(1)}, s32[224]{0:T(256)}, u32[]{:S(2)}) copy-start(s32[224]{0:T(256)} %param.6) | copy-start | bytes 2692
  10.1 8.7 %slice-start.1 = ((s8[5160960]{0:T(1024)(128)(4,1)}), s8[966656]{0:T(1024)(128)(4,1)S(1)}, s32[]{:S(2)}) async-start(s8[5160960]{0:T(1024)(128)(4,1)} %bitcast.44), calls=%async_computation.1 | async-start | bytes 1933312
  10.2 20.5 %collective-permute-start = (f32[32,5,1,8,128]{4,0,3,1,2:T(8,128)S(1)}, f32[32,5,1,8,128]{4,0,3,1,2:T(8,128)S(1)}, u32[]{:S(2)}, u32[]{:S(2)}) collective-permute-start(f32[32,5,1,8,128]{4,0,3,1,2:T(8,128)S(1)} %get-tuple-element.8), channel_id=1, source_target_pairs={{0,1},{1,2},{2,3},{3,4},{4,5},{5,6},{6,7},{7,8},{8,9},{9,10},{10,1... | collective-permute-start | bytes 1966088 | tf_op jit(solution)/shard_map/ppermute | solution.py:112
  30.6 45.4 %copy-start.1 = (s32[528]{0:T(1024)S(1)}, s32[528]{0:T(1024)}, u32[]{:S(2)}) copy-start(s32[528]{0:T(1024)} %constant.112) | copy-start | bytes 6340
  33.9 4.9 %collective-permute-start.2 = (f32[32,224]{0,1:T(8,128)S(1)}, f32[32,224]{0,1:T(8,128)S(1)}, u32[]{:S(2)}, u32[]{:S(2)}) collective-permute-start(f32[32,224]{0,1:T(8,128)S(1)} %select_bitcast_fusion), channel_id=1, source_target_pairs={{0,1},{1,0},{2,3},{3,2},{4,5},{5,4},{6,7},{7,6},{8,9},{9,8},{10,11... | collective-permute-start | bytes 86024 | tf_op jit(solution)/shard_map/ppermute | solution.py:134
  38.9 7.7 %collective-permute-start.3 = (f32[32,224]{0,1:T(8,128)S(1)}, f32[32,224]{0,1:T(8,128)S(1)}, u32[]{:S(2)}, u32[]{:S(2)}) collective-permute-start(f32[32,224]{0,1:T(8,128)S(1)} %fusion.34), channel_id=1, source_target_pairs={{0,2},{1,3},{2,0},{3,1},{4,6},{5,7},{6,4},{7,5},{8,10},{9,11},{10,... | collective-permute-start | bytes 86024 | tf_op jit(solution)/shard_map/ppermute | solution.py:134
  46.6 8.8 %collective-permute-start.4 = (f32[32,224]{0,1:T(8,128)S(1)}, f32[32,224]{0,1:T(8,128)S(1)}, u32[]{:S(2)}, u32[]{:S(2)}) collective-permute-start(f32[32,224]{0,1:T(8,128)S(1)} %add.81), channel_id=1, source_target_pairs={{0,4},{1,5},{2,6},{3,7},{4,0},{5,1},{6,2},{7,3},{8,12},{9,13},{10,... | collective-permute-start | bytes 86024 | tf_op jit(solution)/shard_map/ppermute | solution.py:134
  55.4 4.9 %collective-permute-start.5 = (f32[32,224]{0,1:T(8,128)S(1)}, f32[32,224]{0,1:T(8,128)S(1)}, u32[]{:S(2)}, u32[]{:S(2)}) collective-permute-start(f32[32,224]{0,1:T(8,128)S(1)} %add.82), channel_id=1, source_target_pairs={{0,8},{1,9},{2,10},{3,11},{4,12},{5,13},{6,14},{7,15},{8,0},{9,1},... | collective-permute-start | bytes 86024 | tf_op jit(solution)/shard_map/ppermute | solution.py:134
  60.3 6.4 %collective-permute-start.6 = (f32[32,224]{0,1:T(8,128)S(1)}, f32[32,224]{0,1:T(8,128)S(1)}, u32[]{:S(2)}, u32[]{:S(2)}) collective-permute-start(f32[32,224]{0,1:T(8,128)S(1)} %add.83), channel_id=1, source_target_pairs={{0,16},{1,17},{2,18},{3,19},{4,20},{5,21},{6,22},{7,23},{8,24},{9,... | collective-permute-start | bytes 86024 | tf_op jit(solution)/shard_map/ppermute | solution.py:134
  66.7 1.4 collective-permute-start.7
  68.3 4.4 %collective-permute-start.8 = (f32[32,448]{1,0:T(8,128)S(1)}, f32[32,448]{1,0:T(8,128)S(1)}, u32[]{:S(2)}, u32[]{:S(2)}) collective-permute-start(f32[32,448]{1,0:T(8,128)S(1)} %maximum_select_fusion.2), channel_id=1, source_target_pairs={{0,64},{32,96},{64,0},{96,32},{128,192},{160,224},{192,128},{224,1... | collective-permute-start | bytes 172040 | tf_op jit(solution)/shard_map/ppermute | solution.py:146
  72.7 6.6 %collective-permute-start.9 = (f32[32,896]{1,0:T(8,128)S(1)}, f32[32,896]{1,0:T(8,128)S(1)}, u32[]{:S(2)}, u32[]{:S(2)}) collective-permute-start(f32[32,896]{1,0:T(8,128)S(1)} %maximum_select_fusion.1), channel_id=1, source_target_pairs={{0,128},{32,160},{64,192},{96,224},{128,0},{160,32},{192,64},{224,... | collective-permute-start | bytes 344072 | tf_op jit(solution)/shard_map/ppermute | solution.py:146

commit v9 on v7

--- a/solution.py
+++ b/solution.py
@@ -64,7 +64,7 @@
             for g in range(PANEL // 8):
                 blk_ref[8 * g : 8 * g + 8, :] = groups[g]
         else:
-            for first in range(0, steps, 16):
+            for first in range(0, steps, 8):
                 top = (first // 8) * 8
                 height = PANEL - top
                 seg_rows = lax.broadcasted_iota(jnp.int32, (height, 1), 0) + top
@@ -82,7 +82,7 @@
                     blk_ref[pl.ds(j, 1), :] = scaled
                     return carry
 
-                lax.fori_loop(first, min(first + 16, steps), step, 0)
+                lax.fori_loop(first, min(first + 8, steps), step, 0)
         block = blk_ref[...]
         upper = jnp.where(lanes[:, :PANEL] >= rows[:, :PANEL], block[:, :PANEL], 0.0)
         end = min(c1, valid)

time: 162 us -> 162 us (level)
  no operation moved by 1% of the time
where the time goes in v9:
time: 162 us; the launch traced here: 161 us
  Pallas kernels  58.7 us (36%)
  waiting for transfers between devices  46.5 us (29%)
  matrix products  22.6 us (14%)
  starting transfers between devices  16 us (10%)
  local copies, waits for them, and re-layouts  11.2 us (7%)
  other arithmetic  5.54 us (3%)
    pallas_call x1, Pallas kernels, cholesky_upper(): pl.pallas_call(functools.partial(chol_kernel, size=size, valid=n), out_sh...  58.7 us
    ppermute x5, waiting for transfers between devices, butterfly_sum(): x = x + lax.ppermute(x, axis, [(i, i ^ step) for i in range(count)])  31.5 us
    dot_general x1, matrix products, body(): lax.dot_general(features_t, features_t, (((1,), (1,)), ((), ())), precisi...  11.5 us
    dot_general x3, matrix products, project(): lax.dot_general(left, right, (((1,), (1,)), ((), ())), precision=lax.Prec...  11.1 us
    ppermute x1, starting transfers between devices, neighbour_planes(): high = lax.ppermute(lax.slice_in_dim(block, 0, 1, axis=dim), axis, backward)  7.94 us
    ppermute x3, waiting for transfers between devices, butterfly_gather(): other = lax.ppermute(x, axis, [(i, i ^ step) for i in range(count)])  6.51 us
    ppermute x3, starting transfers between devices, butterfly_gather(): other = lax.ppermute(x, axis, [(i, i ^ step) for i in range(count)])  4.78 us
    ppermute x1, waiting for transfers between devices, neighbour_planes(): high = lax.ppermute(lax.slice_in_dim(block, 0, 1, axis=dim), axis, backward)  4.34 us
  transfers between devices with their start and end apart: 10, of which 10 were waited for; matrix products, arithmetic and copies ran while one was open for 6% of the time, Pallas kernels for 0%

profile of v9, /device:TPU:24, one launch (start us, length us, event | category | flops | bytes accessed | tf_op | source)
XLA Modules:
  0.0 161.5 jit_solution(4782898925724042032)
XLA Ops:
  0.6 1.4 convert_multiply_fusion
  2.1 7.9 %collective-permute-start.1 = (f32[32,5,1,8,128]{4,0,3,1,2:T(8,128)S(1)}, f32[32,5,1,8,128]{4,0,3,1,2:T(8,128)S(1)}, u32[]{:S(2)}, u32[]{:S(2)}) collective-permute-start(f32[32,5,1,8,128]{4,0,3,1,2:T(8,128)S(1)} %get-tuple-element.10), channel_id=1, source_target_pairs={{1,0},{2,1},{3,2},{4,3},{5,4},{6,5},{7,6},{8,7},{9,8},{10,9},{11,1... | collective-permute-start | bytes 1966088 | tf_op jit(solution)/shard_map/ppermute | solution.py:113
  10.1 2.2 %collective-permute-start = (f32[32,5,1,8,128]{4,0,3,1,2:T(8,128)S(1)}, f32[32,5,1,8,128]{4,0,3,1,2:T(8,128)S(1)}, u32[]{:S(2)}, u32[]{:S(2)}) collective-permute-start(f32[32,5,1,8,128]{4,0,3,1,2:T(8,128)S(1)} %get-tuple-element.9), channel_id=1, source_target_pairs={{0,1},{1,2},{2,3},{3,4},{4,5},{5,6},{6,7},{7,8},{8,9},{9,10},{10,1... | collective-permute-start | bytes 1966088 | tf_op jit(solution)/shard_map/ppermute | solution.py:112
  12.3 6.4 %fusion.22 = f32[32,252]{1,0:T(8,128)S(1)} fusion(bf16[252,5,2,8,128]{4,3,2,1,0:T(8,128)(2,1)} %param.8, f32[32,5,2,8,128]{4,0,3,1,2:T(8,128)S(1)} %convert_multiply_fusion, bf16[32,5,2,8,128]{4,3,2,1,0:T(8,128)(2,1)S(1)} %copy-done), kind=kOutput, calls=%fused_computation.33 | convolution fusion | flops 993853440 | bytes 7159296 | tf_op jit(solution)/shard_map/dot_general | solution.py:162
  18.8 0.9 fusion.32
  19.7 4.3 %collective-permute-done.1 = f32[32,5,1,8,128]{4,0,3,1,2:T(8,128)S(1)} collective-permute-done((f32[32,5,1,8,128]{4,0,3,1,2:T(8,128)S(1)}, f32[32,5,1,8,128]{4,0,3,1,2:T(8,128)S(1)}, u32[]{:S(2)}, u32[]{:S(2)}) %collective-permute-start.1) | collective-permute-done | bytes 655392 | tf_op jit(solution)/shard_map/ppermute | solution.py:113
  24.0 2.3 %fusion.21 = f32[32,252]{1,0:T(8,128)S(1)} fusion(bf16[252,5,1,8,128]{4,3,2,1,0:T(8,128)(2,1)S(1)} %get-tuple-element.8, f32[32,5,1,8,128]{4,0,3,1,2:T(8,128)S(1)} %collective-permute-done.1), kind=kOutput, calls=%fused_computation.32 | convolution fusion | flops 495452160 | bytes 3268096 | tf_op jit(solution)/shard_map/dot_general | solution.py:162
  26.4 4.2 %collective-permute-done = f32[32,5,1,8,128]{4,0,3,1,2:T(8,128)S(1)} collective-permute-done((f32[32,5,1,8,128]{4,0,3,1,2:T(8,128)S(1)}, f32[32,5,1,8,128]{4,0,3,1,2:T(8,128)S(1)}, u32[]{:S(2)}, u32[]{:S(2)}) %collective-permute-start) | collective-permute-done | bytes 655392 | tf_op jit(solution)/shard_map/ppermute | solution.py:112
  30.6 2.3 %fusion.28 = f32[32,252]{1,0:T(8,128)S(1)} fusion(f32[32,252]{1,0:T(8,128)S(1)} %fusion.22, f32[32,252]{1,0:T(8,128)S(1)} %fusion.21, bf16[252,5,1,8,128]{4,3,2,1,0:T(8,128)(2,1)S(1)} %get-tuple-element.7, f32[32,5,1,8,128]{4,0,3,1,2:T(8,128)S(1)} %collective-permute-done), kind=kOutput, calls=%fused_computation.35 | convolution fusion | flops 495468288 | bytes 3332608 | tf_op jit(solution)/shard_map/dot_general | solution.py:162
  33.9 4.8 %collective-permute-done.2 = f32[32,224]{0,1:T(8,128)S(1)} collective-permute-done((f32[32,224]{0,1:T(8,128)S(1)}, f32[32,224]{0,1:T(8,128)S(1)}, u32[]{:S(2)}, u32[]{:S(2)}) %collective-permute-start.2) | collective-permute-done | bytes 28704 | tf_op jit(solution)/shard_map/ppermute | solution.py:134
  38.9 7.6 %collective-permute-done.3 = f32[32,224]{0,1:T(8,128)S(1)} collective-permute-done((f32[32,224]{0,1:T(8,128)S(1)}, f32[32,224]{0,1:T(8,128)S(1)}, u32[]{:S(2)}, u32[]{:S(2)}) %collective-permute-start.3) | collective-permute-done | bytes 28704 | tf_op jit(solution)/shard_map/ppermute | solution.py:134
  46.6 8.7 %collective-permute-done.4 = f32[32,224]{0,1:T(8,128)S(1)} collective-permute-done((f32[32,224]{0,1:T(8,128)S(1)}, f32[32,224]{0,1:T(8,128)S(1)}, u32[]{:S(2)}, u32[]{:S(2)}) %collective-permute-start.4) | collective-permute-done | bytes 28704 | tf_op jit(solution)/shard_map/ppermute | solution.py:134
  55.4 4.8 %collective-permute-done.5 = f32[32,224]{0,1:T(8,128)S(1)} collective-permute-done((f32[32,224]{0,1:T(8,128)S(1)}, f32[32,224]{0,1:T(8,128)S(1)}, u32[]{:S(2)}, u32[]{:S(2)}) %collective-permute-start.5) | collective-permute-done | bytes 28704 | tf_op jit(solution)/shard_map/ppermute | solution.py:134
  60.9 5.7 %collective-permute-done.6 = f32[32,224]{0,1:T(8,128)S(1)} collective-permute-done((f32[32,224]{0,1:T(8,128)S(1)}, f32[32,224]{0,1:T(8,128)S(1)}, u32[]{:S(2)}, u32[]{:S(2)}) %collective-permute-start.6) | collective-permute-done | bytes 28704 | tf_op jit(solution)/shard_map/ppermute | solution.py:134
  66.8 1.2 collective-permute-done.7
  68.2 1.6 collective-permute-start.8
  69.8 2.8 %collective-permute-done.8 = f32[32,448]{1,0:T(8,128)S(1)} collective-permute-done((f32[32,448]{1,0:T(8,128)S(1)}, f32[32,448]{1,0:T(8,128)S(1)}, u32[]{:S(2)}, u32[]{:S(2)}) %collective-permute-start.8) | collective-permute-done | bytes 57376 | tf_op jit(solution)/shard_map/ppermute | solution.py:146
  72.7 3.1 %collective-permute-start.9 = (f32[32,896]{1,0:T(8,128)S(1)}, f32[32,896]{1,0:T(8,128)S(1)}, u32[]{:S(2)}, u32[]{:S(2)}) collective-permute-start(f32[32,896]{1,0:T(8,128)S(1)} %maximum_select_fusion.1), channel_id=1, source_target_pairs={{0,128},{32,160},{64,192},{96,224},{128,0},{160,32},{192,64},{224,... | collective-permute-start | bytes 344072 | tf_op jit(solution)/shard_map/ppermute | solution.py:146
  76.5 2.5 %collective-permute-done.9 = f32[32,896]{1,0:T(8,128)S(1)} collective-permute-done((f32[32,896]{1,0:T(8,128)S(1)}, f32[32,896]{1,0:T(8,128)S(1)}, u32[]{:S(2)}, u32[]{:S(2)}) %collective-permute-start.9) | collective-permute-done | bytes 114720 | tf_op jit(solution)/shard_map/ppermute | solution.py:146
  79.1 4.3 %gather_fusion.1 = f32[528,1792]{1,0:T(8,128)} fusion(f32[32,1792]{1,0:T(8,128)S(1)} %maximum_select_fusion, s32[1024]{0:T(1024)S(1)} %pad_clamp_fusion.1), kind=kCustom, calls=%fused_computation.clone | custom fusion | bytes 7571520 | tf_op jit(solution)/shard_map/jit(_take)/gather | solution.py:156
  83.4 4.3 %gather_fusion.2 = f32[528,1792]{1,0:T(8,128)} fusion(f32[32,1792]{1,0:T(8,128)S(1)} %maximum_select_fusion, s32[1024]{0:T(1024)S(1)} %pad_clamp_fusion), kind=kCustom, calls=%fused_computation.1.clone | custom fusion | bytes 7571520 | tf_op jit(solution)/shard_map/jit(_take)/gather | solution.py:156
  87.7 3.7 %mul.21 = f32[528,1792]{1,0:T(8,128)S(1)} multiply(f32[528,1792]{1,0:T(8,128)} %gather_fusion.1, f32[528,1792]{1,0:T(8,128)} %gather_fusion.2) | non-fusion elementwise | flops 946176 | bytes 11354112 | tf_op jit(solution)/shard_map/mul | solution.py:156
  91.4 11.5 %fusion.10.a_ref = f32[561,561]{1,0:T(8,128)} fusion(f32[528,1792]{1,0:T(8,128)S(1)} %mul.21, f32[32,1792]{1,0:T(8,128)S(1)} %maximum_select_fusion, f32[561]{0:T(1024)S(1)} %pad.5.clone), kind=kOutput, calls=%fused_computation.23 | convolution fusion | flops 6770085888 | bytes 5275208 | tf_op jit(solution)/shard_map/dot_general | solution.py:186
  102.8 58.7 %shard_map.77 = f32[561,561]{1,0:T(8,128)} custom-call(f32[561,561]{1,0:T(8,128)} %fusion.10.a_ref), custom_call_target="tpu_custom_call" | custom-call | tf_op jit(solution)/shard_map/pallas_call | solution.py:100
  (40 shorter events, 3.4 us)
Async XLA Ops:
  0.6 11.7 %copy-start = (bf16[32,5,2,8,128]{4,3,2,1,0:T(8,128)(2,1)S(1)}, bf16[32,5,2,8,128]{4,3,2,1,0:T(8,128)(2,1)}, u32[]{:S(2)}) copy-start(bf16[32,5,2,8,128]{4,3,2,1,0:T(8,128)(2,1)} %param.10) | copy-start | bytes 1966084
  2.1 21.9 %collective-permute-start.1 = (f32[32,5,1,8,128]{4,0,3,1,2:T(8,128)S(1)}, f32[32,5,1,8,128]{4,0,3,1,2:T(8,128)S(1)}, u32[]{:S(2)}, u32[]{:S(2)}) collective-permute-start(f32[32,5,1,8,128]{4,0,3,1,2:T(8,128)S(1)} %get-tuple-element.10), channel_id=1, source_target_pairs={{1,0},{2,1},{3,2},{4,3},{5,4},{6,5},{7,6},{8,7},{9,8},{10,9},{11,1... | collective-permute-start | bytes 1966088 | tf_op jit(solution)/shard_map/ppermute | solution.py:113
  10.1 8.7 %slice-start = ((s8[5160960]{0:T(1024)(128)(4,1)}), s8[4194304]{0:T(1024)(128)(4,1)S(1)}, s32[]{:S(2)}) async-start(s8[5160960]{0:T(1024)(128)(4,1)} %bitcast.42), calls=%async_computation | async-start | bytes 8388608
  10.1 8.6 %copy-start.3 = (s32[224]{0:T(256)S(1)}, s32[224]{0:T(256)}, u32[]{:S(2)}) copy-start(s32[224]{0:T(256)} %param.9) | copy-start | bytes 2692
  10.1 8.7 %slice-start.1 = ((s8[5160960]{0:T(1024)(128)(4,1)}), s8[966656]{0:T(1024)(128)(4,1)S(1)}, s32[]{:S(2)}) async-start(s8[5160960]{0:T(1024)(128)(4,1)} %bitcast.42), calls=%async_computation.1 | async-start | bytes 1933312
  10.1 20.5 %collective-permute-start = (f32[32,5,1,8,128]{4,0,3,1,2:T(8,128)S(1)}, f32[32,5,1,8,128]{4,0,3,1,2:T(8,128)S(1)}, u32[]{:S(2)}, u32[]{:S(2)}) collective-permute-start(f32[32,5,1,8,128]{4,0,3,1,2:T(8,128)S(1)} %get-tuple-element.9), channel_id=1, source_target_pairs={{0,1},{1,2},{2,3},{3,4},{4,5},{5,6},{6,7},{7,8},{8,9},{9,10},{10,1... | collective-permute-start | bytes 1966088 | tf_op jit(solution)/shard_map/ppermute | solution.py:112
  30.6 45.2 %copy-start.2 = (s32[528]{0:T(1024)S(1)}, s32[528]{0:T(1024)}, u32[]{:S(2)}) copy-start(s32[528]{0:T(1024)} %constant.121) | copy-start | bytes 6340
  30.6 45.3 %copy-start.1 = (s32[528]{0:T(1024)S(1)}, s32[528]{0:T(1024)}, u32[]{:S(2)}) copy-start(s32[528]{0:T(1024)} %constant.122) | copy-start | bytes 6340
  33.8 4.9 %collective-permute-start.2 = (f32[32,224]{0,1:T(8,128)S(1)}, f32[32,224]{0,1:T(8,128)S(1)}, u32[]{:S(2)}, u32[]{:S(2)}) collective-permute-start(f32[32,224]{0,1:T(8,128)S(1)} %select_bitcast_fusion), channel_id=1, source_target_pairs={{0,1},{1,0},{2,3},{3,2},{4,5},{5,4},{6,7},{7,6},{8,9},{9,8},{10,11... | collective-permute-start | bytes 86024 | tf_op jit(solution)/shard_map/ppermute | solution.py:134
  38.8 7.7 %collective-permute-start.3 = (f32[32,224]{0,1:T(8,128)S(1)}, f32[32,224]{0,1:T(8,128)S(1)}, u32[]{:S(2)}, u32[]{:S(2)}) collective-permute-start(f32[32,224]{0,1:T(8,128)S(1)} %fusion.34), channel_id=1, source_target_pairs={{0,2},{1,3},{2,0},{3,1},{4,6},{5,7},{6,4},{7,5},{8,10},{9,11},{10,... | collective-permute-start | bytes 86024 | tf_op jit(solution)/shard_map/ppermute | solution.py:134
  46.5 8.8 %collective-permute-start.4 = (f32[32,224]{0,1:T(8,128)S(1)}, f32[32,224]{0,1:T(8,128)S(1)}, u32[]{:S(2)}, u32[]{:S(2)}) collective-permute-start(f32[32,224]{0,1:T(8,128)S(1)} %add.79), channel_id=1, source_target_pairs={{0,4},{1,5},{2,6},{3,7},{4,0},{5,1},{6,2},{7,3},{8,12},{9,13},{10,... | collective-permute-start | bytes 86024 | tf_op jit(solution)/shard_map/ppermute | solution.py:134
  55.3 4.9 %collective-permute-start.5 = (f32[32,224]{0,1:T(8,128)S(1)}, f32[32,224]{0,1:T(8,128)S(1)}, u32[]{:S(2)}, u32[]{:S(2)}) collective-permute-start(f32[32,224]{0,1:T(8,128)S(1)} %add.80), channel_id=1, source_target_pairs={{0,8},{1,9},{2,10},{3,11},{4,12},{5,13},{6,14},{7,15},{8,0},{9,1},... | collective-permute-start | bytes 86024 | tf_op jit(solution)/shard_map/ppermute | solution.py:134
  60.2 6.4 %collective-permute-start.6 = (f32[32,224]{0,1:T(8,128)S(1)}, f32[32,224]{0,1:T(8,128)S(1)}, u32[]{:S(2)}, u32[]{:S(2)}) collective-permute-start(f32[32,224]{0,1:T(8,128)S(1)} %add.81), channel_id=1, source_target_pairs={{0,16},{1,17},{2,18},{3,19},{4,20},{5,21},{6,22},{7,23},{8,24},{9,... | collective-permute-start | bytes 86024 | tf_op jit(solution)/shard_map/ppermute | solution.py:134
  66.6 1.4 collective-permute-start.7
  68.2 4.4 %collective-permute-start.8 = (f32[32,448]{1,0:T(8,128)S(1)}, f32[32,448]{1,0:T(8,128)S(1)}, u32[]{:S(2)}, u32[]{:S(2)}) collective-permute-start(f32[32,448]{1,0:T(8,128)S(1)} %maximum_select_fusion.2), channel_id=1, source_target_pairs={{0,64},{32,96},{64,0},{96,32},{128,192},{160,224},{192,128},{224,1... | collective-permute-start | bytes 172040 | tf_op jit(solution)/shard_map/ppermute | solution.py:146
  72.7 6.4 %collective-permute-start.9 = (f32[32,896]{1,0:T(8,128)S(1)}, f32[32,896]{1,0:T(8,128)S(1)}, u32[]{:S(2)}, u32[]{:S(2)}) collective-permute-start(f32[32,896]{1,0:T(8,128)S(1)} %maximum_select_fusion.1), channel_id=1, source_target_pairs={{0,128},{32,160},{64,192},{96,224},{128,0},{160,32},{192,64},{224,... | collective-permute-start | bytes 344072 | tf_op jit(solution)/shard_map/ppermute | solution.py:146
